TPU v7x, 128 devices: a whole 4x4x4 slice. The times are simulated.
128 devices in a mesh: seg: 32 (over y, x, core), head: 4 (over z).
Axes of the slice: x: 4, y: 4, z: 4, core: 2. Of those that a mesh axis runs over, the one named last changes fastest.
Arguments:
- tokens: float32 [16384, 2048], P(('seg', 'head'))
- document_index: int32 [16384], P('seg'), may hold values from 0 to 127, never falling along the last dimension, each value on 1 to 256 neighbouring positions
- block_mask: int32 [32, 4, 4], P('seg'), may hold values from 0 to 1, as said below
- slot_keys: bfloat16 [2, 128, 2048], P(None, None, 'head'), may hold values from -8 to 8
- mem_init: float32 [2, 128, 2048], P(None, None, 'head'), may hold values from -6 to 6
- retain: float32 [2, 32, 32], P(None, 'seg', 'head'), may hold values from 0.005 to 1
- attn_gain: float32 [2, 2048], replicated, may hold values from 0.25 to 4
- mlp_gain: float32 [2, 2048], replicated, may hold values from 0.25 to 4
- w_query: bfloat16 [2, 2048, 2048], P(None, None, 'head')
- w_kv: bfloat16 [2, 2048, 1024], P(None, None, 'head')
- w_out: bfloat16 [2, 2048, 2048], P(None, 'head'), may hold values from -0.125 to 0.125
- w_gate_up: bfloat16 [2, 2048, 2, 4096], P(None, None, None, 'head'), may hold values from -0.125 to 0.125
- w_down: bfloat16 [2, 4096, 2048], P(None, 'head'), may hold values from -0.09375 to 0.09375
Outputs:
- hidden: float32 [16384, 2048], P(('seg', 'head'))
- memory: float32 [2, 32, 128, 2048], P(None, 'seg', None, 'head')
Inputs may be any that keep to these rules, and one draw needn't show every extreme that they name: `document_index`: document numbers never fall along the sequence. `block_mask`: in every segment the blocks on the diagonal are 1 and the blocks above it 0.
All inputs are finite; a program needn't handle non-finite values.
Results may differ from a plain program's by a relative error of at most 0.025.
Values may be sent and summed in bfloat16 or wider, within the bound.
No kernel may reach another device: no remote copies, remote signals or barrier semaphores. Data moves between devices by JAX's collectives and lax.ppermute only.
A program may use at most 192 MiB of HBM per device.

v0:
```python
import jax
import jax.numpy as jnp
from jax import lax
from jax.sharding import PartitionSpec as P

HEADS = 32
KV_HEADS = 8
HD = 64
MEM = 128
SEG_LEN = 512
BLOCK = 128
DEPTH_NUMBER = 2


def prefix(x, axis, combine, identity):
    count, here = (lax.axis_size(axis), lax.axis_index(axis))
    everything = jax.tree.map(lambda part: lax.all_gather(part, axis), x)
    start = jax.tree.map(
        lambda part, zero: jnp.broadcast_to(jnp.asarray(zero, part.dtype), part.shape), x, identity
    )

    def hop(k, before):
        reached = k < here
        new = combine(before, jax.tree.map(lambda part: part[k], everything))
        return jax.tree.map(lambda a, b: jnp.where(reached, a, b), new, before)

    return lax.fori_loop(0, count, hop, start)


def rms_norm(value, gain):
    factor = lax.rsqrt(jnp.mean(value * value, axis=-1, keepdims=True) + 1e-05)
    return (value * factor * gain).astype(jnp.bfloat16)


def rope_tables(position):
    half = HD // 2
    freq = 500000.0 ** (-(jnp.arange(half).astype(jnp.float32) * 2.0 / HD))
    angle = position.astype(jnp.float32)[:, None] * freq[None, :]
    return (jnp.cos(angle), jnp.sin(angle))


def rotate(tensor, cosine, sine):
    half = tensor.shape[-1] // 2
    first = tensor[..., :half]
    second = tensor[..., half:]
    cos_part = cosine[:, None, :]
    sin_part = sine[:, None, :]
    return jnp.concatenate(
        [first * cos_part - second * sin_part, second * cos_part + first * sin_part], axis=-1
    )


def combine(earlier, later):
    return (earlier[0] * later[0], later[0] * earlier[1] + later[1])


def body(
    tokens,
    document_index,
    block_mask,
    slot_keys,
    mem_init,
    retain,
    attn_gain,
    mlp_gain,
    w_query,
    w_kv,
    w_out,
    w_gate_up,
    w_down,
):
    seg_local = document_index.shape[0] // SEG_LEN
    rows_all = seg_local * SEG_LEN
    cols_query = w_query.shape[2]
    local_heads = cols_query // HD
    group = HEADS // KV_HEADS
    local_kv = local_heads // group
    scale = HD ** (-0.5)
    cosine, sine = rope_tables(jnp.arange(rows_all) % SEG_LEN)
    docs = document_index.reshape(seg_local, SEG_LEN)
    causal = jnp.arange(SEG_LEN)[:, None] >= jnp.arange(SEG_LEN)[None, :]
    stream = tokens
    stored = []
    for layer in range(DEPTH_NUMBER):
        query_weight = w_query[layer]
        pair_weight = w_kv[layer]
        out_weight = w_out[layer]
        widening_matrix = w_gate_up[layer]
        down_weight = w_down[layer]
        normed = rms_norm(stream, attn_gain[layer])
        project_piece = lax.all_gather(normed, "head", axis=0, tiled=True)
        projected = jnp.concatenate(
            [
                jnp.dot(project_piece, query_weight, preferred_element_type=jnp.float32),
                jnp.dot(project_piece, pair_weight, preferred_element_type=jnp.float32),
            ],
            axis=1,
        )
        query = rotate(
            projected[:, :cols_query].reshape(rows_all, local_heads, HD), cosine, sine
        ).astype(jnp.bfloat16)
        pairs = projected[:, cols_query:].reshape(rows_all, local_kv, 2, HD)
        lookup_vectors = rotate(pairs[:, :, 0], cosine, sine).astype(jnp.bfloat16)
        values = pairs[:, :, 1].astype(jnp.bfloat16)
        query = query.reshape(seg_local, SEG_LEN, local_kv, group, HD)
        lookup_vectors = lookup_vectors.reshape(seg_local, SEG_LEN, local_kv, HD)
        values = values.reshape(seg_local, SEG_LEN, local_kv, HD)
        slots = slot_keys[layer].reshape(MEM, local_kv, group, HD)
        write_scores = (
            jnp.einsum(
                "mkgd,sjkd->skgmj", slots, lookup_vectors, preferred_element_type=jnp.float32
            )
            * scale
        )
        write_probs = jax.nn.softmax(write_scores, axis=-1).astype(jnp.bfloat16)
        written = jnp.einsum(
            "skgmj,sjkd->smkgd", write_probs, values, preferred_element_type=jnp.float32
        ).reshape(seg_local, MEM, cols_query)
        rates = jnp.repeat(retain[layer], HD, axis=1)[:, None, :]
        keep_total = jnp.ones((1, cols_query), jnp.float32)
        add_total = jnp.zeros((MEM, cols_query), jnp.float32)
        segment = 0
        keep_total = keep_total * rates[segment]
        add_total = rates[segment] * add_total + (1.0 - rates[segment]) * written[segment]
        identity = (
            jnp.ones((1, cols_query), jnp.float32),
            jnp.zeros((MEM, cols_query), jnp.float32),
        )
        keep_before, add_before = prefix((keep_total, add_total), "seg", combine, identity)
        state = keep_before * mem_init[layer] + add_before
        segment = 0
        memory_read = state.astype(jnp.bfloat16).reshape(MEM, local_kv, group, HD)
        state = rates[segment] * state + (1.0 - rates[segment]) * written[segment]
        after_list = [state]
        blocks = jnp.repeat(jnp.repeat(block_mask[segment], BLOCK, axis=0), BLOCK, axis=1)
        allowed = causal & (docs[segment][:, None] == docs[segment][None, :]) & (blocks == 1)
        slot_scores = (
            jnp.einsum("ikgd,mkgd->kgim", query[segment], slots, preferred_element_type=jnp.float32)
            * scale
        )
        token_scores = (
            jnp.einsum(
                "ikgd,jkd->kgij",
                query[segment],
                lookup_vectors[segment],
                preferred_element_type=jnp.float32,
            )
            * scale
        )
        token_scores = jnp.where(allowed, token_scores, -jnp.inf)
        probs = jax.nn.softmax(
            jnp.concatenate([slot_scores, token_scores], axis=-1), axis=-1
        ).astype(jnp.bfloat16)
        result = jnp.einsum(
            "kgim,mkgd->ikgd", probs[..., :MEM], memory_read, preferred_element_type=jnp.float32
        )
        result = result + jnp.einsum(
            "kgij,jkd->ikgd", probs[..., MEM:], values[segment], preferred_element_type=jnp.float32
        )
        outputs = result.reshape(SEG_LEN, cols_query).astype(jnp.bfloat16)
        stored.append(jnp.stack(after_list))
        mixed = lax.psum_scatter(
            jnp.dot(outputs, out_weight, preferred_element_type=jnp.float32),
            "head",
            scatter_dimension=0,
            tiled=True,
        )
        middle = stream + mixed
        both = jnp.einsum(
            "rd,dtf->rtf",
            lax.all_gather(rms_norm(middle, mlp_gain[layer]), "head", axis=0, tiled=True),
            widening_matrix,
            preferred_element_type=jnp.float32,
        )
        inner = (jax.nn.silu(both[:, 0]) * both[:, 1]).astype(jnp.bfloat16)
        down = lax.psum_scatter(
            jnp.dot(inner, down_weight, preferred_element_type=jnp.float32),
            "head",
            scatter_dimension=0,
            tiled=True,
        )
        stream = middle + down
    return (stream, jnp.stack(stored))


def solution(mesh):
    return jax.shard_map(
        body,
        mesh=mesh,
        in_specs=(
            P(("seg", "head"), None),
            P("seg"),
            P("seg", None, None),
            P(None, None, "head"),
            P(None, None, "head"),
            P(None, "seg", "head"),
            P(),
            P(),
            P(None, None, "head"),
            P(None, None, "head"),
            P(None, "head", None),
            P(None, None, None, "head"),
            P(None, "head", None),
        ),
        out_specs=(P(("seg", "head"), None), P(None, "seg", None, "head")),
        check_vma=False,
    )
```

profile of v0, /device:TPU:0, one launch (start us, length us, event | category | flops | bytes accessed | tf_op | source)
XLA Modules:
  0.0 599.9 jit_solution(14999028639408481068)
XLA Ops:
  16.0 30.0 %all-gather.7.cloned.1.call-done = bf16[512,2048]{1,0:T(8,128)(2,1)} async-done(((bf16[128,2048]{1,0:T(8,128)(2,1)}), bf16[512,2048]{1,0:T(8,128)(2,1)}) %all-gather.7.cloned.1.call-update) | async-done | bytes 2097168 | tf_op jit(solution)/shard_map/all_gather | solution.py:91
  46.0 2.3 fusion.22
  51.8 4.5 slice_bitcast_fusion
  56.3 4.0 copy.66
  60.7 24.4 %all_gather.26 = f32[32,1,512]{2,1,0:T(1,128)S(1)} all-gather(f32[1,1,512]{2,1,0:T(1,128)S(1)} %broadcast_in_dim.27), channel_id=1, replica_groups=mesh['seg'=32,'head'=4] {'seg'}, dimensions={0}, use_global_device_ids=true | all-gather | bytes 67584 | tf_op jit(solution)/shard_map/all_gather | solution.py:17
  85.1 3.5 fusion.33
  92.3 4.7 divide_convert_fusion.1
  97.0 3.3 fusion.40
  100.3 3.1 all-gather.9.cloned.1.call-done
  103.4 38.4 %while.32 = (s32[]{:T(128)}, f32[1,512]{1,0:T(1,128)S(1)}, f32[128,512]{1,0:T(8,128)S(1)}, s32[]{:T(128)}, f32[32,1,512]{2,1,0:T(1,128)S(1)}, /*index=5*/f32[32,128,512]{2,1,0:T(8,128)}, s32[]{:T(128)}, s32[]{:T(128)}) while((s32[]{:T(128)}, f32[1,512]{1,0:T(1,128)S(1)}, f32[128,512]{1,0:T(8,128)S(1)}, s32[]{:T(128)}, ...), condition=%wide.region_4.5_spmd.clone, body=%wide.region_3.4_spmd.clone.sunk | while | flops 263684 | bytes 796787 | solution.py:27
  144.5 5.0 fusion.31
  150.1 46.2 %reduce-scatter.5.cloned.1.call-done = f32[128,2048]{1,0:T(8,128)} async-done(((f32[512,2048]{1,0:T(8,128)}), f32[128,2048]{1,0:T(8,128)}) %reduce-scatter.5.cloned.1.call-update) | async-done | bytes 1048592 | tf_op jit(solution)/shard_map/reduce_scatter | solution.py:162
  199.0 14.2 %fusion.92 = (bf16[1,2048,2,1024]{3,2,1,0:T(2,128)(2,1)}, bf16[1,2048,2,1024]{3,2,1,0:T(2,128)(2,1)}) fusion(bf16[2,2048,2,1024]{3,2,1,0:T(2,128)(2,1)} %param.28), kind=kLoop, calls=%fused_computation.164 | loop fusion | bytes 33554432 | tf_op jit(solution)/shard_map/slice | solution.py:88
  213.2 16.3 %all-gather.11.cloned.1.call-done = bf16[512,2048]{1,0:T(8,128)(2,1)} async-done(((bf16[128,2048]{1,0:T(8,128)(2,1)}), bf16[512,2048]{1,0:T(8,128)(2,1)}) %all-gather.11.cloned.1.call-update) | async-done | bytes 2097168 | tf_op jit(solution)/shard_map/all_gather | solution.py:171
  229.5 8.3 %fusion.5 = f32[512,2,1024]{2,0,1:T(8,128)S(1)} fusion(bf16[1,2048,2,1024]{3,2,1,0:T(2,128)(2,1)} %get-tuple-element.307, bf16[512,2048]{1,0:T(8,128)(2,1)} %all-gather.11.cloned.1.call-done), kind=kOutput, calls=%fused_computation.19 | convolution fusion | flops 4294967296 | bytes 14680064 | tf_op jit(solution)/shard_map/rd,dtf->rtf/dot_general | solution.py:169
  237.8 6.6 %fusion.14 = f32[512,2048]{1,0:T(8,128)} fusion(bf16[2,1024,2048]{2,1,0:T(8,128)(2,1)} %param.29, f32[512,2,1024]{2,0,1:T(8,128)S(1)} %fusion.5), kind=kOutput, calls=%fused_computation.30 | convolution fusion | flops 2150629376 | bytes 12582912 | tf_op jit(solution)/shard_map/dot_general | solution.py:177
  244.5 47.0 %reduce-scatter.7.cloned.1.call-done = f32[128,2048]{1,0:T(8,128)} async-done(((f32[512,2048]{1,0:T(8,128)}), f32[128,2048]{1,0:T(8,128)}) %reduce-scatter.7.cloned.1.call-update) | async-done | bytes 1048592 | tf_op jit(solution)/shard_map/reduce_scatter | solution.py:176
  294.9 29.7 %all-gather.13.cloned.1.call-done = bf16[512,2048]{1,0:T(8,128)(2,1)} async-done(((bf16[128,2048]{1,0:T(8,128)(2,1)}), bf16[512,2048]{1,0:T(8,128)(2,1)}) %all-gather.13.cloned.1.call-update) | async-done | bytes 2097168 | tf_op jit(solution)/shard_map/all_gather | solution.py:91
  324.7 2.3 fusion.20
  330.7 4.0 copy.78
  334.6 26.7 %all_gather.30 = f32[32,1,512]{2,1,0:T(1,128)} all-gather(f32[1,1,512]{2,1,0:T(1,128)S(1)} %broadcast_in_dim.64), channel_id=1, replica_groups=mesh['seg'=32,'head'=4] {'seg'}, dimensions={0}, use_global_device_ids=true | all-gather | bytes 67584 | tf_op jit(solution)/shard_map/all_gather | solution.py:17
  361.3 3.5 fusion.27
  368.7 4.7 divide_convert_fusion
  373.4 3.4 fusion.43
  376.8 5.6 all-gather.15.cloned.1.call-done
  382.4 59.5 %while.33 = (s32[]{:T(128)}, f32[1,512]{1,0:T(1,128)S(1)}, f32[128,512]{1,0:T(8,128)S(1)}, s32[]{:T(128)}, f32[32,1,512]{2,1,0:T(1,128)}, /*index=5*/f32[32,128,512]{2,1,0:T(8,128)}, s32[]{:T(128)}, s32[]{:T(128)}) while((s32[]{:T(128)}, f32[1,512]{1,0:T(1,128)S(1)}, f32[128,512]{1,0:T(8,128)S(1)}, s32[]{:T(128)}, ...), condition=%wide.region_15.16_spmd.clone, body=%wide.region_14.15_spmd.clone.sunk | while | flops 263684 | bytes 796787 | solution.py:27
  443.8 4.9 fusion.25
  448.8 46.8 %reduce-scatter.9.cloned.1.call-done = f32[128,2048]{1,0:T(8,128)} async-done(((f32[512,2048]{1,0:T(8,128)}), f32[128,2048]{1,0:T(8,128)}) %reduce-scatter.9.cloned.1.call-update) | async-done | bytes 1048592 | tf_op jit(solution)/shard_map/reduce_scatter | solution.py:162
  498.4 30.4 %all-gather.17.cloned.1.call-done = bf16[512,2048]{1,0:T(8,128)(2,1)} async-done(((bf16[128,2048]{1,0:T(8,128)(2,1)}), bf16[512,2048]{1,0:T(8,128)(2,1)}) %all-gather.17.cloned.1.call-update) | async-done | bytes 2097168 | tf_op jit(solution)/shard_map/all_gather | solution.py:171
  528.8 8.3 %fusion.4 = f32[512,2,1024]{2,0,1:T(8,128)S(1)} fusion(bf16[1,2048,2,1024]{3,2,1,0:T(2,128)(2,1)} %get-tuple-element.306, bf16[512,2048]{1,0:T(8,128)(2,1)} %all-gather.17.cloned.1.call-done), kind=kOutput, calls=%fused_computation.17 | convolution fusion | flops 4294967296 | bytes 14680064 | tf_op jit(solution)/shard_map/rd,dtf->rtf/dot_general | solution.py:169
  537.1 6.6 %fusion.12 = f32[512,2048]{1,0:T(8,128)} fusion(bf16[2,1024,2048]{2,1,0:T(8,128)(2,1)} %param.29, f32[512,2,1024]{2,0,1:T(8,128)S(1)} %fusion.4), kind=kOutput, calls=%fused_computation.28 | convolution fusion | flops 2150629376 | bytes 12582912 | tf_op jit(solution)/shard_map/dot_general | solution.py:177
  545.7 45.1 %reduce-scatter.11.cloned.1.call-done = f32[128,2048]{1,0:T(8,128)} async-done(((f32[512,2048]{1,0:T(8,128)}), f32[128,2048]{1,0:T(8,128)}) %reduce-scatter.11.cloned.1.call-update) | async-done | bytes 1048592 | tf_op jit(solution)/shard_map/reduce_scatter | solution.py:176
  (293 shorter events, 138.2 us)
Async XLA Ops:
  7.2 5.2 copy-start.4
  7.2 38.8 %all-gather.7.cloned.1.call-start = ((), (), s32[]{:S(2)}) async-start(), calls=%async_computation.4 | async-start | bytes 2621440 | tf_op jit(solution)/shard_map/all_gather | solution.py:91
  10.1 4.1 copy-start.14
  12.3 91.1 %all-gather.9.cloned.1.call-start = ((), (), s32[]{:S(2)}) async-start(), calls=%async_computation.5 | async-start | bytes 8650752 | tf_op jit(solution)/shard_map/all_gather | solution.py:17
  15.6 33.3 %copy-start.25 = (f32[512]{0:T(512)}, f32[512]{0:T(512)S(1)}, u32[]{:S(2)}) copy-start(f32[512]{0:T(512)S(1)} %broadcast_in_dim.28) | copy-start | bytes 6148
  15.6 34.4 %copy-start.21 = (f32[512]{0:T(512)}, f32[512]{0:T(512)S(1)}, u32[]{:S(2)}) copy-start(f32[512]{0:T(512)S(1)} %get-tuple-element.337) | copy-start | bytes 6148
  50.7 145.6 %reduce-scatter.5.cloned.1.call-start = ((), (), s32[]{:S(2)}) async-start(), calls=%async_computation.6 | async-start | bytes 5242880 | tf_op jit(solution)/shard_map/reduce_scatter | solution.py:162
  56.3 4.2 copy-start.30
  60.7 28.6 %copy-start.15 = (pred[512,512]{0,1:T(8,128)(4,1)}, pred[512,512]{0,1:T(8,128)(4,1)S(1)}, u32[]{:S(2)}) copy-start(pred[512,512]{0,1:T(8,128)(4,1)S(1)} %fusion.63) | copy-start | bytes 786436
  97.0 45.0 %copy-start.22 = (f32[512]{0:T(512)S(1)}, f32[512]{0:T(512)}, u32[]{:S(2)}) copy-start(f32[512]{0:T(512)} %copy-done.21) | copy-start | bytes 6148
  97.0 45.0 %copy-start.26 = (f32[512]{0:T(512)S(1)}, f32[512]{0:T(512)}, u32[]{:S(2)}) copy-start(f32[512]{0:T(512)} %copy-done.25) | copy-start | bytes 6148
  144.5 5.1 copy-start.29
  144.5 51.8 %copy-start.2 = (f32[128,2048]{1,0:T(8,128)S(1)}, f32[128,2048]{1,0:T(8,128)}, u32[]{:S(2)}) copy-start(f32[128,2048]{1,0:T(8,128)} %param.17) | copy-start | bytes 3145732
  149.5 80.0 %all-gather.11.cloned.1.call-start = ((), (), s32[]{:S(2)}) async-start(), calls=%async_computation.7 | async-start | bytes 2621440 | tf_op jit(solution)/shard_map/all_gather | solution.py:171
  198.7 92.8 %reduce-scatter.7.cloned.1.call-start = ((), (), s32[]{:S(2)}) async-start(), calls=%async_computation.8 | async-start | bytes 5242880 | tf_op jit(solution)/shard_map/reduce_scatter | solution.py:176
  244.4 48.5 %copy-start.19 = (f32[1,2048]{1,0:T(1,128)S(1)}, f32[1,2048]{1,0:T(1,128)}, u32[]{:S(2)}) copy-start(f32[1,2048]{1,0:T(1,128)} %get-tuple-element.330) | copy-start | bytes 24580
  244.4 49.6 %copy-start.3 = (bf16[256,2048]{0,1:T(8,128)(2,1)S(1)}, bf16[256,2048]{0,1:T(8,128)(2,1)}, u32[]{:S(2)}) copy-start(bf16[256,2048]{0,1:T(8,128)(2,1)} %get-tuple-element.310) | copy-start | bytes 3145732
  244.4 50.2 %copy-start.11 = (bf16[1,128,512]{2,1,0:T(8,128)(2,1)S(1)}, bf16[1,128,512]{2,1,0:T(8,128)(2,1)}, u32[]{:S(2)}) copy-start(bf16[1,128,512]{2,1,0:T(8,128)(2,1)} %get-tuple-element.326) | copy-start | bytes 393220
  244.4 50.3 %copy-start.32 = (f32[8]{0:T(128)S(1)}, f32[8]{0:T(128)}, u32[]{:S(2)}) copy-start(f32[8]{0:T(128)} %get-tuple-element.338) | copy-start | bytes 100
  244.4 80.2 %all-gather.13.cloned.1.call-start = ((), (), s32[]{:S(2)}) async-start(), calls=%async_computation.9 | async-start | bytes 2621440 | tf_op jit(solution)/shard_map/all_gather | solution.py:91
  293.9 88.4 %all-gather.15.cloned.1.call-start = ((), (), s32[]{:S(2)}) async-start(), calls=%async_computation.10 | async-start | bytes 8650752 | tf_op jit(solution)/shard_map/all_gather | solution.py:17
  294.9 32.7 %copy-start.27 = (f32[512]{0:T(512)}, f32[512]{0:T(512)S(1)}, u32[]{:S(2)}) copy-start(f32[512]{0:T(512)S(1)} %broadcast_in_dim.65) | copy-start | bytes 6148
  294.9 33.9 %copy-start.23 = (f32[512]{0:T(512)}, f32[512]{0:T(512)S(1)}, u32[]{:S(2)}) copy-start(f32[512]{0:T(512)S(1)} %get-tuple-element.335) | copy-start | bytes 6148
  328.7 32.6 %copy-start.6 = (f32[2,64,4,128]{3,1,2,0:T(8,128)}, f32[2,64,4,128]{3,1,2,0:T(8,128)S(1)}, u32[]{:S(2)}) copy-start(f32[2,64,4,128]{3,1,2,0:T(8,128)S(1)} %fusion.53) | copy-start | bytes 786436
  329.7 165.9 %reduce-scatter.9.cloned.1.call-start = ((), (), s32[]{:S(2)}) async-start(), calls=%async_computation.11 | async-start | bytes 5242880 | tf_op jit(solution)/shard_map/reduce_scatter | solution.py:162
  373.4 68.6 %copy-start.7 = (f32[2,64,4,128]{3,1,2,0:T(8,128)S(1)}, f32[2,64,4,128]{3,1,2,0:T(8,128)}, u32[]{:S(2)}) copy-start(f32[2,64,4,128]{3,1,2,0:T(8,128)} %copy-done.6) | copy-start | bytes 786436
  373.4 68.6 %copy-start.8 = (f32[1,128,512]{1,2,0:T(8,128)S(1)}, f32[1,128,512]{1,2,0:T(8,128)}, u32[]{:S(2)}) copy-start(f32[1,128,512]{1,2,0:T(8,128)} %copy.98) | copy-start | bytes 786436
  373.4 68.6 %copy-start.24 = (f32[512]{0:T(512)S(1)}, f32[512]{0:T(512)}, u32[]{:S(2)}) copy-start(f32[512]{0:T(512)} %copy-done.23) | copy-start | bytes 6148
  373.4 68.6 %copy-start.28 = (f32[512]{0:T(512)S(1)}, f32[512]{0:T(512)}, u32[]{:S(2)}) copy-start(f32[512]{0:T(512)} %copy-done.27) | copy-start | bytes 6148
  448.7 48.3 %copy-start.20 = (f32[1,2048]{1,0:T(1,128)S(1)}, f32[1,2048]{1,0:T(1,128)}, u32[]{:S(2)}) copy-start(f32[1,2048]{1,0:T(1,128)} %get-tuple-element.328) | copy-start | bytes 24580
  448.8 80.0 %all-gather.17.cloned.1.call-start = ((), (), s32[]{:S(2)}) async-start(), calls=%async_computation.12 | async-start | bytes 2621440 | tf_op jit(solution)/shard_map/all_gather | solution.py:171
  498.0 92.7 %reduce-scatter.11.cloned.1.call-start = ((), (), s32[]{:S(2)}) async-start(), calls=%async_computation.13 | async-start | bytes 5242880 | tf_op jit(solution)/shard_map/reduce_scatter | solution.py:176
  (12 other events, 19.6 us)
Sparse Core Ops, SparseCore 0:
  12.5 33.4 all-gather.6
  50.9 52.5 all-gather.8
  149.6 46.6 reduce-scatter.4
  198.9 30.5 all-gather.10
  244.5 46.9 reduce-scatter.6
  294.0 30.5 all-gather.12
  329.8 52.5 all-gather.14
  448.9 46.6 reduce-scatter.8
  498.2 30.5 all-gather.16
  543.8 46.9 reduce-scatter.10
where the time goes:
time: 604 us; the launch traced here: 600 us
  waiting for transfers between devices  300 us (50%)
  other arithmetic  126 us (21%)
  matrix products  67 us (11%)
  blocking collectives  51.1 us (8%)
  local copies, waits for them, and re-layouts  38 us (6%)
  between operations  14.8 us (2%)
    select_n x128, other arithmetic, hop(): return jax.tree.map(lambda a, b: jnp.where(reached, a, b), new, before)  96.3 us
    reduce_scatter x2, waiting for transfers between devices, body(): lax.psum_scatter(jnp.dot(outputs, out_weight, preferred_element_type=jnp....  93 us
    reduce_scatter x2, waiting for transfers between devices, body(): lax.psum_scatter(jnp.dot(inner, down_weight, preferred_element_type=jnp.f...  92.1 us
    all_gather x2, waiting for transfers between devices, body(): project_piece = lax.all_gather(normed, 'head', axis=0, tiled=True)  59.8 us
    all_gather x2, blocking collectives, prefix(): everything = jax.tree.map(lambda part: lax.all_gather(part, axis), x)  51.1 us
    all_gather x2, waiting for transfers between devices, body(): lax.all_gather(rms_norm(middle, mlp_gain[layer]), 'head', axis=0, tiled=T...  46.7 us
    dot_general x2, matrix products, body(): jnp.einsum('rd,dtf->rtf', lax.all_gather(rms_norm(middle, mlp_gain[layer]...  16.6 us
    slice x1, local copies, waits for them, and re-layouts, body(): widening_matrix = w_gate_up[layer]  14.2 us
  transfers between devices with their start and end apart: 10, of which 10 were waited for; matrix products, arithmetic and copies ran while one was open for 11% of the time, Pallas kernels for 0%

commit v1 on v0

--- a/solution.py
+++ b/solution.py
@@ -10,21 +10,6 @@
 SEG_LEN = 512
 BLOCK = 128
 DEPTH_NUMBER = 2
-
-
-def prefix(x, axis, combine, identity):
-    count, here = (lax.axis_size(axis), lax.axis_index(axis))
-    everything = jax.tree.map(lambda part: lax.all_gather(part, axis), x)
-    start = jax.tree.map(
-        lambda part, zero: jnp.broadcast_to(jnp.asarray(zero, part.dtype), part.shape), x, identity
-    )
-
-    def hop(k, before):
-        reached = k < here
-        new = combine(before, jax.tree.map(lambda part: part[k], everything))
-        return jax.tree.map(lambda a, b: jnp.where(reached, a, b), new, before)
-
-    return lax.fori_loop(0, count, hop, start)
 
 
 def rms_norm(value, gain):
@@ -48,10 +33,6 @@
     return jnp.concatenate(
         [first * cos_part - second * sin_part, second * cos_part + first * sin_part], axis=-1
     )
-
-
-def combine(earlier, later):
-    return (earlier[0] * later[0], later[0] * earlier[1] + later[1])
 
 
 def body(
@@ -117,17 +98,20 @@
             "skgmj,sjkd->smkgd", write_probs, values, preferred_element_type=jnp.float32
         ).reshape(seg_local, MEM, cols_query)
         rates = jnp.repeat(retain[layer], HD, axis=1)[:, None, :]
-        keep_total = jnp.ones((1, cols_query), jnp.float32)
-        add_total = jnp.zeros((MEM, cols_query), jnp.float32)
-        segment = 0
-        keep_total = keep_total * rates[segment]
-        add_total = rates[segment] * add_total + (1.0 - rates[segment]) * written[segment]
-        identity = (
-            jnp.ones((1, cols_query), jnp.float32),
-            jnp.zeros((MEM, cols_query), jnp.float32),
+        here = lax.axis_index("seg")
+        count = lax.axis_size("seg")
+        rate_all = lax.all_gather(retain[layer][0], "seg")
+        written_all = lax.all_gather(written[0], "seg")
+        order = jnp.arange(count)
+        inside = (order[None, :] > order[:, None]) & (order[None, :] < here)
+        span = jnp.prod(jnp.where(inside[:, :, None], rate_all[None, :, :], 1.0), axis=1)
+        weight = jnp.where((order < here)[:, None], span * (1.0 - rate_all), 0.0)
+        carry = jnp.prod(jnp.where((order < here)[:, None], rate_all, 1.0), axis=0)
+        weight = jnp.repeat(weight, HD, axis=1)
+        carry = jnp.repeat(carry, HD)
+        state = carry[None, :] * mem_init[layer] + jnp.sum(
+            weight[:, None, :] * written_all, axis=0
         )
-        keep_before, add_before = prefix((keep_total, add_total), "seg", combine, identity)
-        state = keep_before * mem_init[layer] + add_before
         segment = 0
         memory_read = state.astype(jnp.bfloat16).reshape(MEM, local_kv, group, HD)
         state = rates[segment] * state + (1.0 - rates[segment]) * written[segment]
@@ -160,12 +144,12 @@
         outputs = result.reshape(SEG_LEN, cols_query).astype(jnp.bfloat16)
         stored.append(jnp.stack(after_list))
         mixed = lax.psum_scatter(
-            jnp.dot(outputs, out_weight, preferred_element_type=jnp.float32),
+            jnp.dot(outputs, out_weight, preferred_element_type=jnp.float32).astype(jnp.bfloat16),
             "head",
             scatter_dimension=0,
             tiled=True,
         )
-        middle = stream + mixed
+        middle = stream + mixed.astype(jnp.float32)
         both = jnp.einsum(
             "rd,dtf->rtf",
             lax.all_gather(rms_norm(middle, mlp_gain[layer]), "head", axis=0, tiled=True),
@@ -174,12 +158,12 @@
         )
         inner = (jax.nn.silu(both[:, 0]) * both[:, 1]).astype(jnp.bfloat16)
         down = lax.psum_scatter(
-            jnp.dot(inner, down_weight, preferred_element_type=jnp.float32),
+            jnp.dot(inner, down_weight, preferred_element_type=jnp.float32).astype(jnp.bfloat16),
             "head",
             scatter_dimension=0,
             tiled=True,
         )
-        stream = middle + down
+        stream = middle + down.astype(jnp.float32)
     return (stream, jnp.stack(stored))
 
 

time: 604 us -> 463 us (0.77)
  other arithmetic: 126 us -> 43 us
  waiting for transfers between devices: 300 us -> 251 us
  blocking collectives: 51.1 us -> 42.7 us
    select_n x128 -> x0, other arithmetic: 96.3 us -> none  [hop(): return jax.tree.map(lambda a, b: jnp.where(reached, a, b), new, before)]
    reduce_scatter x2, waiting for transfers between devices: 92.1 us -> 55.8 us  [body(): lax.psum_scatter(jnp.dot(inner, down_weight, preferred_element_type=jnp.f...]
    reduce_scatter x2, waiting for transfers between devices: 93 us -> 57.1 us  [body(): lax.psum_scatter(jnp.dot(outputs, out_weight, preferred_element_type=jnp....]
    all_gather x2, waiting for transfers between devices: 8.73 us -> 31.5 us  [body(): written_all = lax.all_gather(written[0], 'seg')]
    reduce_sum x0 -> x2, other arithmetic: none -> 9.3 us  [body(): jnp.sum(weight[:, None, :] * written_all, axis=0)]
    all_gather x2, blocking collectives: 51.1 us -> 42.7 us  [body(): rate_all = lax.all_gather(retain[layer][0], 'seg')]
  transfers between devices with their start and end apart: 10 -> 10, of which waited for: 10 -> 9; matrix products, arithmetic and copies ran while one was open for 11% -> 15% of each run, Pallas kernels for 0% -> 0%
where the time goes in v1:
time: 463 us; the launch traced here: 457 us
  waiting for transfers between devices  251 us (54%)
  matrix products  63.4 us (14%)
  other arithmetic  43 us (9%)
  blocking collectives  42.7 us (9%)
  local copies, waits for them, and re-layouts  41.2 us (9%)
  between operations  15.1 us (3%)
    all_gather x2, waiting for transfers between devices, body(): project_piece = lax.all_gather(normed, 'head', axis=0, tiled=True)  59.4 us
    reduce_scatter x2, waiting for transfers between devices, body(): lax.psum_scatter(jnp.dot(outputs, out_weight, preferred_element_type=jnp....  57.1 us
    reduce_scatter x2, waiting for transfers between devices, body(): lax.psum_scatter(jnp.dot(inner, down_weight, preferred_element_type=jnp.f...  55.8 us
    all_gather x2, waiting for transfers between devices, body(): lax.all_gather(rms_norm(middle, mlp_gain[layer]), 'head', axis=0, tiled=T...  46.8 us
    all_gather x2, blocking collectives, body(): rate_all = lax.all_gather(retain[layer][0], 'seg')  42.7 us
    all_gather x2, waiting for transfers between devices, body(): written_all = lax.all_gather(written[0], 'seg')  31.5 us
    dot_general x2, matrix products, body(): jnp.einsum('rd,dtf->rtf', lax.all_gather(rms_norm(middle, mlp_gain[layer]...  16.6 us
    slice x1, local copies, waits for them, and re-layouts, body(): widening_matrix = w_gate_up[layer]  14.2 us
  transfers between devices with their start and end apart: 10, of which 9 were waited for; matrix products, arithmetic and copies ran while one was open for 15% of the time, Pallas kernels for 0%

profile of v1, /device:TPU:0, one launch (start us, length us, event | category | flops | bytes accessed | tf_op | source)
XLA Modules:
  0.0 457.2 jit_solution(1360425861947462584)
XLA Ops:
  15.5 30.4 %all-gather.9.cloned.1.call-done = bf16[512,2048]{1,0:T(8,128)(2,1)} async-done(((bf16[128,2048]{1,0:T(8,128)(2,1)}), bf16[512,2048]{1,0:T(8,128)(2,1)}) %all-gather.9.cloned.1.call-update) | async-done | bytes 2097168 | tf_op jit(solution)/shard_map/all_gather | solution.py:72
  45.9 2.3 fusion.26
  50.7 3.8 slice_bitcast_fusion
  54.6 2.5 copy.110
  58.5 21.5 %all-gather = f32[32,1,8]{2,1,0:T(1,128)S(1)} all-gather(f32[1,1,8]{2,1,0:T(1,128)S(1)} %get-tuple-element.43), channel_id=2, replica_groups=mesh['seg'=32,'head'=4] {'seg'}, dimensions={0}, use_global_device_ids=true | all-gather | bytes 1056 | tf_op jit(solution)/shard_map/all_gather | solution.py:103
  80.0 21.2 %all-gather.1 = f32[32,1,8]{2,1,0:T(1,128)S(1)} all-gather(f32[1,1,8]{2,1,0:T(1,128)S(1)} %get-tuple-element.42), channel_id=3, replica_groups=mesh['seg'=32,'head'=4] {'seg'}, dimensions={0}, use_global_device_ids=true | all-gather | bytes 1056 | tf_op jit(solution)/shard_map/all_gather | solution.py:103
  106.4 3.0 fusion.35
  113.1 4.7 %divide_convert_fusion.1 = bf16[2,4,512,640]{2,3,1,0:T(8,128)(2,1)} fusion(f32[2,4,512,512]{2,3,1,0:T(8,128)S(1)} %get-tuple-element.47, f32[2,4,512,128]{2,3,1,0:T(8,128)} %copy-done.2, f32[2,4,512]{2,1,0:T(4,128)S(1)} %fusion.5, f32[2,4,512]{2,1,0:T(4,128)S(1)} %reduce_max.61), kind=kLoop, calls=%fused_computation.5 | loop fusion | flops 10485760 | bytes 15761408 | tf_op jit(solution)/shard_map/convert_element_type | solution.py:137
  117.9 3.0 fusion.42
  121.0 4.7 %multiply_reduce_fusion.1 = f32[128,512]{1,0:T(8,128)S(1)} fusion(f32[32,128,512]{2,1,0:T(8,128)} %all-gather.11.cloned.1.call-done, f32[32,512]{1,0:T(8,128)S(1)} %mul.515), kind=kLoop, calls=%fused_computation.13 | loop fusion | flops 4128768 | bytes 8716288 | tf_op jit(solution)/shard_map/reduce_sum | solution.py:112
  127.3 4.2 convolution_convert_fusion.1
  132.9 27.4 %reduce-scatter.5.cloned.1.call-done = bf16[128,2048]{1,0:T(8,128)(2,1)} async-done(((bf16[512,2048]{1,0:T(8,128)(2,1)}), bf16[128,2048]{1,0:T(8,128)(2,1)}) %reduce-scatter.5.cloned.1.call-update) | async-done | bytes 524304 | tf_op jit(solution)/shard_map/reduce_scatter | solution.py:146
  163.8 14.2 %fusion.95 = (bf16[1,2048,2,1024]{3,2,1,0:T(2,128)(2,1)}, bf16[1,2048,2,1024]{3,2,1,0:T(2,128)(2,1)}) fusion(bf16[2,2048,2,1024]{3,2,1,0:T(2,128)(2,1)} %param.24), kind=kLoop, calls=%fused_computation.169 | loop fusion | bytes 33554432 | tf_op jit(solution)/shard_map/slice | solution.py:69
  178.0 16.3 %all-gather.13.cloned.1.call-done = bf16[512,2048]{1,0:T(8,128)(2,1)} async-done(((bf16[128,2048]{1,0:T(8,128)(2,1)}), bf16[512,2048]{1,0:T(8,128)(2,1)}) %all-gather.13.cloned.1.call-update) | async-done | bytes 2097168 | tf_op jit(solution)/shard_map/all_gather | solution.py:155
  194.3 8.3 %fusion.3 = f32[512,2,1024]{2,0,1:T(8,128)S(1)} fusion(bf16[1,2048,2,1024]{3,2,1,0:T(2,128)(2,1)} %get-tuple-element.12, bf16[512,2048]{1,0:T(8,128)(2,1)} %all-gather.13.cloned.1.call-done), kind=kOutput, calls=%fused_computation.9 | convolution fusion | flops 4294967296 | bytes 14680064 | tf_op jit(solution)/shard_map/rd,dtf->rtf/dot_general | solution.py:153
  202.6 6.0 %fusion.16 = bf16[512,2048]{1,0:T(8,128)(2,1)} fusion(bf16[2,1024,2048]{2,1,0:T(8,128)(2,1)} %param.25, f32[512,2,1024]{2,0,1:T(8,128)S(1)} %fusion.3), kind=kOutput, calls=%fused_computation.26 | convolution fusion | flops 2151677952 | bytes 10485760 | tf_op jit(solution)/shard_map/dot_general | solution.py:161
  208.7 29.9 %reduce-scatter.7.cloned.1.call-done = bf16[128,2048]{1,0:T(8,128)(2,1)} async-done(((bf16[512,2048]{1,0:T(8,128)(2,1)}), bf16[128,2048]{1,0:T(8,128)(2,1)}) %reduce-scatter.7.cloned.1.call-update) | async-done | bytes 524304 | tf_op jit(solution)/shard_map/reduce_scatter | solution.py:160
  242.6 29.0 %all-gather.15.cloned.1.call-done = bf16[512,2048]{1,0:T(8,128)(2,1)} async-done(((bf16[128,2048]{1,0:T(8,128)(2,1)}), bf16[512,2048]{1,0:T(8,128)(2,1)}) %all-gather.15.cloned.1.call-update) | async-done | bytes 2097168 | tf_op jit(solution)/shard_map/all_gather | solution.py:72
  271.6 2.3 fusion.24
  276.9 4.0 copy.123
  282.5 3.5 fusion.30
  289.9 4.6 %divide_convert_fusion = bf16[2,4,512,640]{2,3,1,0:T(8,128)(2,1)} fusion(f32[2,4,512,512]{2,3,1,0:T(8,128)S(1)} %get-tuple-element.53, f32[2,4,512,128]{2,3,1,0:T(8,128)} %copy-done.1, f32[2,4,512]{2,1,0:T(4,128)S(1)} %fusion.4, f32[2,4,512]{2,1,0:T(4,128)S(1)} %reduce_max.65), kind=kLoop, calls=%fused_computation.4 | loop fusion | flops 10485760 | bytes 15761408 | tf_op jit(solution)/shard_map/convert_element_type | solution.py:137
  294.5 3.1 fusion.45
  297.6 31.4 %all-gather.17.cloned.1.call-done = f32[32,128,512]{2,1,0:T(8,128)} async-done(((f32[1,128,512]{2,1,0:T(8,128)}), f32[32,128,512]{2,1,0:T(8,128)}) %all-gather.17.cloned.1.call-update) | async-done | bytes 8388624 | tf_op jit(solution)/shard_map/all_gather | solution.py:104
  329.1 4.6 %multiply_reduce_fusion = f32[128,512]{1,0:T(8,128)S(1)} fusion(f32[32,128,512]{2,1,0:T(8,128)} %all-gather.17.cloned.1.call-done, f32[32,512]{1,0:T(8,128)S(1)} %mul.556), kind=kLoop, calls=%fused_computation.12 | loop fusion | flops 4128768 | bytes 8716288 | tf_op jit(solution)/shard_map/reduce_sum | solution.py:112
  335.4 4.3 convolution_convert_fusion
  339.8 29.7 %reduce-scatter.9.cloned.1.call-done = bf16[128,2048]{1,0:T(8,128)(2,1)} async-done(((bf16[512,2048]{1,0:T(8,128)(2,1)}), bf16[128,2048]{1,0:T(8,128)(2,1)}) %reduce-scatter.9.cloned.1.call-update) | async-done | bytes 524304 | tf_op jit(solution)/shard_map/reduce_scatter | solution.py:146
  373.1 30.4 %all-gather.19.cloned.1.call-done = bf16[512,2048]{1,0:T(8,128)(2,1)} async-done(((bf16[128,2048]{1,0:T(8,128)(2,1)}), bf16[512,2048]{1,0:T(8,128)(2,1)}) %all-gather.19.cloned.1.call-update) | async-done | bytes 2097168 | tf_op jit(solution)/shard_map/all_gather | solution.py:155
  403.5 8.3 %fusion.2 = f32[512,2,1024]{2,0,1:T(8,128)S(1)} fusion(bf16[1,2048,2,1024]{3,2,1,0:T(2,128)(2,1)} %get-tuple-element.13, bf16[512,2048]{1,0:T(8,128)(2,1)} %all-gather.19.cloned.1.call-done), kind=kOutput, calls=%fused_computation.7 | convolution fusion | flops 4294967296 | bytes 14680064 | tf_op jit(solution)/shard_map/rd,dtf->rtf/dot_general | solution.py:153
  411.9 5.9 %fusion.19 = bf16[512,2048]{1,0:T(8,128)(2,1)} fusion(bf16[2,1024,2048]{2,1,0:T(8,128)(2,1)} %param.25, f32[512,2,1024]{2,0,1:T(8,128)S(1)} %fusion.2), kind=kOutput, calls=%fused_computation.27 | convolution fusion | flops 2151677952 | bytes 10485760 | tf_op jit(solution)/shard_map/dot_general | solution.py:161
  422.0 25.9 %reduce-scatter.11.cloned.1.call-done = bf16[128,2048]{1,0:T(8,128)(2,1)} async-done(((bf16[512,2048]{1,0:T(8,128)(2,1)}), bf16[128,2048]{1,0:T(8,128)(2,1)}) %reduce-scatter.11.cloned.1.call-update) | async-done | bytes 524304 | tf_op jit(solution)/shard_map/reduce_scatter | solution.py:160
  447.9 2.2 convert_add_fusion
  (188 shorter events, 49.2 us)
Async XLA Ops:
  7.2 5.2 %copy-start.5 = (bf16[2,2048,256]{2,1,0:T(8,128)(2,1)S(1)}, bf16[2,2048,256]{2,1,0:T(8,128)(2,1)}, u32[]{:S(2)}) copy-start(bf16[2,2048,256]{2,1,0:T(8,128)(2,1)} %param.22) | copy-start | bytes 6291460
  7.2 38.8 %all-gather.9.cloned.1.call-start = ((), (), s32[]{:S(2)}) async-start(), calls=%async_computation.4 | async-start | bytes 2621440 | tf_op jit(solution)/shard_map/all_gather | solution.py:72
  12.3 108.7 %all-gather.11.cloned.1.call-start = ((), (), s32[]{:S(2)}) async-start(), calls=%async_computation.5 | async-start | bytes 8650752 | tf_op jit(solution)/shard_map/all_gather | solution.py:104
  49.8 4.8 %copy-start.10 = (f32[2,64,4,128]{3,1,2,0:T(8,128)}, f32[2,64,4,128]{3,1,2,0:T(8,128)S(1)}, u32[]{:S(2)}) copy-start(f32[2,64,4,128]{3,1,2,0:T(8,128)S(1)} %fusion.58) | copy-start | bytes 786436
  50.7 109.6 %reduce-scatter.5.cloned.1.call-start = ((), (), s32[]{:S(2)}) async-start(), calls=%async_computation.6 | async-start | bytes 2621440 | tf_op jit(solution)/shard_map/reduce_scatter | solution.py:146
  54.6 2.5 copy-start.36
  54.6 3.3 copy-start.41
  54.6 50.0 %copy-start.7 = (f32[2,128,512]{2,1,0:T(8,128)S(1)}, f32[2,128,512]{2,1,0:T(8,128)}, u32[]{:S(2)}) copy-start(f32[2,128,512]{2,1,0:T(8,128)} %param.17) | copy-start | bytes 1572868
  57.1 48.4 %copy-start.32 = (s32[512]{0:T(512)S(1)}, s32[512]{0:T(512)}, u32[]{:S(2)}) copy-start(s32[512]{0:T(512)} %param.14) | copy-start | bytes 6148
  57.1 49.3 %copy-start.6 = (bf16[512,2048]{1,0:T(8,128)(2,1)S(1)}, bf16[512,2048]{1,0:T(8,128)(2,1)}, u32[]{:S(2)}) copy-start(bf16[512,2048]{1,0:T(8,128)(2,1)} %copy.110) | copy-start | bytes 6291460
  103.7 5.6 %copy-start.34 = (f32[8]{0:T(128)}, f32[8]{0:T(128)S(1)}, u32[]{:S(2)}) copy-start(f32[8]{0:T(128)S(1)} %get-tuple-element.9) | copy-start | bytes 100
  106.4 3.7 copy-start.20
  113.1 4.8 %copy-start.17 = (f32[512,2,2,64]{0,3,2,1:T(8,128)S(1)}, f32[512,2,2,64]{0,3,2,1:T(8,128)}, u32[]{:S(2)}) copy-start(f32[512,2,2,64]{0,3,2,1:T(8,128)} %copy-done.16) | copy-start | bytes 1572868
  120.9 4.8 %copy-start.39 = (f32[2,4]{1,0:T(2,128)S(1)}, f32[2,4]{1,0:T(2,128)}, u32[]{:S(2)}) copy-start(f32[2,4]{1,0:T(2,128)} %broadcast_in_dim.135) | copy-start | bytes 100
  131.5 28.7 %copy-start = (f32[128,2048]{1,0:T(8,128)S(1)}, f32[128,2048]{1,0:T(8,128)}, u32[]{:S(2)}) copy-start(f32[128,2048]{1,0:T(8,128)} %param.13) | copy-start | bytes 3145732
  131.6 62.7 %all-gather.13.cloned.1.call-start = ((), (), s32[]{:S(2)}) async-start(), calls=%async_computation.7 | async-start | bytes 2621440 | tf_op jit(solution)/shard_map/all_gather | solution.py:155
  163.6 75.0 %reduce-scatter.7.cloned.1.call-start = ((), (), s32[]{:S(2)}) async-start(), calls=%async_computation.8 | async-start | bytes 2621440 | tf_op jit(solution)/shard_map/reduce_scatter | solution.py:160
  208.6 30.0 %copy-start.4 = (bf16[128,2048]{1,0:T(8,128)(2,1)S(1)}, bf16[128,2048]{1,0:T(8,128)(2,1)}, u32[]{:S(2)}) copy-start(bf16[128,2048]{1,0:T(8,128)(2,1)} %reduce-scatter.5.cloned.1.call-done) | copy-start | bytes 1572868
  208.6 31.3 %copy-start.29 = (f32[1,2048]{1,0:T(1,128)S(1)}, f32[1,2048]{1,0:T(1,128)}, u32[]{:S(2)}) copy-start(f32[1,2048]{1,0:T(1,128)} %get-tuple-element.34) | copy-start | bytes 24580
  208.6 63.0 %all-gather.15.cloned.1.call-start = ((), (), s32[]{:S(2)}) async-start(), calls=%async_computation.9 | async-start | bytes 2621440 | tf_op jit(solution)/shard_map/all_gather | solution.py:72
  240.0 2.5 copy-start.15
  240.9 88.1 %all-gather.17.cloned.1.call-start = ((), (), s32[]{:S(2)}) async-start(), calls=%async_computation.10 | async-start | bytes 8650752 | tf_op jit(solution)/shard_map/all_gather | solution.py:104
  275.5 5.4 %copy-start.12 = (f32[2,64,4,128]{3,1,2,0:T(8,128)}, f32[2,64,4,128]{3,1,2,0:T(8,128)S(1)}, u32[]{:S(2)}) copy-start(f32[2,64,4,128]{3,1,2,0:T(8,128)S(1)} %fusion.55) | copy-start | bytes 786436
  276.4 93.0 %reduce-scatter.9.cloned.1.call-start = ((), (), s32[]{:S(2)}) async-start(), calls=%async_computation.11 | async-start | bytes 2621440 | tf_op jit(solution)/shard_map/reduce_scatter | solution.py:146
  276.9 4.0 copy-start.33
  276.9 4.7 %copy-start.14 = (f32[1,128,512]{2,1,0:T(8,128)S(1)}, f32[1,128,512]{2,1,0:T(8,128)}, u32[]{:S(2)}) copy-start(f32[1,128,512]{2,1,0:T(8,128)} %get-tuple-element.24) | copy-start | bytes 786436
  297.6 36.2 %copy-start.9 = (f32[1,128,512]{1,2,0:T(8,128)S(1)}, f32[1,128,512]{1,2,0:T(8,128)}, u32[]{:S(2)}) copy-start(f32[1,128,512]{1,2,0:T(8,128)} %copy.115) | copy-start | bytes 786436
  297.6 36.2 %copy-start.40 = (f32[2,4]{1,0:T(2,128)S(1)}, f32[2,4]{1,0:T(2,128)}, u32[]{:S(2)}) copy-start(f32[2,4]{1,0:T(2,128)} %broadcast_in_dim.145) | copy-start | bytes 100
  339.7 31.0 %copy-start.30 = (f32[1,2048]{1,0:T(1,128)S(1)}, f32[1,2048]{1,0:T(1,128)}, u32[]{:S(2)}) copy-start(f32[1,2048]{1,0:T(1,128)} %get-tuple-element.37) | copy-start | bytes 24580
  339.7 63.8 %all-gather.19.cloned.1.call-start = ((), (), s32[]{:S(2)}) async-start(), calls=%async_computation.12 | async-start | bytes 2621440 | tf_op jit(solution)/shard_map/all_gather | solution.py:155
  372.8 75.1 %reduce-scatter.11.cloned.1.call-start = ((), (), s32[]{:S(2)}) async-start(), calls=%async_computation.13 | async-start | bytes 2621440 | tf_op jit(solution)/shard_map/reduce_scatter | solution.py:160
  419.0 28.9 %copy-start.3 = (bf16[128,2048]{1,0:T(8,128)(2,1)S(1)}, bf16[128,2048]{1,0:T(8,128)(2,1)}, u32[]{:S(2)}) copy-start(bf16[128,2048]{1,0:T(8,128)(2,1)} %reduce-scatter.9.cloned.1.call-done) | copy-start | bytes 1572868
  (20 other events, 22.6 us)
Sparse Core Ops, SparseCore 0:
  12.4 33.4 all-gather.8
  50.8 52.5 all-gather.10
  131.7 28.5 reduce-scatter.4
  163.7 30.5 all-gather.12
  208.8 29.7 reduce-scatter.6
  241.1 30.5 all-gather.14
  276.5 52.4 all-gather.16
  339.9 29.5 reduce-scatter.8
  372.9 30.5 all-gather.18
  418.0 29.8 reduce-scatter.10

commit v2 on v1

--- a/solution.py
+++ b/solution.py
@@ -100,8 +100,18 @@
         rates = jnp.repeat(retain[layer], HD, axis=1)[:, None, :]
         here = lax.axis_index("seg")
         count = lax.axis_size("seg")
-        rate_all = lax.all_gather(retain[layer][0], "seg")
-        written_all = lax.all_gather(written[0], "seg")
+        rate_row = rates[0]
+        rate_high = rate_row.astype(jnp.bfloat16)
+        rest = rate_row - rate_high.astype(jnp.float32)
+        rate_mid = rest.astype(jnp.bfloat16)
+        rate_low = (rest - rate_mid.astype(jnp.float32)).astype(jnp.bfloat16)
+        payload = jnp.concatenate(
+            [written[0].astype(jnp.bfloat16), rate_high, rate_mid, rate_low], axis=0
+        )
+        gathered = lax.all_gather(payload, "seg")
+        written_all = gathered[:, :MEM].astype(jnp.float32)
+        rate_parts = gathered[:, MEM:, ::HD].astype(jnp.float32)
+        rate_all = rate_parts[:, 0] + rate_parts[:, 1] + rate_parts[:, 2]
         order = jnp.arange(count)
         inside = (order[None, :] > order[:, None]) & (order[None, :] < here)
         span = jnp.prod(jnp.where(inside[:, :, None], rate_all[None, :, :], 1.0), axis=1)

time: 463 us -> 435 us (0.940)
  blocking collectives: 42.7 us -> 0 us
  waiting for transfers between devices: 251 us -> 269 us
    all_gather x2 -> x0, blocking collectives: 42.7 us -> none  [body(): rate_all = lax.all_gather(retain[layer][0], 'seg')]
    all_gather x2, waiting for transfers between devices: 31.5 us -> 49 us  [body(): gathered = lax.all_gather(payload, 'seg')]
  transfers between devices with their start and end apart: 10 -> 10, of which waited for: 9 -> 10; matrix products, arithmetic and copies ran while one was open for 15% -> 15% of each run, Pallas kernels for 0% -> 0%
where the time goes in v2:
time: 435 us; the launch traced here: 430 us
  waiting for transfers between devices  269 us (62%)
  matrix products  65.6 us (15%)
  local copies, waits for them, and re-layouts  40.9 us (9%)
  other arithmetic  38.5 us (9%)
  between operations  15.1 us (3%)
    all_gather x2, waiting for transfers between devices, body(): project_piece = lax.all_gather(normed, 'head', axis=0, tiled=True)  58.6 us
    reduce_scatter x2, waiting for transfers between devices, body(): lax.psum_scatter(jnp.dot(outputs, out_weight, preferred_element_type=jnp....  57.7 us
    reduce_scatter x2, waiting for transfers between devices, body(): lax.psum_scatter(jnp.dot(inner, down_weight, preferred_element_type=jnp.f...  56.4 us
    all_gather x2, waiting for transfers between devices, body(): gathered = lax.all_gather(payload, 'seg')  49 us
    all_gather x2, waiting for transfers between devices, body(): lax.all_gather(rms_norm(middle, mlp_gain[layer]), 'head', axis=0, tiled=T...  46.7 us
    dot_general x2, matrix products, body(): jnp.einsum('rd,dtf->rtf', lax.all_gather(rms_norm(middle, mlp_gain[layer]...  16.6 us
    slice x1, local copies, waits for them, and re-layouts, body(): widening_matrix = w_gate_up[layer]  14.2 us
    dot_general x2, matrix products, body(): jnp.dot(inner, down_weight, preferred_element_type=jnp.float32)  11.9 us
  transfers between devices with their start and end apart: 10, of which 10 were waited for; matrix products, arithmetic and copies ran while one was open for 15% of the time, Pallas kernels for 0%

profile of v2, /device:TPU:0, one launch (start us, length us, event | category | flops | bytes accessed | tf_op | source)
XLA Modules:
  0.0 430.2 jit_solution(6112931591459669940)
XLA Ops:
  10.1 2.2 multiply_convert_fusion.3
  16.2 29.7 %all-gather.11.cloned.1.call-done = bf16[512,2048]{1,0:T(8,128)(2,1)} async-done(((bf16[128,2048]{1,0:T(8,128)(2,1)}), bf16[512,2048]{1,0:T(8,128)(2,1)}) %all-gather.11.cloned.1.call-update) | async-done | bytes 2097168 | tf_op jit(solution)/shard_map/all_gather | solution.py:72
  45.9 2.3 fusion.26
  51.9 3.8 slice_bitcast_fusion
  55.7 2.5 copy.128
  59.6 3.6 fusion.35
  66.8 4.6 %divide_convert_fusion.1 = bf16[2,4,512,640]{2,3,1,0:T(8,128)(2,1)} fusion(f32[2,4,512,512]{2,3,1,0:T(8,128)S(1)} %get-tuple-element.49, f32[2,4,512,128]{2,3,1,0:T(8,128)} %copy-done.2, f32[2,4,512]{2,1,0:T(4,128)S(1)} %fusion.5, f32[2,4,512]{2,1,0:T(4,128)S(1)} %reduce_max.61), kind=kLoop, calls=%fused_computation.5 | loop fusion | flops 10485760 | bytes 15761408 | tf_op jit(solution)/shard_map/convert_element_type | solution.py:147
  71.4 3.0 fusion.42
  74.5 23.0 %all-gather.19.cloned.1.call-done = bf16[32,131,512]{2,1,0:T(8,128)(2,1)} async-done(((bf16[1,131,512]{2,1,0:T(8,128)(2,1)}), bf16[32,131,512]{2,1,0:T(8,128)(2,1)}) %all-gather.19.cloned.1.call-update) | async-done | bytes 4292624 | tf_op jit(solution)/shard_map/all_gather | solution.py:111
  99.8 3.1 multiply_reduce_fusion.1
  104.7 4.2 convolution_convert_fusion.1
  110.3 28.2 %reduce-scatter.5.cloned.1.call-done = bf16[128,2048]{1,0:T(8,128)(2,1)} async-done(((bf16[512,2048]{1,0:T(8,128)(2,1)}), bf16[128,2048]{1,0:T(8,128)(2,1)}) %reduce-scatter.5.cloned.1.call-update) | async-done | bytes 524304 | tf_op jit(solution)/shard_map/reduce_scatter | solution.py:156
  142.0 14.2 %fusion.100 = (bf16[1,2048,2,1024]{3,2,1,0:T(2,128)(2,1)}, bf16[1,2048,2,1024]{3,2,1,0:T(2,128)(2,1)}) fusion(bf16[2,2048,2,1024]{3,2,1,0:T(2,128)(2,1)} %param.24), kind=kLoop, calls=%fused_computation.186 | loop fusion | bytes 33554432 | tf_op jit(solution)/shard_map/slice | solution.py:69
  156.2 16.3 %all-gather.13.cloned.1.call-done = bf16[512,2048]{1,0:T(8,128)(2,1)} async-done(((bf16[128,2048]{1,0:T(8,128)(2,1)}), bf16[512,2048]{1,0:T(8,128)(2,1)}) %all-gather.13.cloned.1.call-update) | async-done | bytes 2097168 | tf_op jit(solution)/shard_map/all_gather | solution.py:165
  172.5 8.3 %fusion.3 = f32[512,2,1024]{2,0,1:T(8,128)S(1)} fusion(bf16[1,2048,2,1024]{3,2,1,0:T(2,128)(2,1)} %get-tuple-element.10, bf16[512,2048]{1,0:T(8,128)(2,1)} %all-gather.13.cloned.1.call-done), kind=kOutput, calls=%fused_computation.9 | convolution fusion | flops 4294967296 | bytes 14680064 | tf_op jit(solution)/shard_map/rd,dtf->rtf/dot_general | solution.py:163
  180.8 5.9 %fusion.16 = bf16[512,2048]{1,0:T(8,128)(2,1)} fusion(bf16[2,1024,2048]{2,1,0:T(8,128)(2,1)} %param.25, f32[512,2,1024]{2,0,1:T(8,128)S(1)} %fusion.3), kind=kOutput, calls=%fused_computation.26 | convolution fusion | flops 2151677952 | bytes 10485760 | tf_op jit(solution)/shard_map/dot_general | solution.py:171
  186.9 29.9 %reduce-scatter.7.cloned.1.call-done = bf16[128,2048]{1,0:T(8,128)(2,1)} async-done(((bf16[512,2048]{1,0:T(8,128)(2,1)}), bf16[128,2048]{1,0:T(8,128)(2,1)}) %reduce-scatter.7.cloned.1.call-update) | async-done | bytes 524304 | tf_op jit(solution)/shard_map/reduce_scatter | solution.py:170
  221.0 28.9 %all-gather.15.cloned.1.call-done = bf16[512,2048]{1,0:T(8,128)(2,1)} async-done(((bf16[128,2048]{1,0:T(8,128)(2,1)}), bf16[512,2048]{1,0:T(8,128)(2,1)}) %all-gather.15.cloned.1.call-update) | async-done | bytes 2097168 | tf_op jit(solution)/shard_map/all_gather | solution.py:72
  249.8 2.3 fusion.24
  255.5 4.0 copy.143
  260.3 3.5 fusion.30
  267.7 4.6 %divide_convert_fusion = bf16[2,4,512,640]{2,3,1,0:T(8,128)(2,1)} fusion(f32[2,4,512,512]{2,3,1,0:T(8,128)S(1)} %get-tuple-element.57, f32[2,4,512,128]{2,3,1,0:T(8,128)} %copy-done.1, f32[2,4,512]{2,1,0:T(4,128)S(1)} %fusion.4, f32[2,4,512]{2,1,0:T(4,128)S(1)} %reduce_max.65), kind=kLoop, calls=%fused_computation.4 | loop fusion | flops 10485760 | bytes 15761408 | tf_op jit(solution)/shard_map/convert_element_type | solution.py:147
  272.3 3.1 fusion.45
  275.4 26.0 %all-gather.21.cloned.1.call-done = bf16[32,131,512]{2,1,0:T(8,128)(2,1)} async-done(((bf16[1,131,512]{2,1,0:T(8,128)(2,1)}), bf16[32,131,512]{2,1,0:T(8,128)(2,1)}) %all-gather.21.cloned.1.call-update) | async-done | bytes 4292624 | tf_op jit(solution)/shard_map/all_gather | solution.py:111
  303.7 3.1 multiply_reduce_fusion
  308.6 4.3 %convolution_convert_fusion = bf16[512,2048]{1,0:T(8,128)(2,1)} fusion(bf16[512,512]{0,1:T(8,128)(2,1)S(1)} %bitcast.281, bf16[2,512,2048]{2,1,0:T(8,128)(2,1)} %param.23), kind=kOutput, calls=%fused_computation.28 | convolution fusion | flops 1074790400 | bytes 4718592 | tf_op jit(solution)/shard_map/dot_general | solution.py:157
  313.0 29.5 %reduce-scatter.9.cloned.1.call-done = bf16[128,2048]{1,0:T(8,128)(2,1)} async-done(((bf16[512,2048]{1,0:T(8,128)(2,1)}), bf16[128,2048]{1,0:T(8,128)(2,1)}) %reduce-scatter.9.cloned.1.call-update) | async-done | bytes 524304 | tf_op jit(solution)/shard_map/reduce_scatter | solution.py:156
  346.1 30.4 %all-gather.17.cloned.1.call-done = bf16[512,2048]{1,0:T(8,128)(2,1)} async-done(((bf16[128,2048]{1,0:T(8,128)(2,1)}), bf16[512,2048]{1,0:T(8,128)(2,1)}) %all-gather.17.cloned.1.call-update) | async-done | bytes 2097168 | tf_op jit(solution)/shard_map/all_gather | solution.py:165
  376.6 8.3 %fusion.2 = f32[512,2,1024]{2,0,1:T(8,128)S(1)} fusion(bf16[1,2048,2,1024]{3,2,1,0:T(2,128)(2,1)} %get-tuple-element.11, bf16[512,2048]{1,0:T(8,128)(2,1)} %all-gather.17.cloned.1.call-done), kind=kOutput, calls=%fused_computation.7 | convolution fusion | flops 4294967296 | bytes 14680064 | tf_op jit(solution)/shard_map/rd,dtf->rtf/dot_general | solution.py:163
  384.9 6.0 %fusion.19 = bf16[512,2048]{1,0:T(8,128)(2,1)} fusion(bf16[2,1024,2048]{2,1,0:T(8,128)(2,1)} %param.25, f32[512,2,1024]{2,0,1:T(8,128)S(1)} %fusion.2), kind=kOutput, calls=%fused_computation.27 | convolution fusion | flops 2151677952 | bytes 10485760 | tf_op jit(solution)/shard_map/dot_general | solution.py:171
  394.4 26.5 %reduce-scatter.11.cloned.1.call-done = bf16[128,2048]{1,0:T(8,128)(2,1)} async-done(((bf16[512,2048]{1,0:T(8,128)(2,1)}), bf16[128,2048]{1,0:T(8,128)(2,1)}) %reduce-scatter.11.cloned.1.call-update) | async-done | bytes 524304 | tf_op jit(solution)/shard_map/reduce_scatter | solution.py:170
  420.9 2.2 convert_add_fusion
  (187 shorter events, 47.4 us)
Async XLA Ops:
  7.2 5.2 %copy-start.5 = (bf16[2,2048,256]{2,1,0:T(8,128)(2,1)S(1)}, bf16[2,2048,256]{2,1,0:T(8,128)(2,1)}, u32[]{:S(2)}) copy-start(bf16[2,2048,256]{2,1,0:T(8,128)(2,1)} %param.22) | copy-start | bytes 6291460
  7.2 38.8 %all-gather.11.cloned.1.call-start = ((), (), s32[]{:S(2)}) async-start(), calls=%async_computation.4 | async-start | bytes 2621440 | tf_op jit(solution)/shard_map/all_gather | solution.py:72
  12.3 85.2 %all-gather.19.cloned.1.call-start = ((), (), s32[]{:S(2)}) async-start(), calls=%async_computation.12 | async-start | bytes 4595712 | tf_op jit(solution)/shard_map/all_gather | solution.py:111
  51.3 87.2 %reduce-scatter.5.cloned.1.call-start = ((), (), s32[]{:S(2)}) async-start(), calls=%async_computation.5 | async-start | bytes 2621440 | tf_op jit(solution)/shard_map/reduce_scatter | solution.py:156
  55.7 2.5 copy-start.32
  55.7 2.7 copy-start.6
  55.7 3.5 copy-start.27
  59.5 4.4 %copy-start.16 = (pred[512,512]{0,1:T(8,128)(4,1)}, pred[512,512]{0,1:T(8,128)(4,1)S(1)}, u32[]{:S(2)}) copy-start(pred[512,512]{0,1:T(8,128)(4,1)S(1)} %fusion.65) | copy-start | bytes 786436
  59.5 40.0 %copy-start.28 = (pred[32]{0:T(512)(128)(4,1)}, pred[32]{0:T(512)(128)(4,1)S(1)}, u32[]{:S(2)}) copy-start(pred[32]{0:T(512)(128)(4,1)S(1)} %iota_compare_fusion.2) | copy-start | bytes 100
  59.5 39.4 %copy-start.22 = (pred[32,32]{1,0:T(8,128)(4,1)}, pred[32,32]{1,0:T(8,128)(4,1)S(1)}, u32[]{:S(2)}) copy-start(pred[32,32]{1,0:T(8,128)(4,1)S(1)} %fusion.81) | copy-start | bytes 3076
  66.8 4.6 %copy-start.12 = (f32[512,2,2,64]{0,3,2,1:T(8,128)S(1)}, f32[512,2,2,64]{0,3,2,1:T(8,128)}, u32[]{:S(2)}) copy-start(f32[512,2,2,64]{0,3,2,1:T(8,128)} %copy-done.11) | copy-start | bytes 1572868
  99.6 3.4 copy-start.30
  108.9 29.5 %copy-start = (f32[128,2048]{1,0:T(8,128)S(1)}, f32[128,2048]{1,0:T(8,128)}, u32[]{:S(2)}) copy-start(f32[128,2048]{1,0:T(8,128)} %param.13) | copy-start | bytes 3145732
  109.0 63.6 %all-gather.13.cloned.1.call-start = ((), (), s32[]{:S(2)}) async-start(), calls=%async_computation.6 | async-start | bytes 2621440 | tf_op jit(solution)/shard_map/all_gather | solution.py:165
  141.8 75.0 %reduce-scatter.7.cloned.1.call-start = ((), (), s32[]{:S(2)}) async-start(), calls=%async_computation.7 | async-start | bytes 2621440 | tf_op jit(solution)/shard_map/reduce_scatter | solution.py:170
  186.8 30.0 %copy-start.4 = (bf16[128,2048]{1,0:T(8,128)(2,1)S(1)}, bf16[128,2048]{1,0:T(8,128)(2,1)}, u32[]{:S(2)}) copy-start(bf16[128,2048]{1,0:T(8,128)(2,1)} %reduce-scatter.5.cloned.1.call-done) | copy-start | bytes 1572868
  186.8 31.3 %copy-start.24 = (f32[1,2048]{1,0:T(1,128)S(1)}, f32[1,2048]{1,0:T(1,128)}, u32[]{:S(2)}) copy-start(f32[1,2048]{1,0:T(1,128)} %get-tuple-element.32) | copy-start | bytes 24580
  186.8 63.0 %all-gather.15.cloned.1.call-start = ((), (), s32[]{:S(2)}) async-start(), calls=%async_computation.8 | async-start | bytes 2621440 | tf_op jit(solution)/shard_map/all_gather | solution.py:72
  218.1 2.5 copy-start.10
  218.1 2.7 copy-start.33
  219.1 82.3 %all-gather.21.cloned.1.call-start = ((), (), s32[]{:S(2)}) async-start(), calls=%async_computation.13 | async-start | bytes 4595712 | tf_op jit(solution)/shard_map/all_gather | solution.py:111
  220.9 31.3 %copy-start.20 = (f32[8,64]{1,0:T(8,128)}, f32[8,64]{1,0:T(8,128)S(1)}, u32[]{:S(2)}) copy-start(f32[8,64]{1,0:T(8,128)S(1)} %broadcast_in_dim.151) | copy-start | bytes 6148
  255.2 87.3 %reduce-scatter.9.cloned.1.call-start = ((), (), s32[]{:S(2)}) async-start(), calls=%async_computation.9 | async-start | bytes 2621440 | tf_op jit(solution)/shard_map/reduce_scatter | solution.py:156
  255.5 4.0 copy-start.9
  272.3 30.4 %copy-start.29 = (pred[32]{0:T(512)(128)(4,1)S(1)}, pred[32]{0:T(512)(128)(4,1)}, u32[]{:S(2)}) copy-start(pred[32]{0:T(512)(128)(4,1)} %copy-done.28) | copy-start | bytes 100
  272.3 30.6 %copy-start.23 = (pred[32,32]{1,0:T(8,128)(4,1)S(1)}, pred[32,32]{1,0:T(8,128)(4,1)}, u32[]{:S(2)}) copy-start(pred[32,32]{1,0:T(8,128)(4,1)} %copy-done.22) | copy-start | bytes 3076
  303.7 3.3 copy-start.8
  313.0 30.8 %copy-start.25 = (f32[1,2048]{1,0:T(1,128)S(1)}, f32[1,2048]{1,0:T(1,128)}, u32[]{:S(2)}) copy-start(f32[1,2048]{1,0:T(1,128)} %get-tuple-element.35) | copy-start | bytes 24580
  313.0 63.6 %all-gather.17.cloned.1.call-start = ((), (), s32[]{:S(2)}) async-start(), calls=%async_computation.10 | async-start | bytes 2621440 | tf_op jit(solution)/shard_map/all_gather | solution.py:165
  345.8 75.0 %reduce-scatter.11.cloned.1.call-start = ((), (), s32[]{:S(2)}) async-start(), calls=%async_computation.11 | async-start | bytes 2621440 | tf_op jit(solution)/shard_map/reduce_scatter | solution.py:170
  390.9 2.5 copy-start.7
  391.8 29.0 %copy-start.3 = (bf16[128,2048]{1,0:T(8,128)(2,1)S(1)}, bf16[128,2048]{1,0:T(8,128)(2,1)}, u32[]{:S(2)}) copy-start(bf16[128,2048]{1,0:T(8,128)(2,1)} %reduce-scatter.9.cloned.1.call-done) | copy-start | bytes 1572868
  (13 other events, 13.8 us)
Sparse Core Ops, SparseCore 0:
  12.4 33.4 all-gather.10
  51.4 46.0 all-gather.18
  109.1 29.3 reduce-scatter.4
  141.9 30.5 all-gather.12
  186.9 29.7 reduce-scatter.6
  219.2 30.5 all-gather.14
  255.4 46.0 all-gather.20
  313.1 29.3 reduce-scatter.8
  346.0 30.5 all-gather.16
  391.0 29.7 reduce-scatter.10

commit v3 on v2

--- a/solution.py
+++ b/solution.py
@@ -10,6 +10,48 @@
 SEG_LEN = 512
 BLOCK = 128
 DEPTH_NUMBER = 2
+
+
+def ring_pairs(count, step):
+    return [(i, (i + step) % count) for i in range(count)]
+
+
+def ring_gather(piece, axis):
+    count = lax.axis_size(axis)
+    here = lax.axis_index(axis)
+    rows = piece.shape[0]
+    half = rows // 2
+    ahead = ring_pairs(count, 1)
+    behind = ring_pairs(count, -1)
+    from_before = lax.ppermute(piece, axis, ahead)
+    from_after = lax.ppermute(piece, axis, behind)
+    far_top = lax.ppermute(from_before[:half], axis, ahead)
+    far_bottom = lax.ppermute(from_after[half:], axis, behind)
+    relative = jnp.concatenate([piece, from_after, far_top, far_bottom, from_before], axis=0)
+    return jnp.roll(relative, here * rows, axis=0)
+
+
+def ring_scatter(whole, axis):
+    count = lax.axis_size(axis)
+    here = lax.axis_index(axis)
+    rows = whole.shape[0] // count
+    half = rows // 2
+    ahead = ring_pairs(count, 1)
+    behind = ring_pairs(count, -1)
+
+    def block(offset):
+        return lax.dynamic_slice_in_dim(whole, ((here + offset) % count) * rows, rows)
+
+    far = block(2)
+    sent_top = lax.ppermute(far[:half].astype(jnp.bfloat16), axis, ahead)
+    sent_bottom = lax.ppermute(far[half:].astype(jnp.bfloat16), axis, behind)
+    next_part = block(1)
+    next_part = jnp.concatenate([next_part[:half] + sent_top.astype(jnp.float32), next_part[half:]])
+    prev_part = block(-1)
+    prev_part = jnp.concatenate([prev_part[:half], prev_part[half:] + sent_bottom.astype(jnp.float32)])
+    got_before = lax.ppermute(next_part.astype(jnp.bfloat16), axis, ahead)
+    got_after = lax.ppermute(prev_part.astype(jnp.bfloat16), axis, behind)
+    return block(0) + got_before.astype(jnp.float32) + got_after.astype(jnp.float32)
 
 
 def rms_norm(value, gain):
@@ -69,7 +111,7 @@
         widening_matrix = w_gate_up[layer]
         down_weight = w_down[layer]
         normed = rms_norm(stream, attn_gain[layer])
-        project_piece = lax.all_gather(normed, "head", axis=0, tiled=True)
+        project_piece = ring_gather(normed, "head")
         projected = jnp.concatenate(
             [
                 jnp.dot(project_piece, query_weight, preferred_element_type=jnp.float32),
@@ -153,27 +195,19 @@
         )
         outputs = result.reshape(SEG_LEN, cols_query).astype(jnp.bfloat16)
         stored.append(jnp.stack(after_list))
-        mixed = lax.psum_scatter(
-            jnp.dot(outputs, out_weight, preferred_element_type=jnp.float32).astype(jnp.bfloat16),
-            "head",
-            scatter_dimension=0,
-            tiled=True,
-        )
-        middle = stream + mixed.astype(jnp.float32)
+        mixed = ring_scatter(
+            jnp.dot(outputs, out_weight, preferred_element_type=jnp.float32), "head"
+        )
+        middle = stream + mixed
         both = jnp.einsum(
             "rd,dtf->rtf",
-            lax.all_gather(rms_norm(middle, mlp_gain[layer]), "head", axis=0, tiled=True),
+            ring_gather(rms_norm(middle, mlp_gain[layer]), "head"),
             widening_matrix,
             preferred_element_type=jnp.float32,
         )
         inner = (jax.nn.silu(both[:, 0]) * both[:, 1]).astype(jnp.bfloat16)
-        down = lax.psum_scatter(
-            jnp.dot(inner, down_weight, preferred_element_type=jnp.float32).astype(jnp.bfloat16),
-            "head",
-            scatter_dimension=0,
-            tiled=True,
-        )
-        stream = middle + down.astype(jnp.float32)
+        down = ring_scatter(jnp.dot(inner, down_weight, preferred_element_type=jnp.float32), "head")
+        stream = middle + down
     return (stream, jnp.stack(stored))
 
 

time: 435 us -> 392 us (0.901)
  waiting for transfers between devices: 269 us -> 156 us
  starting transfers between devices: 1.58 us -> 55.8 us
  local copies, waits for them, and re-layouts: 40.9 us -> 62.9 us
  matrix products: 65.6 us -> 54.7 us
    reduce_scatter x4 -> x0, waiting for transfers between devices: 114 us -> none  [the longest x2 57.7 us: body(): lax.psum_scatter(jnp.dot(outputs, out_weight, preferred_element_type=jnp....]
    all_gather x4 -> x0, waiting for transfers between devices: 105 us -> none  [the longest x2 58.6 us: body(): project_piece = lax.all_gather(normed, 'head', axis=0, tiled=True)]
    ppermute x0 -> x32, waiting for transfers between devices: none -> 105 us  [the longest x4 41.4 us: ring_gather(): from_before = lax.ppermute(piece, axis, ahead)]
    ppermute x0 -> x32, starting transfers between devices: none -> 55.5 us  [the longest x4 12 us: ring_gather(): far_bottom = lax.ppermute(from_after[half:], axis, behind)]
    unnamed x73 -> x95, local copies, waits for them, and re-layouts: 2.27 us -> 12.3 us
    convert_element_type x4 -> x0, other arithmetic: 7.17 us -> none  [rms_norm(): return (value * factor * gain).astype(jnp.bfloat16)]
    dot_general x2, matrix products: 11.9 us -> 6.98 us  [body(): jnp.dot(inner, down_weight, preferred_element_type=jnp.float32)]
    dot_general x2, matrix products: 16.6 us -> 12.2 us  [body(): jnp.einsum('rd,dtf->rtf', ring_gather(rms_norm(middle, mlp_gain[layer]),...]
  transfers between devices with their start and end apart: 10 -> 34, of which waited for: 10 -> 25; matrix products, arithmetic and copies ran while one was open for 15% -> 21% of each run, Pallas kernels for 0% -> 0%
where the time goes in v3:
time: 392 us; the launch traced here: 386 us
  waiting for transfers between devices  156 us (40%)
  local copies, waits for them, and re-layouts  62.9 us (16%)
  starting transfers between devices  55.8 us (14%)
  matrix products  54.7 us (14%)
  other arithmetic  41.7 us (11%)
  between operations  15.4 us (4%)
    all_gather x2, waiting for transfers between devices, body(): gathered = lax.all_gather(payload, 'seg')  51.1 us
    ppermute x4, waiting for transfers between devices, ring_gather(): from_before = lax.ppermute(piece, axis, ahead)  41.4 us
    ppermute x4, waiting for transfers between devices, ring_scatter(): got_before = lax.ppermute(next_part.astype(jnp.bfloat16), axis, ahead)  30.7 us
    ppermute x4, waiting for transfers between devices, ring_scatter(): sent_top = lax.ppermute(far[:half].astype(jnp.bfloat16), axis, ahead)  19.2 us
    slice x1, local copies, waits for them, and re-layouts, body(): widening_matrix = w_gate_up[layer]  14 us
    unnamed x95, local copies, waits for them, and re-layouts  12.3 us
    dot_general x2, matrix products, body(): jnp.einsum('rd,dtf->rtf', ring_gather(rms_norm(middle, mlp_gain[layer]),...  12.2 us
    ppermute x4, starting transfers between devices, ring_gather(): far_bottom = lax.ppermute(from_after[half:], axis, behind)  12 us
  transfers between devices with their start and end apart: 34, of which 25 were waited for; matrix products, arithmetic and copies ran while one was open for 21% of the time, Pallas kernels for 0%

profile of v3, /device:TPU:0, one launch (start us, length us, event | category | flops | bytes accessed | tf_op | source)
XLA Modules:
  0.0 386.3 jit_solution(6350148239906696440)
XLA Ops:
  12.5 4.1 %collective-permute-start = (bf16[128,2048]{1,0:T(8,128)(2,1)}, bf16[128,2048]{1,0:T(8,128)(2,1)}, u32[]{:S(2)}, u32[]{:S(2)}) collective-permute-start(bf16[128,2048]{1,0:T(8,128)(2,1)} %get-tuple-element.22), channel_id=1, source_target_pairs={{0,3},{1,0},{2,1},{3,2},{4,7},{5,4},{6,5},{7,6},{8,11},{9,8},{10,9... | collective-permute-start | bytes 1572872 | tf_op jit(solution)/shard_map/ppermute | solution.py:27
  20.4 11.1 %collective-permute-done.1 = bf16[128,2048]{1,0:T(8,128)(2,1)} collective-permute-done((bf16[128,2048]{1,0:T(8,128)(2,1)}, bf16[128,2048]{1,0:T(8,128)(2,1)}, u32[]{:S(2)}, u32[]{:S(2)}) %collective-permute-start.1) | collective-permute-done | bytes 524320 | tf_op jit(solution)/shard_map/ppermute | solution.py:26
  34.9 3.3 collective-permute-start.3
  51.0 3.8 slice_bitcast_fusion
  58.8 3.7 fusion.37
  66.1 4.6 %divide_convert_fusion.1 = bf16[2,4,512,640]{2,3,1,0:T(8,128)(2,1)} fusion(f32[2,4,512,512]{2,3,1,0:T(8,128)S(1)} %get-tuple-element.86, f32[2,4,512,128]{2,3,1,0:T(8,128)} %copy-done.1, f32[2,4,512]{2,1,0:T(4,128)S(1)} %fusion.5, f32[2,4,512]{2,1,0:T(4,128)S(1)} %reduce_max.61), kind=kLoop, calls=%fused_computation.5 | loop fusion | flops 10485760 | bytes 15761408 | tf_op jit(solution)/shard_map/convert_element_type | solution.py:189
  73.7 25.3 %all-gather.7.cloned.1.call-done = bf16[32,131,512]{2,1,0:T(8,128)(2,1)} async-done(((bf16[1,131,512]{2,1,0:T(8,128)(2,1)}), bf16[32,131,512]{2,1,0:T(8,128)(2,1)}) %all-gather.7.cloned.1.call-update) | async-done | bytes 4292624 | tf_op jit(solution)/shard_map/all_gather | solution.py:153
  101.4 3.1 multiply_reduce_fusion.1
  115.9 5.1 %collective-permute-done.4 = bf16[64,2048]{1,0:T(8,128)(2,1)S(1)} collective-permute-done((bf16[64,2048]{1,0:T(8,128)(2,1)S(1)}, bf16[64,2048]{1,0:T(8,128)(2,1)S(1)}, u32[]{:S(2)}, u32[]{:S(2)}) %collective-permute-start.4) | collective-permute-done | bytes 262176 | tf_op jit(solution)/shard_map/ppermute | solution.py:46
  128.3 9.9 %collective-permute-done.5 = bf16[128,2048]{1,0:T(8,128)(2,1)S(1)} collective-permute-done((bf16[128,2048]{1,0:T(8,128)(2,1)}, bf16[128,2048]{1,0:T(8,128)(2,1)S(1)}, u32[]{:S(2)}, u32[]{:S(2)}) %collective-permute-start.5) | collective-permute-done | bytes 524320 | tf_op jit(solution)/shard_map/ppermute | solution.py:52
  143.9 10.1 %collective-permute-done.9 = bf16[128,2048]{1,0:T(8,128)(2,1)S(1)} collective-permute-done((bf16[128,2048]{1,0:T(8,128)(2,1)S(1)}, bf16[128,2048]{1,0:T(8,128)(2,1)S(1)}, u32[]{:S(2)}, u32[]{:S(2)}) %collective-permute-start.9) | collective-permute-done | bytes 524320 | tf_op jit(solution)/shard_map/ppermute | solution.py:26
  154.2 14.0 %fusion.118 = (bf16[1,2048,2,1024]{3,2,1,0:T(2,128)(2,1)}, bf16[1,2048,2,1024]{3,2,1,0:T(2,128)(2,1)S(1)}) fusion(bf16[2,2048,2,1024]{3,2,1,0:T(2,128)(2,1)} %param.26), kind=kLoop, calls=%fused_computation.256 | loop fusion | bytes 33554432 | tf_op jit(solution)/shard_map/slice | solution.py:111
  168.2 3.3 collective-permute-start.11
  171.5 3.8 collective-permute-done.11
  175.4 6.1 %fusion.3 = f32[512,2,1024]{2,0,1:T(8,128)S(1)} fusion(bf16[1,2048,2,1024]{3,2,1,0:T(2,128)(2,1)S(1)} %get-tuple-element.24, s32[]{:T(128)S(6)} %select_n.167, bf16[512,2048]{1,0:T(8,128)(2,1)S(1)} %constant_dynamic-update-slice_fusion.5), kind=kOutput, calls=%fused_computation.9 | convolution fusion | flops 4299161600 | bytes 14680068 | tf_op jit(solution)/shard_map/rd,dtf->rtf/dot_general | solution.py:202
  181.5 4.6 %fusion.12 = f32[512,2048]{1,0:T(8,128)S(1)} fusion(bf16[2,1024,2048]{2,1,0:T(8,128)(2,1)} %param.27, f32[512,2,1024]{2,0,1:T(8,128)S(1)} %fusion.3), kind=kOutput, calls=%fused_computation.30 | convolution fusion | flops 2150629376 | bytes 12582912 | tf_op jit(solution)/shard_map/dot_general | solution.py:209
  190.2 4.9 %collective-permute-done.12 = bf16[64,2048]{1,0:T(8,128)(2,1)S(1)} collective-permute-done((bf16[64,2048]{1,0:T(8,128)(2,1)S(1)}, bf16[64,2048]{1,0:T(8,128)(2,1)S(1)}, u32[]{:S(2)}, u32[]{:S(2)}) %collective-permute-start.12) | collective-permute-done | bytes 262176 | tf_op jit(solution)/shard_map/ppermute | solution.py:46
  199.0 6.9 %collective-permute-done.13 = bf16[128,2048]{1,0:T(8,128)(2,1)S(1)} collective-permute-done((bf16[128,2048]{1,0:T(8,128)(2,1)S(1)}, bf16[128,2048]{1,0:T(8,128)(2,1)S(1)}, u32[]{:S(2)}, u32[]{:S(2)}) %collective-permute-start.13) | collective-permute-done | bytes 524320 | tf_op jit(solution)/shard_map/ppermute | solution.py:52
  212.0 10.0 %collective-permute-done.17 = bf16[128,2048]{1,0:T(8,128)(2,1)S(1)} collective-permute-done((bf16[128,2048]{1,0:T(8,128)(2,1)}, bf16[128,2048]{1,0:T(8,128)(2,1)S(1)}, u32[]{:S(2)}, u32[]{:S(2)}) %collective-permute-start.17) | collective-permute-done | bytes 524320 | tf_op jit(solution)/shard_map/ppermute | solution.py:26
  240.8 4.0 %copy.143 = bf16[512,2048]{1,0:T(8,128)(2,1)} copy(bf16[512,2048]{0,1:T(8,128)(2,1)} %get-tuple-element.33) | data formatting | bytes 4194304 | tf_op jit(solution)/shard_map/dot_general | solution.py:117
  245.6 3.7 fusion.32
  253.2 4.6 %divide_convert_fusion = bf16[2,4,512,640]{2,3,1,0:T(8,128)(2,1)} fusion(f32[2,4,512,512]{2,3,1,0:T(8,128)S(1)} %get-tuple-element.94, f32[2,4,512,128]{2,3,1,0:T(8,128)} %copy-done, f32[2,4,512]{2,1,0:T(4,128)S(1)} %fusion.4, f32[2,4,512]{2,1,0:T(4,128)S(1)} %reduce_max.65), kind=kLoop, calls=%fused_computation.4 | loop fusion | flops 10485760 | bytes 15761408 | tf_op jit(solution)/shard_map/convert_element_type | solution.py:189
  257.8 3.1 fusion.47
  260.9 25.7 %all-gather.9.cloned.1.call-done = bf16[32,131,512]{2,1,0:T(8,128)(2,1)} async-done(((bf16[1,131,512]{2,1,0:T(8,128)(2,1)}), bf16[32,131,512]{2,1,0:T(8,128)(2,1)}) %all-gather.9.cloned.1.call-update) | async-done | bytes 4292624 | tf_op jit(solution)/shard_map/all_gather | solution.py:153
  289.0 3.1 multiply_reduce_fusion
  301.1 6.4 %collective-permute-done.20 = bf16[64,2048]{1,0:T(8,128)(2,1)S(1)} collective-permute-done((bf16[64,2048]{1,0:T(8,128)(2,1)S(1)}, bf16[64,2048]{1,0:T(8,128)(2,1)S(1)}, u32[]{:S(2)}, u32[]{:S(2)}) %collective-permute-start.20) | collective-permute-done | bytes 262176 | tf_op jit(solution)/shard_map/ppermute | solution.py:46
  311.4 10.8 %collective-permute-done.21 = bf16[128,2048]{1,0:T(8,128)(2,1)S(1)} collective-permute-done((bf16[128,2048]{1,0:T(8,128)(2,1)S(1)}, bf16[128,2048]{1,0:T(8,128)(2,1)S(1)}, u32[]{:S(2)}, u32[]{:S(2)}) %collective-permute-start.21) | collective-permute-done | bytes 524320 | tf_op jit(solution)/shard_map/ppermute | solution.py:52
  326.2 10.1 %collective-permute-done.25 = bf16[128,2048]{1,0:T(8,128)(2,1)S(1)} collective-permute-done((bf16[128,2048]{1,0:T(8,128)(2,1)S(1)}, bf16[128,2048]{1,0:T(8,128)(2,1)S(1)}, u32[]{:S(2)}, u32[]{:S(2)}) %collective-permute-start.25) | collective-permute-done | bytes 524320 | tf_op jit(solution)/shard_map/ppermute | solution.py:26
  336.5 3.3 collective-permute-start.27
  339.8 4.2 %collective-permute-done.26 = bf16[64,2048]{1,0:T(8,128)(2,1)S(1)} collective-permute-done((bf16[64,2048]{1,0:T(8,128)(2,1)S(1)}, bf16[64,2048]{1,0:T(8,128)(2,1)S(1)}, u32[]{:S(2)}, u32[]{:S(2)}) %collective-permute-start.26) | collective-permute-done | bytes 262176 | tf_op jit(solution)/shard_map/ppermute | solution.py:28
  344.2 6.1 %fusion.2 = f32[512,2,1024]{2,0,1:T(8,128)S(1)} fusion(bf16[1,2048,2,1024]{3,2,1,0:T(2,128)(2,1)S(1)} %bitcast.257, s32[]{:T(128)S(6)} %select_n.167, bf16[512,2048]{1,0:T(8,128)(2,1)S(1)} %constant_dynamic-update-slice_fusion.15), kind=kOutput, calls=%fused_computation.7 | convolution fusion | flops 4299161600 | bytes 14680068 | tf_op jit(solution)/shard_map/rd,dtf->rtf/dot_general | solution.py:202
  372.3 3.1 collective-permute-done.29
  (287 shorter events, 144.8 us)
Async XLA Ops:
  7.2 91.9 %all-gather.7.cloned.1.call-start = ((), (), s32[]{:S(2)}) async-start(), calls=%async_computation | async-start | bytes 4595712 | tf_op jit(solution)/shard_map/all_gather | solution.py:153
  12.5 21.5 %collective-permute-start = (bf16[128,2048]{1,0:T(8,128)(2,1)}, bf16[128,2048]{1,0:T(8,128)(2,1)}, u32[]{:S(2)}, u32[]{:S(2)}) collective-permute-start(bf16[128,2048]{1,0:T(8,128)(2,1)} %get-tuple-element.22), channel_id=1, source_target_pairs={{0,3},{1,0},{2,1},{3,2},{4,7},{5,4},{6,5},{7,6},{8,11},{9,8},{10,9... | collective-permute-start | bytes 1572872 | tf_op jit(solution)/shard_map/ppermute | solution.py:27
  16.6 14.9 %collective-permute-start.1 = (bf16[128,2048]{1,0:T(8,128)(2,1)}, bf16[128,2048]{1,0:T(8,128)(2,1)}, u32[]{:S(2)}, u32[]{:S(2)}) collective-permute-start(bf16[128,2048]{1,0:T(8,128)(2,1)} %get-tuple-element.22), channel_id=1, source_target_pairs={{0,1},{1,2},{2,3},{3,0},{4,5},{5,6},{6,7},{7,4},{8,9},{9,10},{10,1... | collective-permute-start | bytes 1572872 | tf_op jit(solution)/shard_map/ppermute | solution.py:26
  32.5 8.2 %collective-permute-start.2 = (bf16[64,2048]{1,0:T(8,128)(2,1)S(1)}, bf16[64,2048]{1,0:T(8,128)(2,1)S(1)}, u32[]{:S(2)}, u32[]{:S(2)}) collective-permute-start(bf16[64,2048]{1,0:T(8,128)(2,1)S(1)} %slice.346), channel_id=1, source_target_pairs={{0,1},{1,2},{2,3},{3,0},{4,5},{5,6},{6,7},{7,4},{8,9},{9,10},{10,1... | collective-permute-start | bytes 786440 | tf_op jit(solution)/shard_map/ppermute | solution.py:28
  34.9 7.4 %collective-permute-start.3 = (bf16[64,2048]{1,0:T(8,128)(2,1)S(1)}, bf16[64,2048]{1,0:T(8,128)(2,1)S(1)}, u32[]{:S(2)}, u32[]{:S(2)}) collective-permute-start(bf16[64,2048]{1,0:T(8,128)(2,1)S(1)} %slice.347), channel_id=1, source_target_pairs={{0,3},{1,0},{2,1},{3,2},{4,7},{5,4},{6,5},{7,6},{8,11},{9,8},{10,9... | collective-permute-start | bytes 786440 | tf_op jit(solution)/shard_map/ppermute | solution.py:29
  50.8 235.9 %all-gather.9.cloned.1.call-start = ((), (), s32[]{:S(2)}) async-start(), calls=%async_computation.1 | async-start | bytes 4595712 | tf_op jit(solution)/shard_map/all_gather | solution.py:153
  111.3 9.7 %collective-permute-start.4 = (bf16[64,2048]{1,0:T(8,128)(2,1)S(1)}, bf16[64,2048]{1,0:T(8,128)(2,1)S(1)}, u32[]{:S(2)}, u32[]{:S(2)}) collective-permute-start(bf16[64,2048]{1,0:T(8,128)(2,1)S(1)} %get-tuple-element.59), channel_id=1, source_target_pairs={{0,1},{1,2},{2,3},{3,0},{4,5},{5,6},{6,7},{7,4},{8,9},{9,10},{10,1... | collective-permute-start | bytes 786440 | tf_op jit(solution)/shard_map/ppermute | solution.py:46
  112.9 8.2 %collective-permute-start.6 = (bf16[64,2048]{1,0:T(8,128)(2,1)S(1)}, bf16[64,2048]{1,0:T(8,128)(2,1)S(1)}, u32[]{:S(2)}, u32[]{:S(2)}) collective-permute-start(bf16[64,2048]{1,0:T(8,128)(2,1)S(1)} %get-tuple-element.60), channel_id=1, source_target_pairs={{0,3},{1,0},{2,1},{3,2},{4,7},{5,4},{6,5},{7,6},{8,11},{9,8},{10,9... | collective-permute-start | bytes 786440 | tf_op jit(solution)/shard_map/ppermute | solution.py:47
  123.2 14.9 %collective-permute-start.5 = (bf16[128,2048]{1,0:T(8,128)(2,1)}, bf16[128,2048]{1,0:T(8,128)(2,1)S(1)}, u32[]{:S(2)}, u32[]{:S(2)}) collective-permute-start(bf16[128,2048]{1,0:T(8,128)(2,1)} %pad_maximum_fusion.1), channel_id=1, source_target_pairs={{0,1},{1,2},{2,3},{3,0},{4,5},{5,6},{6,7},{7,4},{8,9},{9,10},{10,1... | collective-permute-start | bytes 1572872 | tf_op jit(solution)/shard_map/ppermute | solution.py:52
  126.0 12.9 %collective-permute-start.7 = (bf16[128,2048]{1,0:T(8,128)(2,1)}, bf16[128,2048]{1,0:T(8,128)(2,1)S(1)}, u32[]{:S(2)}, u32[]{:S(2)}) collective-permute-start(bf16[128,2048]{1,0:T(8,128)(2,1)} %pad_maximum_fusion.2), channel_id=1, source_target_pairs={{0,3},{1,0},{2,1},{3,2},{4,7},{5,4},{6,5},{7,6},{8,11},{9,8},{10,9... | collective-permute-start | bytes 1572872 | tf_op jit(solution)/shard_map/ppermute | solution.py:53
  140.6 13.4 %collective-permute-start.9 = (bf16[128,2048]{1,0:T(8,128)(2,1)S(1)}, bf16[128,2048]{1,0:T(8,128)(2,1)S(1)}, u32[]{:S(2)}, u32[]{:S(2)}) collective-permute-start(bf16[128,2048]{1,0:T(8,128)(2,1)S(1)} %get-tuple-element.18), channel_id=1, source_target_pairs={{0,1},{1,2},{2,3},{3,0},{4,5},{5,6},{6,7},{7,4},{8,9},{9,10},{10,1... | collective-permute-start | bytes 1572872 | tf_op jit(solution)/shard_map/ppermute | solution.py:26
  142.0 26.2 %collective-permute-start.8 = (bf16[128,2048]{1,0:T(8,128)(2,1)S(1)}, bf16[128,2048]{1,0:T(8,128)(2,1)S(1)}, u32[]{:S(2)}, u32[]{:S(2)}) collective-permute-start(bf16[128,2048]{1,0:T(8,128)(2,1)S(1)} %get-tuple-element.18), channel_id=1, source_target_pairs={{0,3},{1,0},{2,1},{3,2},{4,7},{5,4},{6,5},{7,6},{8,11},{9,8},{10,9... | collective-permute-start | bytes 1572872 | tf_op jit(solution)/shard_map/ppermute | solution.py:27
  154.1 17.4 %collective-permute-start.10 = (bf16[64,2048]{1,0:T(8,128)(2,1)S(1)}, bf16[64,2048]{1,0:T(8,128)(2,1)S(1)}, u32[]{:S(2)}, u32[]{:S(2)}) collective-permute-start(bf16[64,2048]{1,0:T(8,128)(2,1)S(1)} %slice.362), channel_id=1, source_target_pairs={{0,1},{1,2},{2,3},{3,0},{4,5},{5,6},{6,7},{7,4},{8,9},{9,10},{10,1... | collective-permute-start | bytes 786440 | tf_op jit(solution)/shard_map/ppermute | solution.py:28
  186.2 8.8 %collective-permute-start.12 = (bf16[64,2048]{1,0:T(8,128)(2,1)S(1)}, bf16[64,2048]{1,0:T(8,128)(2,1)S(1)}, u32[]{:S(2)}, u32[]{:S(2)}) collective-permute-start(bf16[64,2048]{1,0:T(8,128)(2,1)S(1)} %get-tuple-element.57), channel_id=1, source_target_pairs={{0,1},{1,2},{2,3},{3,0},{4,5},{5,6},{6,7},{7,4},{8,9},{9,10},{10,1... | collective-permute-start | bytes 786440 | tf_op jit(solution)/shard_map/ppermute | solution.py:46
  187.1 8.0 %collective-permute-start.14 = (bf16[64,2048]{1,0:T(8,128)(2,1)S(1)}, bf16[64,2048]{1,0:T(8,128)(2,1)S(1)}, u32[]{:S(2)}, u32[]{:S(2)}) collective-permute-start(bf16[64,2048]{1,0:T(8,128)(2,1)S(1)} %get-tuple-element.58), channel_id=1, source_target_pairs={{0,3},{1,0},{2,1},{3,2},{4,7},{5,4},{6,5},{7,6},{8,11},{9,8},{10,9... | collective-permute-start | bytes 786440 | tf_op jit(solution)/shard_map/ppermute | solution.py:47
  195.2 10.6 %collective-permute-start.13 = (bf16[128,2048]{1,0:T(8,128)(2,1)S(1)}, bf16[128,2048]{1,0:T(8,128)(2,1)S(1)}, u32[]{:S(2)}, u32[]{:S(2)}) collective-permute-start(bf16[128,2048]{1,0:T(8,128)(2,1)S(1)} %pad_maximum_fusion.3), channel_id=1, source_target_pairs={{0,1},{1,2},{2,3},{3,0},{4,5},{5,6},{6,7},{7,4},{8,9},{9,10},{10,1... | collective-permute-start | bytes 1572872 | tf_op jit(solution)/shard_map/ppermute | solution.py:52
  196.3 10.7 %collective-permute-start.15 = (bf16[128,2048]{1,0:T(8,128)(2,1)S(1)}, bf16[128,2048]{1,0:T(8,128)(2,1)S(1)}, u32[]{:S(2)}, u32[]{:S(2)}) collective-permute-start(bf16[128,2048]{1,0:T(8,128)(2,1)S(1)} %pad_maximum_fusion.4), channel_id=1, source_target_pairs={{0,3},{1,0},{2,1},{3,2},{4,7},{5,4},{6,5},{7,6},{8,11},{9,8},{10,9... | collective-permute-start | bytes 1572872 | tf_op jit(solution)/shard_map/ppermute | solution.py:53
  208.6 13.4 %collective-permute-start.17 = (bf16[128,2048]{1,0:T(8,128)(2,1)}, bf16[128,2048]{1,0:T(8,128)(2,1)S(1)}, u32[]{:S(2)}, u32[]{:S(2)}) collective-permute-start(bf16[128,2048]{1,0:T(8,128)(2,1)} %get-tuple-element.14), channel_id=1, source_target_pairs={{0,1},{1,2},{2,3},{3,0},{4,5},{5,6},{6,7},{7,4},{8,9},{9,10},{10,1... | collective-permute-start | bytes 1572872 | tf_op jit(solution)/shard_map/ppermute | solution.py:26
  210.9 15.0 %collective-permute-start.16 = (bf16[128,2048]{1,0:T(8,128)(2,1)}, bf16[128,2048]{1,0:T(8,128)(2,1)}, u32[]{:S(2)}, u32[]{:S(2)}) collective-permute-start(bf16[128,2048]{1,0:T(8,128)(2,1)} %get-tuple-element.14), channel_id=1, source_target_pairs={{0,3},{1,0},{2,1},{3,2},{4,7},{5,4},{6,5},{7,6},{8,11},{9,8},{10,9... | collective-permute-start | bytes 1572872 | tf_op jit(solution)/shard_map/ppermute | solution.py:27
  222.7 8.4 %collective-permute-start.18 = (bf16[64,2048]{1,0:T(8,128)(2,1)}, bf16[64,2048]{1,0:T(8,128)(2,1)}, u32[]{:S(2)}, u32[]{:S(2)}) collective-permute-start(bf16[64,2048]{1,0:T(8,128)(2,1)} %slice.368), channel_id=1, source_target_pairs={{0,1},{1,2},{2,3},{3,0},{4,5},{5,6},{6,7},{7,4},{8,9},{9,10},{10,1... | collective-permute-start | bytes 786440 | tf_op jit(solution)/shard_map/ppermute | solution.py:28
  297.7 9.7 %collective-permute-start.20 = (bf16[64,2048]{1,0:T(8,128)(2,1)S(1)}, bf16[64,2048]{1,0:T(8,128)(2,1)S(1)}, u32[]{:S(2)}, u32[]{:S(2)}) collective-permute-start(bf16[64,2048]{1,0:T(8,128)(2,1)S(1)} %get-tuple-element.53), channel_id=1, source_target_pairs={{0,1},{1,2},{2,3},{3,0},{4,5},{5,6},{6,7},{7,4},{8,9},{9,10},{10,1... | collective-permute-start | bytes 786440 | tf_op jit(solution)/shard_map/ppermute | solution.py:46
  299.4 8.2 %collective-permute-start.22 = (bf16[64,2048]{1,0:T(8,128)(2,1)S(1)}, bf16[64,2048]{1,0:T(8,128)(2,1)S(1)}, u32[]{:S(2)}, u32[]{:S(2)}) collective-permute-start(bf16[64,2048]{1,0:T(8,128)(2,1)S(1)} %get-tuple-element.54), channel_id=1, source_target_pairs={{0,3},{1,0},{2,1},{3,2},{4,7},{5,4},{6,5},{7,6},{8,11},{9,8},{10,9... | collective-permute-start | bytes 786440 | tf_op jit(solution)/shard_map/ppermute | solution.py:47
  307.7 14.4 %collective-permute-start.21 = (bf16[128,2048]{1,0:T(8,128)(2,1)S(1)}, bf16[128,2048]{1,0:T(8,128)(2,1)S(1)}, u32[]{:S(2)}, u32[]{:S(2)}) collective-permute-start(bf16[128,2048]{1,0:T(8,128)(2,1)S(1)} %pad_maximum_fusion.6), channel_id=1, source_target_pairs={{0,1},{1,2},{2,3},{3,0},{4,5},{5,6},{6,7},{7,4},{8,9},{9,10},{10,1... | collective-permute-start | bytes 1572872 | tf_op jit(solution)/shard_map/ppermute | solution.py:52
  309.4 12.9 %collective-permute-start.23 = (bf16[128,2048]{1,0:T(8,128)(2,1)S(1)}, bf16[128,2048]{1,0:T(8,128)(2,1)S(1)}, u32[]{:S(2)}, u32[]{:S(2)}) collective-permute-start(bf16[128,2048]{1,0:T(8,128)(2,1)S(1)} %pad_maximum_fusion.7), channel_id=1, source_target_pairs={{0,3},{1,0},{2,1},{3,2},{4,7},{5,4},{6,5},{7,6},{8,11},{9,8},{10,9... | collective-permute-start | bytes 1572872 | tf_op jit(solution)/shard_map/ppermute | solution.py:53
  322.9 13.4 %collective-permute-start.25 = (bf16[128,2048]{1,0:T(8,128)(2,1)S(1)}, bf16[128,2048]{1,0:T(8,128)(2,1)S(1)}, u32[]{:S(2)}, u32[]{:S(2)}) collective-permute-start(bf16[128,2048]{1,0:T(8,128)(2,1)S(1)} %get-tuple-element.8), channel_id=1, source_target_pairs={{0,1},{1,2},{2,3},{3,0},{4,5},{5,6},{6,7},{7,4},{8,9},{9,10},{10,1... | collective-permute-start | bytes 1572872 | tf_op jit(solution)/shard_map/ppermute | solution.py:26
  324.2 12.2 %collective-permute-start.24 = (bf16[128,2048]{1,0:T(8,128)(2,1)S(1)}, bf16[128,2048]{1,0:T(8,128)(2,1)S(1)}, u32[]{:S(2)}, u32[]{:S(2)}) collective-permute-start(bf16[128,2048]{1,0:T(8,128)(2,1)S(1)} %get-tuple-element.8), channel_id=1, source_target_pairs={{0,3},{1,0},{2,1},{3,2},{4,7},{5,4},{6,5},{7,6},{8,11},{9,8},{10,9... | collective-permute-start | bytes 1572872 | tf_op jit(solution)/shard_map/ppermute | solution.py:27
  336.4 7.7 %collective-permute-start.26 = (bf16[64,2048]{1,0:T(8,128)(2,1)S(1)}, bf16[64,2048]{1,0:T(8,128)(2,1)S(1)}, u32[]{:S(2)}, u32[]{:S(2)}) collective-permute-start(bf16[64,2048]{1,0:T(8,128)(2,1)S(1)} %slice.384), channel_id=1, source_target_pairs={{0,1},{1,2},{2,3},{3,0},{4,5},{5,6},{6,7},{7,4},{8,9},{9,10},{10,1... | collective-permute-start | bytes 786440 | tf_op jit(solution)/shard_map/ppermute | solution.py:28
  336.5 7.6 %collective-permute-start.27 = (bf16[64,2048]{1,0:T(8,128)(2,1)S(1)}, bf16[64,2048]{1,0:T(8,128)(2,1)S(1)}, u32[]{:S(2)}, u32[]{:S(2)}) collective-permute-start(bf16[64,2048]{1,0:T(8,128)(2,1)S(1)} %slice.385), channel_id=1, source_target_pairs={{0,3},{1,0},{2,1},{3,2},{4,7},{5,4},{6,5},{7,6},{8,11},{9,8},{10,9... | collective-permute-start | bytes 786440 | tf_op jit(solution)/shard_map/ppermute | solution.py:29
  354.8 7.7 %collective-permute-start.28 = (bf16[64,2048]{1,0:T(8,128)(2,1)S(1)}, bf16[64,2048]{1,0:T(8,128)(2,1)S(1)}, u32[]{:S(2)}, u32[]{:S(2)}) collective-permute-start(bf16[64,2048]{1,0:T(8,128)(2,1)S(1)} %get-tuple-element.51), channel_id=1, source_target_pairs={{0,1},{1,2},{2,3},{3,0},{4,5},{5,6},{6,7},{7,4},{8,9},{9,10},{10,1... | collective-permute-start | bytes 786440 | tf_op jit(solution)/shard_map/ppermute | solution.py:46
  355.2 7.3 %collective-permute-start.30 = (bf16[64,2048]{1,0:T(8,128)(2,1)S(1)}, bf16[64,2048]{1,0:T(8,128)(2,1)S(1)}, u32[]{:S(2)}, u32[]{:S(2)}) collective-permute-start(bf16[64,2048]{1,0:T(8,128)(2,1)S(1)} %get-tuple-element.52), channel_id=1, source_target_pairs={{0,3},{1,0},{2,1},{3,2},{4,7},{5,4},{6,5},{7,6},{8,11},{9,8},{10,9... | collective-permute-start | bytes 786440 | tf_op jit(solution)/shard_map/ppermute | solution.py:47
  364.7 10.8 %collective-permute-start.29 = (bf16[128,2048]{1,0:T(8,128)(2,1)}, bf16[128,2048]{1,0:T(8,128)(2,1)}, u32[]{:S(2)}, u32[]{:S(2)}) collective-permute-start(bf16[128,2048]{1,0:T(8,128)(2,1)} %pad_maximum_fusion.8), channel_id=1, source_target_pairs={{0,1},{1,2},{2,3},{3,0},{4,5},{5,6},{6,7},{7,4},{8,9},{9,10},{10,1... | collective-permute-start | bytes 1572872 | tf_op jit(solution)/shard_map/ppermute | solution.py:52
  367.0 9.5 %collective-permute-start.31 = (bf16[128,2048]{1,0:T(8,128)(2,1)}, bf16[128,2048]{1,0:T(8,128)(2,1)}, u32[]{:S(2)}, u32[]{:S(2)}) collective-permute-start(bf16[128,2048]{1,0:T(8,128)(2,1)} %pad_maximum_fusion.9), channel_id=1, source_target_pairs={{0,3},{1,0},{2,1},{3,2},{4,7},{5,4},{6,5},{7,6},{8,11},{9,8},{10,9... | collective-permute-start | bytes 1572872 | tf_op jit(solution)/shard_map/ppermute | solution.py:53
  (42 other events, 458.9 us)
Sparse Core Ops, SparseCore 0:
  50.9 48.1 all-gather.6
  240.9 45.7 all-gather.8

commit v4 on v3

--- a/solution.py
+++ b/solution.py
@@ -1,7 +1,7 @@
 import jax
 import jax.numpy as jnp
 from jax import lax
-from jax.sharding import PartitionSpec as P
+from jax.sharding import Mesh, PartitionSpec as P
 
 HEADS = 32
 KV_HEADS = 8
@@ -10,6 +10,21 @@
 SEG_LEN = 512
 BLOCK = 128
 DEPTH_NUMBER = 2
+
+
+ROW_AXES = ("sx", "sc")
+COLUMN_AXIS = "sy"
+SEG_AXES = ("sy", "sx", "sc")
+
+
+def prefix_weights(rate_all, upto):
+    count = rate_all.shape[0]
+    order = jnp.arange(count)
+    inside = (order[None, :] > order[:, None]) & (order[None, :] < upto)
+    span = jnp.prod(jnp.where(inside[:, :, None], rate_all[None, :, :], 1.0), axis=1)
+    weight = jnp.where((order < upto)[:, None], span * (1.0 - rate_all), 0.0)
+    carry = jnp.prod(jnp.where((order < upto)[:, None], rate_all, 1.0), axis=0)
+    return jnp.repeat(weight, HD, axis=1), jnp.repeat(carry, HD)
 
 
 def ring_pairs(count, step):
@@ -140,8 +155,8 @@
             "skgmj,sjkd->smkgd", write_probs, values, preferred_element_type=jnp.float32
         ).reshape(seg_local, MEM, cols_query)
         rates = jnp.repeat(retain[layer], HD, axis=1)[:, None, :]
-        here = lax.axis_index("seg")
-        count = lax.axis_size("seg")
+        here = lax.axis_index(ROW_AXES)
+        row = lax.axis_index(COLUMN_AXIS)
         rate_row = rates[0]
         rate_high = rate_row.astype(jnp.bfloat16)
         rest = rate_row - rate_high.astype(jnp.float32)
@@ -150,20 +165,27 @@
         payload = jnp.concatenate(
             [written[0].astype(jnp.bfloat16), rate_high, rate_mid, rate_low], axis=0
         )
-        gathered = lax.all_gather(payload, "seg")
+        gathered = lax.all_gather(payload, ROW_AXES)
         written_all = gathered[:, :MEM].astype(jnp.float32)
         rate_parts = gathered[:, MEM:, ::HD].astype(jnp.float32)
         rate_all = rate_parts[:, 0] + rate_parts[:, 1] + rate_parts[:, 2]
-        order = jnp.arange(count)
-        inside = (order[None, :] > order[:, None]) & (order[None, :] < here)
-        span = jnp.prod(jnp.where(inside[:, :, None], rate_all[None, :, :], 1.0), axis=1)
-        weight = jnp.where((order < here)[:, None], span * (1.0 - rate_all), 0.0)
-        carry = jnp.prod(jnp.where((order < here)[:, None], rate_all, 1.0), axis=0)
-        weight = jnp.repeat(weight, HD, axis=1)
-        carry = jnp.repeat(carry, HD)
-        state = carry[None, :] * mem_init[layer] + jnp.sum(
-            weight[:, None, :] * written_all, axis=0
-        )
+        weight, carry = prefix_weights(rate_all, here)
+        local = jnp.sum(weight[:, None, :] * written_all, axis=0)
+        weight_total, carry_total = prefix_weights(rate_all, rate_all.shape[0])
+        total = jnp.sum(weight_total[:, None, :] * written_all, axis=0)
+        summary = jnp.concatenate([total, carry_total[None, :]], axis=0)
+        row_sums = lax.all_gather(summary, COLUMN_AXIS)
+        totals = row_sums[:, :MEM]
+        keeps = row_sums[:, MEM, ::HD]
+        order = jnp.arange(keeps.shape[0])
+        inside = (order[None, :] > order[:, None]) & (order[None, :] < row)
+        span = jnp.prod(jnp.where(inside[:, :, None], keeps[None, :, :], 1.0), axis=1)
+        row_weight = jnp.repeat(jnp.where((order < row)[:, None], span, 0.0), HD, axis=1)
+        row_carry = jnp.repeat(jnp.prod(jnp.where((order < row)[:, None], keeps, 1.0), axis=0), HD)
+        entering = row_carry[None, :] * mem_init[layer] + jnp.sum(
+            row_weight[:, None, :] * totals, axis=0
+        )
+        state = carry[None, :] * entering + local
         segment = 0
         memory_read = state.astype(jnp.bfloat16).reshape(MEM, local_kv, group, HD)
         state = rates[segment] * state + (1.0 - rates[segment]) * written[segment]
@@ -212,16 +234,21 @@
 
 
 def solution(mesh):
+    seg_size = mesh.shape["seg"]
+    head_size = mesh.shape["head"]
+    fine = Mesh(
+        mesh.devices.reshape(seg_size // 8, 4, 2, head_size), SEG_AXES + ("head",)
+    )
     return jax.shard_map(
         body,
-        mesh=mesh,
+        mesh=fine,
         in_specs=(
-            P(("seg", "head"), None),
-            P("seg"),
-            P("seg", None, None),
-            P(None, None, "head"),
-            P(None, None, "head"),
-            P(None, "seg", "head"),
+            P(SEG_AXES + ("head",), None),
+            P(SEG_AXES),
+            P(SEG_AXES, None, None),
+            P(None, None, "head"),
+            P(None, None, "head"),
+            P(None, SEG_AXES, "head"),
             P(),
             P(),
             P(None, None, "head"),
@@ -230,6 +257,6 @@
             P(None, None, None, "head"),
             P(None, "head", None),
         ),
-        out_specs=(P(("seg", "head"), None), P(None, "seg", None, "head")),
+        out_specs=(P(SEG_AXES + ("head",), None), P(None, SEG_AXES, None, "head")),
         check_vma=False,
     )

time: 392 us -> 414 us (1.056)
  local copies, waits for them, and re-layouts: 62.9 us -> 85 us
  other arithmetic: 41.7 us -> 47.6 us
  matrix products: 54.7 us -> 49 us
    unnamed x95 -> x130, local copies, waits for them, and re-layouts: 12.3 us -> 23.8 us
    all_gather x2 -> x4, waiting for transfers between devices: 51.1 us -> 62.2 us  [the longest x2 33.4 us: body(): row_sums = lax.all_gather(summary, COLUMN_AXIS)]
    ppermute x4, waiting for transfers between devices: 41.4 us -> 30.4 us  [ring_gather(): from_before = lax.ppermute(piece, axis, ahead)]
    dot_general x2, matrix products: 6.15 us -> 1.69 us  [body(): jnp.einsum('kgij,jkd->ikgd', probs[..., MEM:], values[segment], preferred...]
  transfers between devices with their start and end apart: 34 -> 36, of which waited for: 25 -> 27; matrix products, arithmetic and copies ran while one was open for 21% -> 22% of each run, Pallas kernels for 0% -> 0%
where the time goes in v4:
time: 414 us; the launch traced here: 407 us
  waiting for transfers between devices  155 us (37%)
  local copies, waits for them, and re-layouts  85 us (21%)
  starting transfers between devices  55.4 us (13%)
  matrix products  49 us (12%)
  other arithmetic  47.6 us (11%)
  between operations  15.2 us (4%)
    all_gather x2, waiting for transfers between devices, body(): row_sums = lax.all_gather(summary, COLUMN_AXIS)  33.4 us
    ppermute x4, waiting for transfers between devices, ring_gather(): from_before = lax.ppermute(piece, axis, ahead)  30.4 us
    ppermute x4, waiting for transfers between devices, ring_scatter(): got_before = lax.ppermute(next_part.astype(jnp.bfloat16), axis, ahead)  29.1 us
    all_gather x2, waiting for transfers between devices, body(): gathered = lax.all_gather(payload, ROW_AXES)  28.8 us
    unnamed x130, local copies, waits for them, and re-layouts  23.8 us
    ppermute x4, waiting for transfers between devices, ring_scatter(): sent_top = lax.ppermute(far[:half].astype(jnp.bfloat16), axis, ahead)  19 us
    slice x1, local copies, waits for them, and re-layouts, body(): widening_matrix = w_gate_up[layer]  14 us
    dot_general x2, matrix products, body(): jnp.einsum('rd,dtf->rtf', ring_gather(rms_norm(middle, mlp_gain[layer]),...  12.2 us
  transfers between devices with their start and end apart: 36, of which 27 were waited for; matrix products, arithmetic and copies ran while one was open for 22% of the time, Pallas kernels for 0%

profile of v4, /device:TPU:0, one launch (start us, length us, event | category | flops | bytes accessed | tf_op | source)
XLA Modules:
  0.0 407.5 jit_solution(12734407925242642454)
XLA Ops:
  11.9 4.1 %collective-permute-start = (bf16[128,2048]{1,0:T(8,128)(2,1)}, bf16[128,2048]{1,0:T(8,128)(2,1)}, u32[]{:S(2)}, u32[]{:S(2)}) collective-permute-start(bf16[128,2048]{1,0:T(8,128)(2,1)} %get-tuple-element.32), channel_id=1, source_target_pairs={{0,3},{1,0},{2,1},{3,2},{4,7},{5,4},{6,5},{7,6},{8,11},{9,8},{10,9... | collective-permute-start | bytes 1572872 | tf_op jit(solution)/shard_map/ppermute | solution.py:42
  19.2 3.8 slice_bitcast_fusion
  26.4 4.5 %collective-permute-done.1 = bf16[128,2048]{1,0:T(8,128)(2,1)} collective-permute-done((bf16[128,2048]{1,0:T(8,128)(2,1)}, bf16[128,2048]{1,0:T(8,128)(2,1)}, u32[]{:S(2)}, u32[]{:S(2)}) %collective-permute-start.1) | collective-permute-done | bytes 524320 | tf_op jit(solution)/shard_map/ppermute | solution.py:41
  40.3 3.3 collective-permute-start.3
  57.0 3.0 fusion.41
  62.4 3.3 copy-done.1
  67.2 15.0 %all-gather.13.cloned.1.call-done = bf16[8,131,512]{2,1,0:T(8,128)(2,1)} async-done(((bf16[1,131,512]{2,1,0:T(8,128)(2,1)}), bf16[8,131,512]{2,1,0:T(8,128)(2,1)}) %all-gather.13.cloned.1.call-update) | async-done | bytes 1073168 | tf_op jit(solution)/shard_map/all_gather | solution.py:168
  86.4 5.1 %divide_convert_fusion.1 = bf16[2,4,512,640]{2,3,1,0:T(8,128)(2,1)S(1)} fusion(f32[2,4,512,512]{2,3,1,0:T(8,128)} %copy-done.1, f32[2,4,512,128]{2,3,1,0:T(8,128)S(1)} %get-tuple-element.100, f32[2,4,512]{2,1,0:T(4,128)S(1)} %fusion.5, f32[2,4,512]{2,1,0:T(4,128)S(1)} %reduce_max.61), kind=kLoop, calls=%fused_computation.5 | loop fusion | flops 10485760 | bytes 15761408 | tf_op jit(solution)/shard_map/convert_element_type | solution.py:211
  94.1 16.7 %all-gather.15.cloned.1.call-done = f32[4,129,512]{2,1,0:T(8,128)} async-done(((f32[1,129,512]{2,1,0:T(8,128)}), f32[4,129,512]{2,1,0:T(8,128)}) %all-gather.15.cloned.1.call-update) | async-done | bytes 1056784 | tf_op jit(solution)/shard_map/all_gather | solution.py:177
  124.9 3.1 collective-permute-done.4
  134.4 6.6 %collective-permute-done.5 = bf16[128,2048]{1,0:T(8,128)(2,1)S(1)} collective-permute-done((bf16[128,2048]{1,0:T(8,128)(2,1)S(1)}, bf16[128,2048]{1,0:T(8,128)(2,1)S(1)}, u32[]{:S(2)}, u32[]{:S(2)}) %collective-permute-start.5) | collective-permute-done | bytes 524320 | tf_op jit(solution)/shard_map/ppermute | solution.py:67
  147.5 8.4 %collective-permute-done.9 = bf16[128,2048]{1,0:T(8,128)(2,1)S(1)} collective-permute-done((bf16[128,2048]{1,0:T(8,128)(2,1)S(1)}, bf16[128,2048]{1,0:T(8,128)(2,1)S(1)}, u32[]{:S(2)}, u32[]{:S(2)}) %collective-permute-start.9) | collective-permute-done | bytes 524320 | tf_op jit(solution)/shard_map/ppermute | solution.py:41
  157.4 14.0 %fusion.131 = (bf16[1,2048,2,1024]{3,2,1,0:T(2,128)(2,1)}, bf16[1,2048,2,1024]{3,2,1,0:T(2,128)(2,1)S(1)}) fusion(bf16[2,2048,2,1024]{3,2,1,0:T(2,128)(2,1)} %param.26), kind=kLoop, calls=%fused_computation.292 | loop fusion | bytes 33554432 | tf_op jit(solution)/shard_map/slice | solution.py:126
  173.7 4.1 %collective-permute-done.11 = bf16[64,2048]{1,0:T(8,128)(2,1)S(1)} collective-permute-done((bf16[64,2048]{1,0:T(8,128)(2,1)S(1)}, bf16[64,2048]{1,0:T(8,128)(2,1)S(1)}, u32[]{:S(2)}, u32[]{:S(2)}) %collective-permute-start.11) | collective-permute-done | bytes 262176 | tf_op jit(solution)/shard_map/ppermute | solution.py:44
  177.9 6.1 %fusion.3 = f32[512,2,1024]{2,0,1:T(8,128)S(1)} fusion(bf16[1,2048,2,1024]{3,2,1,0:T(2,128)(2,1)S(1)} %get-tuple-element.34, s32[]{:T(128)S(6)} %select_n.217, bf16[512,2048]{1,0:T(8,128)(2,1)S(1)} %constant_dynamic-update-slice_fusion.5), kind=kOutput, calls=%fused_computation.9 | convolution fusion | flops 4299161600 | bytes 14680068 | tf_op jit(solution)/shard_map/rd,dtf->rtf/dot_general | solution.py:224
  184.0 4.6 %fusion.12 = f32[512,2048]{1,0:T(8,128)S(1)} fusion(bf16[2,1024,2048]{2,1,0:T(8,128)(2,1)} %param.27, f32[512,2,1024]{2,0,1:T(8,128)S(1)} %fusion.3), kind=kOutput, calls=%fused_computation.28 | convolution fusion | flops 2150629376 | bytes 12582912 | tf_op jit(solution)/shard_map/dot_general | solution.py:231
  192.3 7.0 %collective-permute-done.12 = bf16[64,2048]{1,0:T(8,128)(2,1)S(1)} collective-permute-done((bf16[64,2048]{1,0:T(8,128)(2,1)S(1)}, bf16[64,2048]{1,0:T(8,128)(2,1)S(1)}, u32[]{:S(2)}, u32[]{:S(2)}) %collective-permute-start.12) | collective-permute-done | bytes 262176 | tf_op jit(solution)/shard_map/ppermute | solution.py:61
  203.5 11.7 %collective-permute-done.13 = bf16[128,2048]{1,0:T(8,128)(2,1)S(1)} collective-permute-done((bf16[128,2048]{1,0:T(8,128)(2,1)S(1)}, bf16[128,2048]{1,0:T(8,128)(2,1)S(1)}, u32[]{:S(2)}, u32[]{:S(2)}) %collective-permute-start.13) | collective-permute-done | bytes 524320 | tf_op jit(solution)/shard_map/ppermute | solution.py:67
  221.8 8.5 %collective-permute-done.17 = bf16[128,2048]{1,0:T(8,128)(2,1)} collective-permute-done((bf16[128,2048]{1,0:T(8,128)(2,1)}, bf16[128,2048]{1,0:T(8,128)(2,1)}, u32[]{:S(2)}, u32[]{:S(2)}) %collective-permute-start.17) | collective-permute-done | bytes 524320 | tf_op jit(solution)/shard_map/ppermute | solution.py:41
  242.5 3.3 collective-permute-start.19
  261.1 3.1 fusion.36
  266.6 3.3 copy-done
  271.4 13.8 %all-gather.17.cloned.1.call-done = bf16[8,131,512]{2,1,0:T(8,128)(2,1)} async-done(((bf16[1,131,512]{2,1,0:T(8,128)(2,1)}), bf16[8,131,512]{2,1,0:T(8,128)(2,1)}) %all-gather.17.cloned.1.call-update) | async-done | bytes 1073168 | tf_op jit(solution)/shard_map/all_gather | solution.py:168
  290.0 5.1 %divide_convert_fusion = bf16[2,4,512,640]{2,3,1,0:T(8,128)(2,1)S(1)} fusion(f32[2,4,512,512]{2,3,1,0:T(8,128)} %copy-done, f32[2,4,512,128]{2,3,1,0:T(8,128)S(1)} %get-tuple-element.108, f32[2,4,512]{2,1,0:T(4,128)S(1)} %fusion.4, f32[2,4,512]{2,1,0:T(4,128)S(1)} %reduce_max.65), kind=kLoop, calls=%fused_computation.4 | loop fusion | flops 10485760 | bytes 15761408 | tf_op jit(solution)/shard_map/convert_element_type | solution.py:211
  297.8 16.7 %all-gather.19.cloned.1.call-done = f32[4,129,512]{2,1,0:T(8,128)} async-done(((f32[1,129,512]{2,1,0:T(8,128)}), f32[4,129,512]{2,1,0:T(8,128)}) %all-gather.19.cloned.1.call-update) | async-done | bytes 1056784 | tf_op jit(solution)/shard_map/all_gather | solution.py:177
  319.7 2.9 fusion.34
  326.1 4.3 %collective-permute-done.20 = bf16[64,2048]{1,0:T(8,128)(2,1)S(1)} collective-permute-done((bf16[64,2048]{1,0:T(8,128)(2,1)S(1)}, bf16[64,2048]{1,0:T(8,128)(2,1)S(1)}, u32[]{:S(2)}, u32[]{:S(2)}) %collective-permute-start.20) | collective-permute-done | bytes 262176 | tf_op jit(solution)/shard_map/ppermute | solution.py:61
  334.4 8.0 %collective-permute-done.21 = bf16[128,2048]{1,0:T(8,128)(2,1)S(1)} collective-permute-done((bf16[128,2048]{1,0:T(8,128)(2,1)S(1)}, bf16[128,2048]{1,0:T(8,128)(2,1)S(1)}, u32[]{:S(2)}, u32[]{:S(2)}) %collective-permute-start.21) | collective-permute-done | bytes 524320 | tf_op jit(solution)/shard_map/ppermute | solution.py:67
  347.0 9.1 %collective-permute-done.25 = bf16[128,2048]{1,0:T(8,128)(2,1)S(1)} collective-permute-done((bf16[128,2048]{1,0:T(8,128)(2,1)S(1)}, bf16[128,2048]{1,0:T(8,128)(2,1)S(1)}, u32[]{:S(2)}, u32[]{:S(2)}) %collective-permute-start.25) | collective-permute-done | bytes 524320 | tf_op jit(solution)/shard_map/ppermute | solution.py:41
  359.7 4.2 %collective-permute-done.26 = bf16[64,2048]{1,0:T(8,128)(2,1)S(1)} collective-permute-done((bf16[64,2048]{1,0:T(8,128)(2,1)S(1)}, bf16[64,2048]{1,0:T(8,128)(2,1)S(1)}, u32[]{:S(2)}, u32[]{:S(2)}) %collective-permute-start.26) | collective-permute-done | bytes 262176 | tf_op jit(solution)/shard_map/ppermute | solution.py:43
  364.1 6.1 %fusion.2 = f32[512,2,1024]{2,0,1:T(8,128)S(1)} fusion(bf16[1,2048,2,1024]{3,2,1,0:T(2,128)(2,1)S(1)} %bitcast.278, s32[]{:T(128)S(6)} %select_n.217, bf16[512,2048]{1,0:T(8,128)(2,1)S(1)} %constant_dynamic-update-slice_fusion.15), kind=kOutput, calls=%fused_computation.7 | convolution fusion | flops 4299161600 | bytes 14680068 | tf_op jit(solution)/shard_map/rd,dtf->rtf/dot_general | solution.py:224
  379.6 4.7 %collective-permute-done.28 = bf16[64,2048]{1,0:T(8,128)(2,1)S(1)} collective-permute-done((bf16[64,2048]{1,0:T(8,128)(2,1)S(1)}, bf16[64,2048]{1,0:T(8,128)(2,1)S(1)}, u32[]{:S(2)}, u32[]{:S(2)}) %collective-permute-start.28) | collective-permute-done | bytes 262176 | tf_op jit(solution)/shard_map/ppermute | solution.py:61
  (359 shorter events, 174.8 us)
Async XLA Ops:
  7.2 75.0 %all-gather.13.cloned.1.call-start = ((), (), s32[]{:S(2)}) async-start(), calls=%async_computation | async-start | bytes 1253376 | tf_op jit(solution)/shard_map/all_gather | solution.py:168
  11.9 27.4 %collective-permute-start = (bf16[128,2048]{1,0:T(8,128)(2,1)}, bf16[128,2048]{1,0:T(8,128)(2,1)}, u32[]{:S(2)}, u32[]{:S(2)}) collective-permute-start(bf16[128,2048]{1,0:T(8,128)(2,1)} %get-tuple-element.32), channel_id=1, source_target_pairs={{0,3},{1,0},{2,1},{3,2},{4,7},{5,4},{6,5},{7,6},{8,11},{9,8},{10,9... | collective-permute-start | bytes 1572872 | tf_op jit(solution)/shard_map/ppermute | solution.py:42
  16.0 14.9 %collective-permute-start.1 = (bf16[128,2048]{1,0:T(8,128)(2,1)}, bf16[128,2048]{1,0:T(8,128)(2,1)}, u32[]{:S(2)}, u32[]{:S(2)}) collective-permute-start(bf16[128,2048]{1,0:T(8,128)(2,1)} %get-tuple-element.32), channel_id=1, source_target_pairs={{0,1},{1,2},{2,3},{3,0},{4,5},{5,6},{6,7},{7,4},{8,9},{9,10},{10,1... | collective-permute-start | bytes 1572872 | tf_op jit(solution)/shard_map/ppermute | solution.py:41
  32.6 12.8 %collective-permute-start.2 = (bf16[64,2048]{1,0:T(8,128)(2,1)}, bf16[64,2048]{1,0:T(8,128)(2,1)}, u32[]{:S(2)}, u32[]{:S(2)}) collective-permute-start(bf16[64,2048]{1,0:T(8,128)(2,1)} %slice.362), channel_id=1, source_target_pairs={{0,1},{1,2},{2,3},{3,0},{4,5},{5,6},{6,7},{7,4},{8,9},{9,10},{10,1... | collective-permute-start | bytes 786440 | tf_op jit(solution)/shard_map/ppermute | solution.py:43
  40.3 7.5 %collective-permute-start.3 = (bf16[64,2048]{1,0:T(8,128)(2,1)S(1)}, bf16[64,2048]{1,0:T(8,128)(2,1)S(1)}, u32[]{:S(2)}, u32[]{:S(2)}) collective-permute-start(bf16[64,2048]{1,0:T(8,128)(2,1)S(1)} %slice.363), channel_id=1, source_target_pairs={{0,3},{1,0},{2,1},{3,2},{4,7},{5,4},{6,5},{7,6},{8,11},{9,8},{10,9... | collective-permute-start | bytes 786440 | tf_op jit(solution)/shard_map/ppermute | solution.py:44
  56.7 54.1 %all-gather.15.cloned.1.call-start = ((), (), s32[]{:S(2)}) async-start(), calls=%async_computation.1 | async-start | bytes 1392640 | tf_op jit(solution)/shard_map/all_gather | solution.py:177
  86.3 198.9 %all-gather.17.cloned.1.call-start = ((), (), s32[]{:S(2)}) async-start(), calls=%async_computation.2 | async-start | bytes 1253376 | tf_op jit(solution)/shard_map/all_gather | solution.py:168
  120.3 7.7 %collective-permute-start.4 = (bf16[64,2048]{1,0:T(8,128)(2,1)S(1)}, bf16[64,2048]{1,0:T(8,128)(2,1)S(1)}, u32[]{:S(2)}, u32[]{:S(2)}) collective-permute-start(bf16[64,2048]{1,0:T(8,128)(2,1)S(1)} %get-tuple-element.69), channel_id=1, source_target_pairs={{0,1},{1,2},{2,3},{3,0},{4,5},{5,6},{6,7},{7,4},{8,9},{9,10},{10,1... | collective-permute-start | bytes 786440 | tf_op jit(solution)/shard_map/ppermute | solution.py:61
  129.7 11.4 %collective-permute-start.5 = (bf16[128,2048]{1,0:T(8,128)(2,1)S(1)}, bf16[128,2048]{1,0:T(8,128)(2,1)S(1)}, u32[]{:S(2)}, u32[]{:S(2)}) collective-permute-start(bf16[128,2048]{1,0:T(8,128)(2,1)S(1)} %pad_maximum_fusion.1), channel_id=1, source_target_pairs={{0,1},{1,2},{2,3},{3,0},{4,5},{5,6},{6,7},{7,4},{8,9},{9,10},{10,1... | collective-permute-start | bytes 1572872 | tf_op jit(solution)/shard_map/ppermute | solution.py:67
  132.1 10.3 %collective-permute-start.7 = (bf16[128,2048]{1,0:T(8,128)(2,1)}, bf16[128,2048]{1,0:T(8,128)(2,1)S(1)}, u32[]{:S(2)}, u32[]{:S(2)}) collective-permute-start(bf16[128,2048]{1,0:T(8,128)(2,1)} %pad_maximum_fusion.2), channel_id=1, source_target_pairs={{0,3},{1,0},{2,1},{3,2},{4,7},{5,4},{6,5},{7,6},{8,11},{9,8},{10,9... | collective-permute-start | bytes 1572872 | tf_op jit(solution)/shard_map/ppermute | solution.py:68
  144.2 11.7 %collective-permute-start.9 = (bf16[128,2048]{1,0:T(8,128)(2,1)S(1)}, bf16[128,2048]{1,0:T(8,128)(2,1)S(1)}, u32[]{:S(2)}, u32[]{:S(2)}) collective-permute-start(bf16[128,2048]{1,0:T(8,128)(2,1)S(1)} %get-tuple-element.27), channel_id=1, source_target_pairs={{0,1},{1,2},{2,3},{3,0},{4,5},{5,6},{6,7},{7,4},{8,9},{9,10},{10,1... | collective-permute-start | bytes 1572872 | tf_op jit(solution)/shard_map/ppermute | solution.py:41
  145.5 25.8 %collective-permute-start.8 = (bf16[128,2048]{1,0:T(8,128)(2,1)S(1)}, bf16[128,2048]{1,0:T(8,128)(2,1)S(1)}, u32[]{:S(2)}, u32[]{:S(2)}) collective-permute-start(bf16[128,2048]{1,0:T(8,128)(2,1)S(1)} %get-tuple-element.27), channel_id=1, source_target_pairs={{0,3},{1,0},{2,1},{3,2},{4,7},{5,4},{6,5},{7,6},{8,11},{9,8},{10,9... | collective-permute-start | bytes 1572872 | tf_op jit(solution)/shard_map/ppermute | solution.py:42
  155.9 17.8 %collective-permute-start.10 = (bf16[64,2048]{1,0:T(8,128)(2,1)S(1)}, bf16[64,2048]{1,0:T(8,128)(2,1)S(1)}, u32[]{:S(2)}, u32[]{:S(2)}) collective-permute-start(bf16[64,2048]{1,0:T(8,128)(2,1)S(1)} %slice.379), channel_id=1, source_target_pairs={{0,1},{1,2},{2,3},{3,0},{4,5},{5,6},{6,7},{7,4},{8,9},{9,10},{10,1... | collective-permute-start | bytes 786440 | tf_op jit(solution)/shard_map/ppermute | solution.py:43
  188.7 10.6 %collective-permute-start.12 = (bf16[64,2048]{1,0:T(8,128)(2,1)S(1)}, bf16[64,2048]{1,0:T(8,128)(2,1)S(1)}, u32[]{:S(2)}, u32[]{:S(2)}) collective-permute-start(bf16[64,2048]{1,0:T(8,128)(2,1)S(1)} %get-tuple-element.67), channel_id=1, source_target_pairs={{0,1},{1,2},{2,3},{3,0},{4,5},{5,6},{6,7},{7,4},{8,9},{9,10},{10,1... | collective-permute-start | bytes 786440 | tf_op jit(solution)/shard_map/ppermute | solution.py:61
  190.7 9.2 %collective-permute-start.14 = (bf16[64,2048]{1,0:T(8,128)(2,1)S(1)}, bf16[64,2048]{1,0:T(8,128)(2,1)S(1)}, u32[]{:S(2)}, u32[]{:S(2)}) collective-permute-start(bf16[64,2048]{1,0:T(8,128)(2,1)S(1)} %get-tuple-element.68), channel_id=1, source_target_pairs={{0,3},{1,0},{2,1},{3,2},{4,7},{5,4},{6,5},{7,6},{8,11},{9,8},{10,9... | collective-permute-start | bytes 786440 | tf_op jit(solution)/shard_map/ppermute | solution.py:62
  200.0 15.2 %collective-permute-start.13 = (bf16[128,2048]{1,0:T(8,128)(2,1)S(1)}, bf16[128,2048]{1,0:T(8,128)(2,1)S(1)}, u32[]{:S(2)}, u32[]{:S(2)}) collective-permute-start(bf16[128,2048]{1,0:T(8,128)(2,1)S(1)} %pad_maximum_fusion.3), channel_id=1, source_target_pairs={{0,1},{1,2},{2,3},{3,0},{4,5},{5,6},{6,7},{7,4},{8,9},{9,10},{10,1... | collective-permute-start | bytes 1572872 | tf_op jit(solution)/shard_map/ppermute | solution.py:67
  201.7 14.6 %collective-permute-start.15 = (bf16[128,2048]{1,0:T(8,128)(2,1)S(1)}, bf16[128,2048]{1,0:T(8,128)(2,1)S(1)}, u32[]{:S(2)}, u32[]{:S(2)}) collective-permute-start(bf16[128,2048]{1,0:T(8,128)(2,1)S(1)} %pad_maximum_fusion.4), channel_id=1, source_target_pairs={{0,3},{1,0},{2,1},{3,2},{4,7},{5,4},{6,5},{7,6},{8,11},{9,8},{10,9... | collective-permute-start | bytes 1572872 | tf_op jit(solution)/shard_map/ppermute | solution.py:68
  217.8 12.4 %collective-permute-start.17 = (bf16[128,2048]{1,0:T(8,128)(2,1)}, bf16[128,2048]{1,0:T(8,128)(2,1)}, u32[]{:S(2)}, u32[]{:S(2)}) collective-permute-start(bf16[128,2048]{1,0:T(8,128)(2,1)} %get-tuple-element.23), channel_id=1, source_target_pairs={{0,1},{1,2},{2,3},{3,0},{4,5},{5,6},{6,7},{7,4},{8,9},{9,10},{10,1... | collective-permute-start | bytes 1572872 | tf_op jit(solution)/shard_map/ppermute | solution.py:41
  219.0 22.5 %collective-permute-start.16 = (bf16[128,2048]{1,0:T(8,128)(2,1)}, bf16[128,2048]{1,0:T(8,128)(2,1)}, u32[]{:S(2)}, u32[]{:S(2)}) collective-permute-start(bf16[128,2048]{1,0:T(8,128)(2,1)} %get-tuple-element.23), channel_id=1, source_target_pairs={{0,3},{1,0},{2,1},{3,2},{4,7},{5,4},{6,5},{7,6},{8,11},{9,8},{10,9... | collective-permute-start | bytes 1572872 | tf_op jit(solution)/shard_map/ppermute | solution.py:42
  232.0 15.8 %collective-permute-start.18 = (bf16[64,2048]{1,0:T(8,128)(2,1)}, bf16[64,2048]{1,0:T(8,128)(2,1)}, u32[]{:S(2)}, u32[]{:S(2)}) collective-permute-start(bf16[64,2048]{1,0:T(8,128)(2,1)} %slice.385), channel_id=1, source_target_pairs={{0,1},{1,2},{2,3},{3,0},{4,5},{5,6},{6,7},{7,4},{8,9},{9,10},{10,1... | collective-permute-start | bytes 786440 | tf_op jit(solution)/shard_map/ppermute | solution.py:43
  242.5 7.2 %collective-permute-start.19 = (bf16[64,2048]{1,0:T(8,128)(2,1)S(1)}, bf16[64,2048]{1,0:T(8,128)(2,1)S(1)}, u32[]{:S(2)}, u32[]{:S(2)}) collective-permute-start(bf16[64,2048]{1,0:T(8,128)(2,1)S(1)} %slice.386), channel_id=1, source_target_pairs={{0,3},{1,0},{2,1},{3,2},{4,7},{5,4},{6,5},{7,6},{8,11},{9,8},{10,9... | collective-permute-start | bytes 786440 | tf_op jit(solution)/shard_map/ppermute | solution.py:44
  260.9 53.6 %all-gather.19.cloned.1.call-start = ((), (), s32[]{:S(2)}) async-start(), calls=%async_computation.3 | async-start | bytes 1392640 | tf_op jit(solution)/shard_map/all_gather | solution.py:177
  322.7 7.7 %collective-permute-start.20 = (bf16[64,2048]{1,0:T(8,128)(2,1)S(1)}, bf16[64,2048]{1,0:T(8,128)(2,1)S(1)}, u32[]{:S(2)}, u32[]{:S(2)}) collective-permute-start(bf16[64,2048]{1,0:T(8,128)(2,1)S(1)} %get-tuple-element.63), channel_id=1, source_target_pairs={{0,1},{1,2},{2,3},{3,0},{4,5},{5,6},{6,7},{7,4},{8,9},{9,10},{10,1... | collective-permute-start | bytes 786440 | tf_op jit(solution)/shard_map/ppermute | solution.py:61
  331.0 11.4 %collective-permute-start.21 = (bf16[128,2048]{1,0:T(8,128)(2,1)S(1)}, bf16[128,2048]{1,0:T(8,128)(2,1)S(1)}, u32[]{:S(2)}, u32[]{:S(2)}) collective-permute-start(bf16[128,2048]{1,0:T(8,128)(2,1)S(1)} %pad_maximum_fusion.6), channel_id=1, source_target_pairs={{0,1},{1,2},{2,3},{3,0},{4,5},{5,6},{6,7},{7,4},{8,9},{9,10},{10,1... | collective-permute-start | bytes 1572872 | tf_op jit(solution)/shard_map/ppermute | solution.py:67
  332.6 10.5 %collective-permute-start.23 = (bf16[128,2048]{1,0:T(8,128)(2,1)S(1)}, bf16[128,2048]{1,0:T(8,128)(2,1)S(1)}, u32[]{:S(2)}, u32[]{:S(2)}) collective-permute-start(bf16[128,2048]{1,0:T(8,128)(2,1)S(1)} %pad_maximum_fusion.7), channel_id=1, source_target_pairs={{0,3},{1,0},{2,1},{3,2},{4,7},{5,4},{6,5},{7,6},{8,11},{9,8},{10,9... | collective-permute-start | bytes 1572872 | tf_op jit(solution)/shard_map/ppermute | solution.py:68
  343.7 12.4 %collective-permute-start.25 = (bf16[128,2048]{1,0:T(8,128)(2,1)S(1)}, bf16[128,2048]{1,0:T(8,128)(2,1)S(1)}, u32[]{:S(2)}, u32[]{:S(2)}) collective-permute-start(bf16[128,2048]{1,0:T(8,128)(2,1)S(1)} %get-tuple-element.18), channel_id=1, source_target_pairs={{0,1},{1,2},{2,3},{3,0},{4,5},{5,6},{6,7},{7,4},{8,9},{9,10},{10,1... | collective-permute-start | bytes 1572872 | tf_op jit(solution)/shard_map/ppermute | solution.py:41
  345.2 12.3 %collective-permute-start.24 = (bf16[128,2048]{1,0:T(8,128)(2,1)S(1)}, bf16[128,2048]{1,0:T(8,128)(2,1)S(1)}, u32[]{:S(2)}, u32[]{:S(2)}) collective-permute-start(bf16[128,2048]{1,0:T(8,128)(2,1)S(1)} %get-tuple-element.18), channel_id=1, source_target_pairs={{0,3},{1,0},{2,1},{3,2},{4,7},{5,4},{6,5},{7,6},{8,11},{9,8},{10,9... | collective-permute-start | bytes 1572872 | tf_op jit(solution)/shard_map/ppermute | solution.py:42
  356.1 7.9 %collective-permute-start.26 = (bf16[64,2048]{1,0:T(8,128)(2,1)S(1)}, bf16[64,2048]{1,0:T(8,128)(2,1)S(1)}, u32[]{:S(2)}, u32[]{:S(2)}) collective-permute-start(bf16[64,2048]{1,0:T(8,128)(2,1)S(1)} %slice.402), channel_id=1, source_target_pairs={{0,1},{1,2},{2,3},{3,0},{4,5},{5,6},{6,7},{7,4},{8,9},{9,10},{10,1... | collective-permute-start | bytes 786440 | tf_op jit(solution)/shard_map/ppermute | solution.py:43
  374.7 9.6 %collective-permute-start.28 = (bf16[64,2048]{1,0:T(8,128)(2,1)S(1)}, bf16[64,2048]{1,0:T(8,128)(2,1)S(1)}, u32[]{:S(2)}, u32[]{:S(2)}) collective-permute-start(bf16[64,2048]{1,0:T(8,128)(2,1)S(1)} %get-tuple-element.61), channel_id=1, source_target_pairs={{0,1},{1,2},{2,3},{3,0},{4,5},{5,6},{6,7},{7,4},{8,9},{9,10},{10,1... | collective-permute-start | bytes 786440 | tf_op jit(solution)/shard_map/ppermute | solution.py:61
  375.9 8.4 %collective-permute-start.30 = (bf16[64,2048]{1,0:T(8,128)(2,1)S(1)}, bf16[64,2048]{1,0:T(8,128)(2,1)S(1)}, u32[]{:S(2)}, u32[]{:S(2)}) collective-permute-start(bf16[64,2048]{1,0:T(8,128)(2,1)S(1)} %get-tuple-element.62), channel_id=1, source_target_pairs={{0,3},{1,0},{2,1},{3,2},{4,7},{5,4},{6,5},{7,6},{8,11},{9,8},{10,9... | collective-permute-start | bytes 786440 | tf_op jit(solution)/shard_map/ppermute | solution.py:62
  386.5 10.7 %collective-permute-start.29 = (bf16[128,2048]{1,0:T(8,128)(2,1)}, bf16[128,2048]{1,0:T(8,128)(2,1)}, u32[]{:S(2)}, u32[]{:S(2)}) collective-permute-start(bf16[128,2048]{1,0:T(8,128)(2,1)} %pad_maximum_fusion.8), channel_id=1, source_target_pairs={{0,1},{1,2},{2,3},{3,0},{4,5},{5,6},{6,7},{7,4},{8,9},{9,10},{10,1... | collective-permute-start | bytes 1572872 | tf_op jit(solution)/shard_map/ppermute | solution.py:67
  388.0 9.9 %collective-permute-start.31 = (bf16[128,2048]{1,0:T(8,128)(2,1)}, bf16[128,2048]{1,0:T(8,128)(2,1)}, u32[]{:S(2)}, u32[]{:S(2)}) collective-permute-start(bf16[128,2048]{1,0:T(8,128)(2,1)} %pad_maximum_fusion.9), channel_id=1, source_target_pairs={{0,3},{1,0},{2,1},{3,2},{4,7},{5,4},{6,5},{7,6},{8,11},{9,8},{10,9... | collective-permute-start | bytes 1572872 | tf_op jit(solution)/shard_map/ppermute | solution.py:68
  (62 other events, 549.6 us)
Sparse Core Ops, SparseCore 0:
  56.9 25.2 all-gather.12
  86.4 24.3 all-gather.14
  261.0 24.1 all-gather.16
  290.1 24.3 all-gather.18

commit v5 on v3

--- a/solution.py
+++ b/solution.py
@@ -52,6 +52,39 @@
     got_before = lax.ppermute(next_part.astype(jnp.bfloat16), axis, ahead)
     got_after = lax.ppermute(prev_part.astype(jnp.bfloat16), axis, behind)
     return block(0) + got_before.astype(jnp.float32) + got_after.astype(jnp.float32)
+
+
+def ring_pieces(piece, axis):
+    count = lax.axis_size(axis)
+    rows = piece.shape[0]
+    half = rows // 2
+    ahead = ring_pairs(count, 1)
+    behind = ring_pairs(count, -1)
+    from_before = lax.ppermute(piece, axis, ahead)
+    from_after = lax.ppermute(piece, axis, behind)
+    far_top = lax.ppermute(from_before[:half], axis, ahead)
+    far_bottom = lax.ppermute(from_after[half:], axis, behind)
+    return from_before, from_after, jnp.concatenate([far_top, far_bottom], axis=0)
+
+
+def ring_scatter_parts(own, next_part, prev_part, far, axis):
+    count = lax.axis_size(axis)
+    half = own.shape[0] // 2
+    ahead = ring_pairs(count, 1)
+    behind = ring_pairs(count, -1)
+    sent_top = lax.ppermute(far[:half].astype(jnp.bfloat16), axis, ahead)
+    sent_bottom = lax.ppermute(far[half:].astype(jnp.bfloat16), axis, behind)
+    next_part = jnp.concatenate([next_part[:half] + sent_top.astype(jnp.float32), next_part[half:]])
+    prev_part = jnp.concatenate([prev_part[:half], prev_part[half:] + sent_bottom.astype(jnp.float32)])
+    got_before = lax.ppermute(next_part.astype(jnp.bfloat16), axis, ahead)
+    got_after = lax.ppermute(prev_part.astype(jnp.bfloat16), axis, behind)
+    return own + got_before.astype(jnp.float32) + got_after.astype(jnp.float32)
+
+
+def feed_forward(rows, widening_matrix, down_weight):
+    both = jnp.einsum("rd,dtf->rtf", rows, widening_matrix, preferred_element_type=jnp.float32)
+    inner = (jax.nn.silu(both[:, 0]) * both[:, 1]).astype(jnp.bfloat16)
+    return jnp.dot(inner, down_weight, preferred_element_type=jnp.float32)
 
 
 def rms_norm(value, gain):
@@ -108,7 +141,6 @@
         query_weight = w_query[layer]
         pair_weight = w_kv[layer]
         out_weight = w_out[layer]
-        widening_matrix = w_gate_up[layer]
         down_weight = w_down[layer]
         normed = rms_norm(stream, attn_gain[layer])
         project_piece = ring_gather(normed, "head")
@@ -151,6 +183,10 @@
             [written[0].astype(jnp.bfloat16), rate_high, rate_mid, rate_low], axis=0
         )
         gathered = lax.all_gather(payload, "seg")
+        if layer == 0:
+            gathered, gate_up_slices = lax.optimization_barrier(
+                (gathered, [w_gate_up[index] for index in range(DEPTH_NUMBER)])
+            )
         written_all = gathered[:, :MEM].astype(jnp.float32)
         rate_parts = gathered[:, MEM:, ::HD].astype(jnp.float32)
         rate_all = rate_parts[:, 0] + rate_parts[:, 1] + rate_parts[:, 2]
@@ -199,14 +235,18 @@
             jnp.dot(outputs, out_weight, preferred_element_type=jnp.float32), "head"
         )
         middle = stream + mixed
-        both = jnp.einsum(
-            "rd,dtf->rtf",
-            ring_gather(rms_norm(middle, mlp_gain[layer]), "head"),
-            widening_matrix,
-            preferred_element_type=jnp.float32,
-        )
-        inner = (jax.nn.silu(both[:, 0]) * both[:, 1]).astype(jnp.bfloat16)
-        down = ring_scatter(jnp.dot(inner, down_weight, preferred_element_type=jnp.float32), "head")
+        mlp_piece = rms_norm(middle, mlp_gain[layer])
+        from_before, from_after, far_rows = ring_pieces(mlp_piece, "head")
+        widening_matrix = gate_up_slices[layer]
+        own_part = feed_forward(mlp_piece, widening_matrix, down_weight)
+        side_parts = feed_forward(
+            jnp.concatenate([from_before, from_after], axis=0), widening_matrix, down_weight
+        )
+        far_part = feed_forward(far_rows, widening_matrix, down_weight)
+        piece_rows = mlp_piece.shape[0]
+        down = ring_scatter_parts(
+            own_part, side_parts[piece_rows:], side_parts[:piece_rows], far_part, "head"
+        )
         stream = middle + down
     return (stream, jnp.stack(stored))
 

time: 392 us -> 389 us (level)
  waiting for transfers between devices: 156 us -> 125 us
  local copies, waits for them, and re-layouts: 62.9 us -> 78.3 us
  matrix products: 54.7 us -> 68.1 us
    ppermute x0 -> x16, waiting for transfers between devices: none -> 32 us  [the longest x2 17.1 us: ring_pieces(): from_before = lax.ppermute(piece, axis, ahead)]
    ppermute x0 -> x16, starting transfers between devices: none -> 27.5 us  [the longest x2 7.04 us: ring_scatter_parts(): got_after = lax.ppermute(prev_part.astype(jnp.bfloat16), axis, behind)]
    ppermute x4 -> x2, waiting for transfers between devices: 41.4 us -> 19.8 us  [ring_gather(): from_before = lax.ppermute(piece, axis, ahead)]
    optimization_barrier x0 -> x1, local copies, waits for them, and re-layouts: none -> 15.7 us  [body(): lax.optimization_barrier((gathered, [w_gate_up[index] for index in range(...]
    dot_general x4 -> x12, matrix products: 19.2 us -> 34 us  [the longest x6 25.8 us: feed_forward(): jnp.einsum('rd,dtf->rtf', rows, widening_matrix, preferred_element_type=j...]
    squeeze x0 -> x1, local copies, waits for them, and re-layouts: none -> 14.6 us  [body(): w_gate_up[index]]
    all_gather x2, waiting for transfers between devices: 51.1 us -> 38.1 us  [body(): gathered = lax.all_gather(payload, 'seg')]
    slice x2 -> x9, local copies, waits for them, and re-layouts: 14.6 us -> 2.73 us  [the longest x2 0.99 us: ring_pieces(): far_bottom = lax.ppermute(from_after[half:], axis, behind)]
  transfers between devices with their start and end apart: 34 -> 34, of which waited for: 25 -> 21; matrix products, arithmetic and copies ran while one was open for 21% -> 28% of each run, Pallas kernels for 0% -> 0%
where the time goes in v5:
time: 389 us; the launch traced here: 383 us
  waiting for transfers between devices  125 us (32%)
  local copies, waits for them, and re-layouts  78.3 us (20%)
  matrix products  68.1 us (18%)
  starting transfers between devices  55.3 us (14%)
  other arithmetic  40.7 us (10%)
  between operations  15.8 us (4%)
    all_gather x2, waiting for transfers between devices, body(): gathered = lax.all_gather(payload, 'seg')  38.1 us
    dot_general x6, matrix products, feed_forward(): jnp.einsum('rd,dtf->rtf', rows, widening_matrix, preferred_element_type=j...  25.8 us
    ppermute x2, waiting for transfers between devices, ring_gather(): from_before = lax.ppermute(piece, axis, ahead)  19.8 us
    ppermute x2, waiting for transfers between devices, ring_scatter(): got_before = lax.ppermute(next_part.astype(jnp.bfloat16), axis, ahead)  19.8 us
    ppermute x2, waiting for transfers between devices, ring_pieces(): from_before = lax.ppermute(piece, axis, ahead)  17.1 us
    optimization_barrier x1, local copies, waits for them, and re-layouts, body(): lax.optimization_barrier((gathered, [w_gate_up[index] for index in range(...  15.7 us
    squeeze x1, local copies, waits for them, and re-layouts, body(): w_gate_up[index]  14.6 us
    ppermute x2, waiting for transfers between devices, ring_scatter(): sent_top = lax.ppermute(far[:half].astype(jnp.bfloat16), axis, ahead)  11.5 us
  transfers between devices with their start and end apart: 34, of which 21 were waited for; matrix products, arithmetic and copies ran while one was open for 28% of the time, Pallas kernels for 0%

profile of v5, /device:TPU:0, one launch (start us, length us, event | category | flops | bytes accessed | tf_op | source)
XLA Modules:
  0.0 383.0 jit_solution(4836981183902222893)
XLA Ops:
  12.5 4.1 %collective-permute-start = (bf16[128,2048]{1,0:T(8,128)(2,1)}, bf16[128,2048]{1,0:T(8,128)(2,1)}, u32[]{:S(2)}, u32[]{:S(2)}) collective-permute-start(bf16[128,2048]{1,0:T(8,128)(2,1)} %get-tuple-element.24), channel_id=1, source_target_pairs={{0,3},{1,0},{2,1},{3,2},{4,7},{5,4},{6,5},{7,6},{8,11},{9,8},{10,9... | collective-permute-start | bytes 1572872 | tf_op jit(solution)/shard_map/ppermute | solution.py:27
  20.4 11.1 %collective-permute-done.1 = bf16[128,2048]{1,0:T(8,128)(2,1)} collective-permute-done((bf16[128,2048]{1,0:T(8,128)(2,1)}, bf16[128,2048]{1,0:T(8,128)(2,1)}, u32[]{:S(2)}, u32[]{:S(2)}) %collective-permute-start.1) | collective-permute-done | bytes 524320 | tf_op jit(solution)/shard_map/ppermute | solution.py:26
  34.9 3.3 collective-permute-start.3
  51.1 3.9 %slice_bitcast_fusion.2 = (bf16[512,2048]{0,1:T(8,128)(2,1)}, bf16[512,2048]{0,1:T(8,128)(2,1)S(1)}) fusion(bf16[2,2048,512]{2,1,0:T(8,128)(2,1)} %param.23), kind=kLoop, calls=%fused_computation.75 | loop fusion | bytes 8388608 | tf_op jit(solution)/shard_map/dot_general | solution.py:149
  58.8 14.6 %slice_bitcast_fusion = (bf16[2048,2,1024]{2,1,0:T(2,128)(2,1)}, bf16[2048,2,1024]{2,1,0:T(2,128)(2,1)}) fusion(bf16[2,2048,2,1024]{3,2,1,0:T(2,128)(2,1)} %param.26), kind=kLoop, calls=%fused_computation.10 | loop fusion | bytes 33554432 | tf_op jit(solution)/shard_map/squeeze | solution.py:188
  79.1 4.6 %divide_convert_fusion.1 = bf16[2,4,512,640]{2,3,1,0:T(8,128)(2,1)} fusion(f32[2,4,512,512]{2,3,1,0:T(8,128)S(1)} %get-tuple-element.88, f32[2,4,512,128]{2,3,1,0:T(8,128)} %copy-done.1, f32[2,4,512]{2,1,0:T(4,128)S(1)} %fusion.3, f32[2,4,512]{2,1,0:T(4,128)S(1)} %reduce_max.61), kind=kLoop, calls=%fused_computation.5 | loop fusion | flops 10485760 | bytes 15761408 | tf_op jit(solution)/shard_map/convert_element_type | solution.py:225
  86.8 12.3 %all-gather.7.cloned.1.call-done = bf16[32,131,512]{2,1,0:T(8,128)(2,1)} async-done(((bf16[1,131,512]{2,1,0:T(8,128)(2,1)}), bf16[32,131,512]{2,1,0:T(8,128)(2,1)}) %all-gather.7.cloned.1.call-update) | async-done | bytes 4292624 | tf_op jit(solution)/shard_map/all_gather | solution.py:185
  99.0 15.7 %copy.139 = bf16[32,131,512]{0,2,1:T(8,128)(2,1)} copy(bf16[32,131,512]{2,1,0:T(8,128)(2,1)} %all-gather.7.cloned.1.call-done) | data formatting | bytes 8585216 | tf_op jit(solution)/shard_map/optimization_barrier | solution.py:187
  131.2 5.1 %collective-permute-done.4 = bf16[64,2048]{1,0:T(8,128)(2,1)S(1)} collective-permute-done((bf16[64,2048]{1,0:T(8,128)(2,1)S(1)}, bf16[64,2048]{1,0:T(8,128)(2,1)S(1)}, u32[]{:S(2)}, u32[]{:S(2)}) %collective-permute-start.4) | collective-permute-done | bytes 262176 | tf_op jit(solution)/shard_map/ppermute | solution.py:46
  143.3 9.9 %collective-permute-done.5 = bf16[128,2048]{1,0:T(8,128)(2,1)S(1)} collective-permute-done((bf16[128,2048]{1,0:T(8,128)(2,1)}, bf16[128,2048]{1,0:T(8,128)(2,1)S(1)}, u32[]{:S(2)}, u32[]{:S(2)}) %collective-permute-start.5) | collective-permute-done | bytes 524320 | tf_op jit(solution)/shard_map/ppermute | solution.py:52
  159.1 10.1 %collective-permute-done.8 = bf16[128,2048]{1,0:T(8,128)(2,1)S(1)} collective-permute-done((bf16[128,2048]{1,0:T(8,128)(2,1)S(1)}, bf16[128,2048]{1,0:T(8,128)(2,1)S(1)}, u32[]{:S(2)}, u32[]{:S(2)}) %collective-permute-start.8) | collective-permute-done | bytes 524320 | tf_op jit(solution)/shard_map/ppermute | solution.py:63
  169.3 3.7 collective-permute-start.11
  173.1 6.3 %fusion.12 = f32[256,2,1024]{2,0,1:T(8,128)S(1)} fusion(bf16[2048,2,1024]{2,1,0:T(2,128)(2,1)} %get-tuple-element.7, bf16[128,2048]{1,0:T(8,128)(2,1)S(1)} %collective-permute-done.9, bf16[128,2048]{1,0:T(8,128)(2,1)S(1)} %collective-permute-done.8), kind=kOutput, calls=%fused_computation.22 | convolution fusion | flops 2149580800 | bytes 11534336 | tf_op jit(solution)/shard_map/rd,dtf->rtf/dot_general | solution.py:85
  184.7 3.2 collective-permute-start.14
  187.9 4.5 %collective-permute-done.12 = bf16[64,2048]{1,0:T(8,128)(2,1)S(1)} collective-permute-done((bf16[64,2048]{1,0:T(8,128)(2,1)S(1)}, bf16[64,2048]{1,0:T(8,128)(2,1)S(1)}, u32[]{:S(2)}, u32[]{:S(2)}) %collective-permute-start.12) | collective-permute-done | bytes 262176 | tf_op jit(solution)/shard_map/ppermute | solution.py:75
  192.7 3.5 collective-permute-start.15
  200.0 3.5 collective-permute-done.13
  208.5 8.7 %collective-permute-done.17 = bf16[128,2048]{1,0:T(8,128)(2,1)S(1)} collective-permute-done((bf16[128,2048]{1,0:T(8,128)(2,1)}, bf16[128,2048]{1,0:T(8,128)(2,1)S(1)}, u32[]{:S(2)}, u32[]{:S(2)}) %collective-permute-start.17) | collective-permute-done | bytes 524320 | tf_op jit(solution)/shard_map/ppermute | solution.py:26
  236.5 4.2 %copy.161 = bf16[512,2048]{1,0:T(8,128)(2,1)} copy(bf16[512,2048]{0,1:T(8,128)(2,1)} %get-tuple-element.31) | data formatting | bytes 4194304 | tf_op jit(solution)/shard_map/dot_general | solution.py:149
  241.5 3.7 fusion.52
  249.1 4.6 %divide_convert_fusion = bf16[2,4,512,640]{2,3,1,0:T(8,128)(2,1)} fusion(f32[2,4,512,512]{2,3,1,0:T(8,128)S(1)} %get-tuple-element.98, f32[2,4,512,128]{2,3,1,0:T(8,128)} %copy-done, f32[2,4,512]{2,1,0:T(4,128)S(1)} %fusion.2, f32[2,4,512]{2,1,0:T(4,128)S(1)} %reduce_max.65), kind=kLoop, calls=%fused_computation.4 | loop fusion | flops 10485760 | bytes 15761408 | tf_op jit(solution)/shard_map/convert_element_type | solution.py:225
  256.8 25.8 %all-gather.9.cloned.1.call-done = bf16[32,131,512]{2,1,0:T(8,128)(2,1)} async-done(((bf16[1,131,512]{2,1,0:T(8,128)(2,1)}), bf16[32,131,512]{2,1,0:T(8,128)(2,1)}) %all-gather.9.cloned.1.call-update) | async-done | bytes 4292624 | tf_op jit(solution)/shard_map/all_gather | solution.py:185
  297.0 6.3 %collective-permute-done.20 = bf16[64,2048]{1,0:T(8,128)(2,1)S(1)} collective-permute-done((bf16[64,2048]{1,0:T(8,128)(2,1)S(1)}, bf16[64,2048]{1,0:T(8,128)(2,1)S(1)}, u32[]{:S(2)}, u32[]{:S(2)}) %collective-permute-start.20) | collective-permute-done | bytes 262176 | tf_op jit(solution)/shard_map/ppermute | solution.py:46
  308.2 9.9 %collective-permute-done.21 = bf16[128,2048]{1,0:T(8,128)(2,1)S(1)} collective-permute-done((bf16[128,2048]{1,0:T(8,128)(2,1)S(1)}, bf16[128,2048]{1,0:T(8,128)(2,1)S(1)}, u32[]{:S(2)}, u32[]{:S(2)}) %collective-permute-start.21) | collective-permute-done | bytes 524320 | tf_op jit(solution)/shard_map/ppermute | solution.py:52
  328.9 7.0 %collective-permute-done.24 = bf16[128,2048]{1,0:T(8,128)(2,1)} collective-permute-done((bf16[128,2048]{1,0:T(8,128)(2,1)}, bf16[128,2048]{1,0:T(8,128)(2,1)}, u32[]{:S(2)}, u32[]{:S(2)}) %collective-permute-start.24) | collective-permute-done | bytes 524320 | tf_op jit(solution)/shard_map/ppermute | solution.py:63
  337.9 3.3 collective-permute-start.27
  341.2 6.7 %fusion.6 = f32[256,2,1024]{2,0,1:T(8,128)S(1)} fusion(bf16[2048,2,1024]{2,1,0:T(2,128)(2,1)} %get-tuple-element.8, bf16[128,2048]{1,0:T(8,128)(2,1)} %collective-permute-done.25, bf16[128,2048]{1,0:T(8,128)(2,1)} %collective-permute-done.24), kind=kOutput, calls=%fused_computation.16 | convolution fusion | flops 2149580800 | bytes 11534336 | tf_op jit(solution)/shard_map/rd,dtf->rtf/dot_general | solution.py:85
  348.0 3.7 fusion.183
  355.6 3.2 collective-permute-start.30
  358.9 4.5 %collective-permute-done.28 = bf16[64,2048]{1,0:T(8,128)(2,1)S(1)} collective-permute-done((bf16[64,2048]{1,0:T(8,128)(2,1)S(1)}, bf16[64,2048]{1,0:T(8,128)(2,1)S(1)}, u32[]{:S(2)}, u32[]{:S(2)}) %collective-permute-start.28) | collective-permute-done | bytes 262176 | tf_op jit(solution)/shard_map/ppermute | solution.py:75
  363.7 3.6 collective-permute-start.31
  367.2 4.0 %fusion.8 = f32[128,2,1024]{2,0,1:T(8,128)S(1)} fusion(bf16[2048,2,1024]{2,1,0:T(2,128)(2,1)S(1)} %bitcast.299, bf16[128,2048]{1,0:T(8,128)(2,1)} %multiply_convert_fusion), kind=kOutput, calls=%fused_computation.18 | convolution fusion | flops 1073741824 | bytes 9961472 | tf_op jit(solution)/shard_map/rd,dtf->rtf/dot_general | solution.py:85
  (299 shorter events, 148.7 us)
Async XLA Ops:
  7.2 91.9 %all-gather.7.cloned.1.call-start = ((), (), s32[]{:S(2)}) async-start(), calls=%async_computation | async-start | bytes 4595712 | tf_op jit(solution)/shard_map/all_gather | solution.py:185
  12.5 21.5 %collective-permute-start = (bf16[128,2048]{1,0:T(8,128)(2,1)}, bf16[128,2048]{1,0:T(8,128)(2,1)}, u32[]{:S(2)}, u32[]{:S(2)}) collective-permute-start(bf16[128,2048]{1,0:T(8,128)(2,1)} %get-tuple-element.24), channel_id=1, source_target_pairs={{0,3},{1,0},{2,1},{3,2},{4,7},{5,4},{6,5},{7,6},{8,11},{9,8},{10,9... | collective-permute-start | bytes 1572872 | tf_op jit(solution)/shard_map/ppermute | solution.py:27
  16.6 14.9 %collective-permute-start.1 = (bf16[128,2048]{1,0:T(8,128)(2,1)}, bf16[128,2048]{1,0:T(8,128)(2,1)}, u32[]{:S(2)}, u32[]{:S(2)}) collective-permute-start(bf16[128,2048]{1,0:T(8,128)(2,1)} %get-tuple-element.24), channel_id=1, source_target_pairs={{0,1},{1,2},{2,3},{3,0},{4,5},{5,6},{6,7},{7,4},{8,9},{9,10},{10,1... | collective-permute-start | bytes 1572872 | tf_op jit(solution)/shard_map/ppermute | solution.py:26
  32.5 8.2 %collective-permute-start.2 = (bf16[64,2048]{1,0:T(8,128)(2,1)S(1)}, bf16[64,2048]{1,0:T(8,128)(2,1)S(1)}, u32[]{:S(2)}, u32[]{:S(2)}) collective-permute-start(bf16[64,2048]{1,0:T(8,128)(2,1)S(1)} %slice.390), channel_id=1, source_target_pairs={{0,1},{1,2},{2,3},{3,0},{4,5},{5,6},{6,7},{7,4},{8,9},{9,10},{10,1... | collective-permute-start | bytes 786440 | tf_op jit(solution)/shard_map/ppermute | solution.py:28
  50.8 231.8 %all-gather.9.cloned.1.call-start = ((), (), s32[]{:S(2)}) async-start(), calls=%async_computation.1 | async-start | bytes 4595712 | tf_op jit(solution)/shard_map/all_gather | solution.py:185
  126.7 9.7 %collective-permute-start.4 = (bf16[64,2048]{1,0:T(8,128)(2,1)S(1)}, bf16[64,2048]{1,0:T(8,128)(2,1)S(1)}, u32[]{:S(2)}, u32[]{:S(2)}) collective-permute-start(bf16[64,2048]{1,0:T(8,128)(2,1)S(1)} %get-tuple-element.61), channel_id=1, source_target_pairs={{0,1},{1,2},{2,3},{3,0},{4,5},{5,6},{6,7},{7,4},{8,9},{9,10},{10,1... | collective-permute-start | bytes 786440 | tf_op jit(solution)/shard_map/ppermute | solution.py:46
  128.3 8.2 %collective-permute-start.6 = (bf16[64,2048]{1,0:T(8,128)(2,1)S(1)}, bf16[64,2048]{1,0:T(8,128)(2,1)S(1)}, u32[]{:S(2)}, u32[]{:S(2)}) collective-permute-start(bf16[64,2048]{1,0:T(8,128)(2,1)S(1)} %get-tuple-element.62), channel_id=1, source_target_pairs={{0,3},{1,0},{2,1},{3,2},{4,7},{5,4},{6,5},{7,6},{8,11},{9,8},{10,9... | collective-permute-start | bytes 786440 | tf_op jit(solution)/shard_map/ppermute | solution.py:47
  138.6 14.6 %collective-permute-start.5 = (bf16[128,2048]{1,0:T(8,128)(2,1)}, bf16[128,2048]{1,0:T(8,128)(2,1)S(1)}, u32[]{:S(2)}, u32[]{:S(2)}) collective-permute-start(bf16[128,2048]{1,0:T(8,128)(2,1)} %pad_maximum_fusion.1), channel_id=1, source_target_pairs={{0,1},{1,2},{2,3},{3,0},{4,5},{5,6},{6,7},{7,4},{8,9},{9,10},{10,1... | collective-permute-start | bytes 1572872 | tf_op jit(solution)/shard_map/ppermute | solution.py:52
  141.0 12.9 %collective-permute-start.7 = (bf16[128,2048]{1,0:T(8,128)(2,1)}, bf16[128,2048]{1,0:T(8,128)(2,1)S(1)}, u32[]{:S(2)}, u32[]{:S(2)}) collective-permute-start(bf16[128,2048]{1,0:T(8,128)(2,1)} %pad_maximum_fusion.2), channel_id=1, source_target_pairs={{0,3},{1,0},{2,1},{3,2},{4,7},{5,4},{6,5},{7,6},{8,11},{9,8},{10,9... | collective-permute-start | bytes 1572872 | tf_op jit(solution)/shard_map/ppermute | solution.py:53
  155.8 13.4 %collective-permute-start.8 = (bf16[128,2048]{1,0:T(8,128)(2,1)S(1)}, bf16[128,2048]{1,0:T(8,128)(2,1)S(1)}, u32[]{:S(2)}, u32[]{:S(2)}) collective-permute-start(bf16[128,2048]{1,0:T(8,128)(2,1)S(1)} %multiply_convert_fusion.2), channel_id=1, source_target_pairs={{0,1},{1,2},{2,3},{3,0},{4,5},{5,6},{6,7},{7,4},{8,9},{9,10},{10,1... | collective-permute-start | bytes 1572872 | tf_op jit(solution)/shard_map/ppermute | solution.py:63
  157.1 12.2 %collective-permute-start.9 = (bf16[128,2048]{1,0:T(8,128)(2,1)S(1)}, bf16[128,2048]{1,0:T(8,128)(2,1)S(1)}, u32[]{:S(2)}, u32[]{:S(2)}) collective-permute-start(bf16[128,2048]{1,0:T(8,128)(2,1)S(1)} %multiply_convert_fusion.2), channel_id=1, source_target_pairs={{0,3},{1,0},{2,1},{3,2},{4,7},{5,4},{6,5},{7,6},{8,11},{9,8},{10,9... | collective-permute-start | bytes 1572872 | tf_op jit(solution)/shard_map/ppermute | solution.py:64
  169.2 11.6 %collective-permute-start.10 = (bf16[64,2048]{1,0:T(8,128)(2,1)S(1)}, bf16[64,2048]{1,0:T(8,128)(2,1)S(1)}, u32[]{:S(2)}, u32[]{:S(2)}) collective-permute-start(bf16[64,2048]{1,0:T(8,128)(2,1)S(1)} %slice.410), channel_id=1, source_target_pairs={{0,1},{1,2},{2,3},{3,0},{4,5},{5,6},{6,7},{7,4},{8,9},{9,10},{10,1... | collective-permute-start | bytes 786440 | tf_op jit(solution)/shard_map/ppermute | solution.py:65
  169.3 11.4 %collective-permute-start.11 = (bf16[64,2048]{1,0:T(8,128)(2,1)S(1)}, bf16[64,2048]{1,0:T(8,128)(2,1)S(1)}, u32[]{:S(2)}, u32[]{:S(2)}) collective-permute-start(bf16[64,2048]{1,0:T(8,128)(2,1)S(1)} %slice.411), channel_id=1, source_target_pairs={{0,3},{1,0},{2,1},{3,2},{4,7},{5,4},{6,5},{7,6},{8,11},{9,8},{10,9... | collective-permute-start | bytes 786440 | tf_op jit(solution)/shard_map/ppermute | solution.py:66
  184.6 7.8 %collective-permute-start.12 = (bf16[64,2048]{1,0:T(8,128)(2,1)S(1)}, bf16[64,2048]{1,0:T(8,128)(2,1)S(1)}, u32[]{:S(2)}, u32[]{:S(2)}) collective-permute-start(bf16[64,2048]{1,0:T(8,128)(2,1)S(1)} %get-tuple-element.59), channel_id=1, source_target_pairs={{0,1},{1,2},{2,3},{3,0},{4,5},{5,6},{6,7},{7,4},{8,9},{9,10},{10,1... | collective-permute-start | bytes 786440 | tf_op jit(solution)/shard_map/ppermute | solution.py:75
  184.7 7.8 %collective-permute-start.14 = (bf16[64,2048]{1,0:T(8,128)(2,1)S(1)}, bf16[64,2048]{1,0:T(8,128)(2,1)S(1)}, u32[]{:S(2)}, u32[]{:S(2)}) collective-permute-start(bf16[64,2048]{1,0:T(8,128)(2,1)S(1)} %get-tuple-element.60), channel_id=1, source_target_pairs={{0,3},{1,0},{2,1},{3,2},{4,7},{5,4},{6,5},{7,6},{8,11},{9,8},{10,9... | collective-permute-start | bytes 786440 | tf_op jit(solution)/shard_map/ppermute | solution.py:76
  192.6 10.9 %collective-permute-start.13 = (bf16[128,2048]{1,0:T(8,128)(2,1)S(1)}, bf16[128,2048]{1,0:T(8,128)(2,1)S(1)}, u32[]{:S(2)}, u32[]{:S(2)}) collective-permute-start(bf16[128,2048]{1,0:T(8,128)(2,1)S(1)} %pad_maximum_fusion.3), channel_id=1, source_target_pairs={{0,1},{1,2},{2,3},{3,0},{4,5},{5,6},{6,7},{7,4},{8,9},{9,10},{10,1... | collective-permute-start | bytes 1572872 | tf_op jit(solution)/shard_map/ppermute | solution.py:79
  192.7 10.7 %collective-permute-start.15 = (bf16[128,2048]{1,0:T(8,128)(2,1)S(1)}, bf16[128,2048]{1,0:T(8,128)(2,1)S(1)}, u32[]{:S(2)}, u32[]{:S(2)}) collective-permute-start(bf16[128,2048]{1,0:T(8,128)(2,1)S(1)} %pad_maximum_fusion.4), channel_id=1, source_target_pairs={{0,3},{1,0},{2,1},{3,2},{4,7},{5,4},{6,5},{7,6},{8,11},{9,8},{10,9... | collective-permute-start | bytes 1572872 | tf_op jit(solution)/shard_map/ppermute | solution.py:80
  205.1 12.1 %collective-permute-start.17 = (bf16[128,2048]{1,0:T(8,128)(2,1)}, bf16[128,2048]{1,0:T(8,128)(2,1)S(1)}, u32[]{:S(2)}, u32[]{:S(2)}) collective-permute-start(bf16[128,2048]{1,0:T(8,128)(2,1)} %get-tuple-element.18), channel_id=1, source_target_pairs={{0,1},{1,2},{2,3},{3,0},{4,5},{5,6},{6,7},{7,4},{8,9},{9,10},{10,1... | collective-permute-start | bytes 1572872 | tf_op jit(solution)/shard_map/ppermute | solution.py:26
  206.4 14.7 %collective-permute-start.16 = (bf16[128,2048]{1,0:T(8,128)(2,1)}, bf16[128,2048]{1,0:T(8,128)(2,1)}, u32[]{:S(2)}, u32[]{:S(2)}) collective-permute-start(bf16[128,2048]{1,0:T(8,128)(2,1)} %get-tuple-element.18), channel_id=1, source_target_pairs={{0,3},{1,0},{2,1},{3,2},{4,7},{5,4},{6,5},{7,6},{8,11},{9,8},{10,9... | collective-permute-start | bytes 1572872 | tf_op jit(solution)/shard_map/ppermute | solution.py:27
  217.9 8.4 %collective-permute-start.18 = (bf16[64,2048]{1,0:T(8,128)(2,1)}, bf16[64,2048]{1,0:T(8,128)(2,1)}, u32[]{:S(2)}, u32[]{:S(2)}) collective-permute-start(bf16[64,2048]{1,0:T(8,128)(2,1)} %slice.419), channel_id=1, source_target_pairs={{0,1},{1,2},{2,3},{3,0},{4,5},{5,6},{6,7},{7,4},{8,9},{9,10},{10,1... | collective-permute-start | bytes 786440 | tf_op jit(solution)/shard_map/ppermute | solution.py:28
  293.7 9.7 %collective-permute-start.20 = (bf16[64,2048]{1,0:T(8,128)(2,1)S(1)}, bf16[64,2048]{1,0:T(8,128)(2,1)S(1)}, u32[]{:S(2)}, u32[]{:S(2)}) collective-permute-start(bf16[64,2048]{1,0:T(8,128)(2,1)S(1)} %get-tuple-element.55), channel_id=1, source_target_pairs={{0,1},{1,2},{2,3},{3,0},{4,5},{5,6},{6,7},{7,4},{8,9},{9,10},{10,1... | collective-permute-start | bytes 786440 | tf_op jit(solution)/shard_map/ppermute | solution.py:46
  295.3 8.2 %collective-permute-start.22 = (bf16[64,2048]{1,0:T(8,128)(2,1)S(1)}, bf16[64,2048]{1,0:T(8,128)(2,1)S(1)}, u32[]{:S(2)}, u32[]{:S(2)}) collective-permute-start(bf16[64,2048]{1,0:T(8,128)(2,1)S(1)} %get-tuple-element.56), channel_id=1, source_target_pairs={{0,3},{1,0},{2,1},{3,2},{4,7},{5,4},{6,5},{7,6},{8,11},{9,8},{10,9... | collective-permute-start | bytes 786440 | tf_op jit(solution)/shard_map/ppermute | solution.py:47
  303.6 14.4 %collective-permute-start.21 = (bf16[128,2048]{1,0:T(8,128)(2,1)S(1)}, bf16[128,2048]{1,0:T(8,128)(2,1)S(1)}, u32[]{:S(2)}, u32[]{:S(2)}) collective-permute-start(bf16[128,2048]{1,0:T(8,128)(2,1)S(1)} %pad_maximum_fusion.6), channel_id=1, source_target_pairs={{0,1},{1,2},{2,3},{3,0},{4,5},{5,6},{6,7},{7,4},{8,9},{9,10},{10,1... | collective-permute-start | bytes 1572872 | tf_op jit(solution)/shard_map/ppermute | solution.py:52
  306.1 13.2 %collective-permute-start.23 = (bf16[128,2048]{1,0:T(8,128)(2,1)}, bf16[128,2048]{1,0:T(8,128)(2,1)}, u32[]{:S(2)}, u32[]{:S(2)}) collective-permute-start(bf16[128,2048]{1,0:T(8,128)(2,1)} %pad_maximum_fusion.7), channel_id=1, source_target_pairs={{0,3},{1,0},{2,1},{3,2},{4,7},{5,4},{6,5},{7,6},{8,11},{9,8},{10,9... | collective-permute-start | bytes 1572872 | tf_op jit(solution)/shard_map/ppermute | solution.py:53
  322.2 13.7 %collective-permute-start.24 = (bf16[128,2048]{1,0:T(8,128)(2,1)}, bf16[128,2048]{1,0:T(8,128)(2,1)}, u32[]{:S(2)}, u32[]{:S(2)}) collective-permute-start(bf16[128,2048]{1,0:T(8,128)(2,1)} %multiply_convert_fusion), channel_id=1, source_target_pairs={{0,1},{1,2},{2,3},{3,0},{4,5},{5,6},{6,7},{7,4},{8,9},{9,10},{10,1... | collective-permute-start | bytes 1572872 | tf_op jit(solution)/shard_map/ppermute | solution.py:63
  323.4 13.5 %collective-permute-start.25 = (bf16[128,2048]{1,0:T(8,128)(2,1)}, bf16[128,2048]{1,0:T(8,128)(2,1)}, u32[]{:S(2)}, u32[]{:S(2)}) collective-permute-start(bf16[128,2048]{1,0:T(8,128)(2,1)} %multiply_convert_fusion), channel_id=1, source_target_pairs={{0,3},{1,0},{2,1},{3,2},{4,7},{5,4},{6,5},{7,6},{8,11},{9,8},{10,9... | collective-permute-start | bytes 1572872 | tf_op jit(solution)/shard_map/ppermute | solution.py:64
  336.8 14.8 %collective-permute-start.26 = (bf16[64,2048]{1,0:T(8,128)(2,1)S(1)}, bf16[64,2048]{1,0:T(8,128)(2,1)S(1)}, u32[]{:S(2)}, u32[]{:S(2)}) collective-permute-start(bf16[64,2048]{1,0:T(8,128)(2,1)S(1)} %slice.440), channel_id=1, source_target_pairs={{0,1},{1,2},{2,3},{3,0},{4,5},{5,6},{6,7},{7,4},{8,9},{9,10},{10,1... | collective-permute-start | bytes 786440 | tf_op jit(solution)/shard_map/ppermute | solution.py:65
  337.9 13.8 %collective-permute-start.27 = (bf16[64,2048]{1,0:T(8,128)(2,1)S(1)}, bf16[64,2048]{1,0:T(8,128)(2,1)S(1)}, u32[]{:S(2)}, u32[]{:S(2)}) collective-permute-start(bf16[64,2048]{1,0:T(8,128)(2,1)S(1)} %slice.441), channel_id=1, source_target_pairs={{0,3},{1,0},{2,1},{3,2},{4,7},{5,4},{6,5},{7,6},{8,11},{9,8},{10,9... | collective-permute-start | bytes 786440 | tf_op jit(solution)/shard_map/ppermute | solution.py:66
  355.5 7.8 %collective-permute-start.28 = (bf16[64,2048]{1,0:T(8,128)(2,1)S(1)}, bf16[64,2048]{1,0:T(8,128)(2,1)S(1)}, u32[]{:S(2)}, u32[]{:S(2)}) collective-permute-start(bf16[64,2048]{1,0:T(8,128)(2,1)S(1)} %get-tuple-element.53), channel_id=1, source_target_pairs={{0,1},{1,2},{2,3},{3,0},{4,5},{5,6},{6,7},{7,4},{8,9},{9,10},{10,1... | collective-permute-start | bytes 786440 | tf_op jit(solution)/shard_map/ppermute | solution.py:75
  355.6 7.7 %collective-permute-start.30 = (bf16[64,2048]{1,0:T(8,128)(2,1)S(1)}, bf16[64,2048]{1,0:T(8,128)(2,1)S(1)}, u32[]{:S(2)}, u32[]{:S(2)}) collective-permute-start(bf16[64,2048]{1,0:T(8,128)(2,1)S(1)} %get-tuple-element.54), channel_id=1, source_target_pairs={{0,3},{1,0},{2,1},{3,2},{4,7},{5,4},{6,5},{7,6},{8,11},{9,8},{10,9... | collective-permute-start | bytes 786440 | tf_op jit(solution)/shard_map/ppermute | solution.py:76
  363.5 10.9 %collective-permute-start.29 = (bf16[128,2048]{1,0:T(8,128)(2,1)S(1)}, bf16[128,2048]{1,0:T(8,128)(2,1)S(1)}, u32[]{:S(2)}, u32[]{:S(2)}) collective-permute-start(bf16[128,2048]{1,0:T(8,128)(2,1)S(1)} %pad_maximum_fusion.8), channel_id=1, source_target_pairs={{0,1},{1,2},{2,3},{3,0},{4,5},{5,6},{6,7},{7,4},{8,9},{9,10},{10,1... | collective-permute-start | bytes 1572872 | tf_op jit(solution)/shard_map/ppermute | solution.py:79
  363.7 10.8 %collective-permute-start.31 = (bf16[128,2048]{1,0:T(8,128)(2,1)S(1)}, bf16[128,2048]{1,0:T(8,128)(2,1)S(1)}, u32[]{:S(2)}, u32[]{:S(2)}) collective-permute-start(bf16[128,2048]{1,0:T(8,128)(2,1)S(1)} %pad_maximum_fusion.9), channel_id=1, source_target_pairs={{0,3},{1,0},{2,1},{3,2},{4,7},{5,4},{6,5},{7,6},{8,11},{9,8},{10,9... | collective-permute-start | bytes 1572872 | tf_op jit(solution)/shard_map/ppermute | solution.py:80
  (48 other events, 644.4 us)
Sparse Core Ops, SparseCore 0:
  50.9 48.1 all-gather.6
  236.6 45.8 all-gather.8

commit v6 on v5

--- a/solution.py
+++ b/solution.py
@@ -144,6 +144,10 @@
         down_weight = w_down[layer]
         normed = rms_norm(stream, attn_gain[layer])
         project_piece = ring_gather(normed, "head")
+        if layer == 0:
+            project_piece, gate_up_slices = lax.optimization_barrier(
+                (project_piece, [w_gate_up[index] for index in range(DEPTH_NUMBER)])
+            )
         projected = jnp.concatenate(
             [
                 jnp.dot(project_piece, query_weight, preferred_element_type=jnp.float32),
@@ -183,10 +187,6 @@
             [written[0].astype(jnp.bfloat16), rate_high, rate_mid, rate_low], axis=0
         )
         gathered = lax.all_gather(payload, "seg")
-        if layer == 0:
-            gathered, gate_up_slices = lax.optimization_barrier(
-                (gathered, [w_gate_up[index] for index in range(DEPTH_NUMBER)])
-            )
         written_all = gathered[:, :MEM].astype(jnp.float32)
         rate_parts = gathered[:, MEM:, ::HD].astype(jnp.float32)
         rate_all = rate_parts[:, 0] + rate_parts[:, 1] + rate_parts[:, 2]

time: 389 us -> 391 us (level)
  waiting for transfers between devices: 125 us -> 144 us
  local copies, waits for them, and re-layouts: 78.3 us -> 62.9 us
  starting transfers between devices: 55.3 us -> 50.7 us
    ppermute x2, waiting for transfers between devices: 17.1 us -> 0.01 us  [ring_pieces(): from_before = lax.ppermute(piece, axis, ahead)]
    ppermute x2, waiting for transfers between devices: 1.11 us -> 18.2 us  [ring_scatter(): got_after = lax.ppermute(prev_part.astype(jnp.bfloat16), axis, behind)]
    ppermute x2, waiting for transfers between devices: 0.01 us -> 16.6 us  [ring_pieces(): from_after = lax.ppermute(piece, axis, behind)]
    optimization_barrier x1 -> x0, local copies, waits for them, and re-layouts: 15.7 us -> none  [body(): lax.optimization_barrier((gathered, [w_gate_up[index] for index in range(...]
    all_gather x2, waiting for transfers between devices: 38.1 us -> 51.5 us  [body(): gathered = lax.all_gather(payload, 'seg')]
    ppermute x2, waiting for transfers between devices: 19.8 us -> 8.57 us  [ring_scatter(): got_before = lax.ppermute(next_part.astype(jnp.bfloat16), axis, ahead)]
    ppermute x2, waiting for transfers between devices: 19.8 us -> 10 us  [ring_gather(): from_before = lax.ppermute(piece, axis, ahead)]
    ppermute x2, waiting for transfers between devices: 5.89 us -> 10.1 us  [ring_scatter_parts(): got_before = lax.ppermute(next_part.astype(jnp.bfloat16), axis, ahead)]
  transfers between devices with their start and end apart: 34 -> 34, of which waited for: 21 -> 24; matrix products, arithmetic and copies ran while one was open for 28% -> 29% of each run, Pallas kernels for 0% -> 0%
where the time goes in v6:
time: 391 us; the launch traced here: 384 us
  waiting for transfers between devices  144 us (37%)
  matrix products  68.1 us (17%)
  local copies, waits for them, and re-layouts  62.9 us (16%)
  starting transfers between devices  50.7 us (13%)
  other arithmetic  42.6 us (11%)
  between operations  15.8 us (4%)
    all_gather x2, waiting for transfers between devices, body(): gathered = lax.all_gather(payload, 'seg')  51.5 us
    dot_general x6, matrix products, feed_forward(): jnp.einsum('rd,dtf->rtf', rows, widening_matrix, preferred_element_type=j...  26.4 us
    ppermute x2, waiting for transfers between devices, ring_scatter(): got_after = lax.ppermute(prev_part.astype(jnp.bfloat16), axis, behind)  18.2 us
    ppermute x2, waiting for transfers between devices, ring_pieces(): from_after = lax.ppermute(piece, axis, behind)  16.6 us
    squeeze x1, local copies, waits for them, and re-layouts, body(): w_gate_up[index]  14.2 us
    ppermute x2, waiting for transfers between devices, ring_scatter(): sent_top = lax.ppermute(far[:half].astype(jnp.bfloat16), axis, ahead)  11.5 us
    dot_general x3, local copies, waits for them, and re-layouts, body(): jnp.dot(project_piece, query_weight, preferred_element_type=jnp.float32)  10.5 us
    ppermute x2, waiting for transfers between devices, ring_scatter_parts(): got_before = lax.ppermute(next_part.astype(jnp.bfloat16), axis, ahead)  10.1 us
  transfers between devices with their start and end apart: 34, of which 24 were waited for; matrix products, arithmetic and copies ran while one was open for 29% of the time, Pallas kernels for 0%

profile of v6, /device:TPU:0, one launch (start us, length us, event | category | flops | bytes accessed | tf_op | source)
XLA Modules:
  0.0 383.9 jit_solution(3296475473165009302)
XLA Ops:
  12.2 4.1 %collective-permute-start = (bf16[128,2048]{1,0:T(8,128)(2,1)}, bf16[128,2048]{1,0:T(8,128)(2,1)}, u32[]{:S(2)}, u32[]{:S(2)}) collective-permute-start(bf16[128,2048]{1,0:T(8,128)(2,1)} %get-tuple-element.24), channel_id=1, source_target_pairs={{0,3},{1,0},{2,1},{3,2},{4,7},{5,4},{6,5},{7,6},{8,11},{9,8},{10,9... | collective-permute-start | bytes 1572872 | tf_op jit(solution)/shard_map/ppermute | solution.py:27
  16.4 14.2 %slice_bitcast_fusion = (bf16[2048,2,1024]{2,1,0:T(2,128)(2,1)}, bf16[2048,2,1024]{2,1,0:T(2,128)(2,1)}) fusion(bf16[2,2048,2,1024]{3,2,1,0:T(2,128)(2,1)} %param.26), kind=kLoop, calls=%fused_computation.10 | loop fusion | bytes 33554432 | tf_op jit(solution)/shard_map/squeeze | solution.py:149
  40.2 3.3 collective-permute-start.3
  55.9 3.9 %slice_bitcast_fusion.2 = (bf16[512,2048]{0,1:T(8,128)(2,1)}, bf16[512,2048]{0,1:T(8,128)(2,1)S(1)}) fusion(bf16[2,2048,512]{2,1,0:T(8,128)(2,1)} %param.23), kind=kLoop, calls=%fused_computation.75 | loop fusion | bytes 8388608 | tf_op jit(solution)/shard_map/dot_general | solution.py:153
  63.7 3.5 fusion.57
  70.9 4.6 %divide_convert_fusion.1 = bf16[2,4,512,640]{2,3,1,0:T(8,128)(2,1)} fusion(f32[2,4,512,512]{2,3,1,0:T(8,128)S(1)} %get-tuple-element.88, f32[2,4,512,128]{2,3,1,0:T(8,128)} %copy-done.1, f32[2,4,512]{2,1,0:T(4,128)S(1)} %fusion.3, f32[2,4,512]{2,1,0:T(4,128)S(1)} %reduce_max.61), kind=kLoop, calls=%fused_computation.5 | loop fusion | flops 10485760 | bytes 15761408 | tf_op jit(solution)/shard_map/convert_element_type | solution.py:225
  78.5 25.4 %all-gather.7.cloned.1.call-done = bf16[32,131,512]{2,1,0:T(8,128)(2,1)} async-done(((bf16[1,131,512]{2,1,0:T(8,128)(2,1)}), bf16[32,131,512]{2,1,0:T(8,128)(2,1)}) %all-gather.7.cloned.1.call-update) | async-done | bytes 4292624 | tf_op jit(solution)/shard_map/all_gather | solution.py:189
  120.8 5.1 %collective-permute-done.4 = bf16[64,2048]{1,0:T(8,128)(2,1)S(1)} collective-permute-done((bf16[64,2048]{1,0:T(8,128)(2,1)S(1)}, bf16[64,2048]{1,0:T(8,128)(2,1)S(1)}, u32[]{:S(2)}, u32[]{:S(2)}) %collective-permute-start.4) | collective-permute-done | bytes 262176 | tf_op jit(solution)/shard_map/ppermute | solution.py:46
  133.0 8.9 %collective-permute-done.7 = bf16[128,2048]{1,0:T(8,128)(2,1)S(1)} collective-permute-done((bf16[128,2048]{1,0:T(8,128)(2,1)}, bf16[128,2048]{1,0:T(8,128)(2,1)S(1)}, u32[]{:S(2)}, u32[]{:S(2)}) %collective-permute-start.7) | collective-permute-done | bytes 524320 | tf_op jit(solution)/shard_map/ppermute | solution.py:53
  141.9 4.6 %collective-permute-done.5 = bf16[128,2048]{1,0:T(8,128)(2,1)S(1)} collective-permute-done((bf16[128,2048]{1,0:T(8,128)(2,1)}, bf16[128,2048]{1,0:T(8,128)(2,1)S(1)}, u32[]{:S(2)}, u32[]{:S(2)}) %collective-permute-start.5) | collective-permute-done | bytes 524320 | tf_op jit(solution)/shard_map/ppermute | solution.py:52
  150.5 10.0 %collective-permute-done.9 = bf16[128,2048]{1,0:T(8,128)(2,1)S(1)} collective-permute-done((bf16[128,2048]{1,0:T(8,128)(2,1)S(1)}, bf16[128,2048]{1,0:T(8,128)(2,1)S(1)}, u32[]{:S(2)}, u32[]{:S(2)}) %collective-permute-start.9) | collective-permute-done | bytes 524320 | tf_op jit(solution)/shard_map/ppermute | solution.py:64
  162.7 6.6 %fusion.12 = f32[256,2,1024]{2,0,1:T(8,128)S(1)} fusion(bf16[2048,2,1024]{2,1,0:T(2,128)(2,1)} %get-tuple-element.7, bf16[128,2048]{1,0:T(8,128)(2,1)S(1)} %collective-permute-done.9, bf16[128,2048]{1,0:T(8,128)(2,1)S(1)} %collective-permute-done.8), kind=kOutput, calls=%fused_computation.22 | convolution fusion | flops 2149580800 | bytes 11534336 | tf_op jit(solution)/shard_map/rd,dtf->rtf/dot_general | solution.py:85
  177.9 4.3 %collective-permute-done.12 = bf16[64,2048]{1,0:T(8,128)(2,1)S(1)} collective-permute-done((bf16[64,2048]{1,0:T(8,128)(2,1)S(1)}, bf16[64,2048]{1,0:T(8,128)(2,1)S(1)}, u32[]{:S(2)}, u32[]{:S(2)}) %collective-permute-start.12) | collective-permute-done | bytes 262176 | tf_op jit(solution)/shard_map/ppermute | solution.py:75
  183.0 3.8 collective-permute-start.15
  193.5 6.0 %collective-permute-done.13 = bf16[128,2048]{1,0:T(8,128)(2,1)S(1)} collective-permute-done((bf16[128,2048]{1,0:T(8,128)(2,1)S(1)}, bf16[128,2048]{1,0:T(8,128)(2,1)S(1)}, u32[]{:S(2)}, u32[]{:S(2)}) %collective-permute-start.13) | collective-permute-done | bytes 524320 | tf_op jit(solution)/shard_map/ppermute | solution.py:79
  201.1 3.2 collective-permute-start.16
  204.5 10.0 %collective-permute-done.17 = bf16[128,2048]{1,0:T(8,128)(2,1)S(1)} collective-permute-done((bf16[128,2048]{1,0:T(8,128)(2,1)}, bf16[128,2048]{1,0:T(8,128)(2,1)S(1)}, u32[]{:S(2)}, u32[]{:S(2)}) %collective-permute-start.17) | collective-permute-done | bytes 524320 | tf_op jit(solution)/shard_map/ppermute | solution.py:26
  218.3 3.3 collective-permute-start.19
  233.2 4.2 %copy.161 = bf16[512,2048]{1,0:T(8,128)(2,1)} copy(bf16[512,2048]{0,1:T(8,128)(2,1)} %get-tuple-element.31) | data formatting | bytes 4194304 | tf_op jit(solution)/shard_map/dot_general | solution.py:153
  238.2 3.7 fusion.52
  245.7 4.6 %divide_convert_fusion = bf16[2,4,512,640]{2,3,1,0:T(8,128)(2,1)} fusion(f32[2,4,512,512]{2,3,1,0:T(8,128)S(1)} %get-tuple-element.98, f32[2,4,512,128]{2,3,1,0:T(8,128)} %copy-done, f32[2,4,512]{2,1,0:T(4,128)S(1)} %fusion.2, f32[2,4,512]{2,1,0:T(4,128)S(1)} %reduce_max.65), kind=kLoop, calls=%fused_computation.4 | loop fusion | flops 10485760 | bytes 15761408 | tf_op jit(solution)/shard_map/convert_element_type | solution.py:225
  253.5 26.1 %all-gather.9.cloned.1.call-done = bf16[32,131,512]{2,1,0:T(8,128)(2,1)} async-done(((bf16[1,131,512]{2,1,0:T(8,128)(2,1)}), bf16[32,131,512]{2,1,0:T(8,128)(2,1)}) %all-gather.9.cloned.1.call-update) | async-done | bytes 4292624 | tf_op jit(solution)/shard_map/all_gather | solution.py:189
  294.0 6.3 %collective-permute-done.20 = bf16[64,2048]{1,0:T(8,128)(2,1)S(1)} collective-permute-done((bf16[64,2048]{1,0:T(8,128)(2,1)S(1)}, bf16[64,2048]{1,0:T(8,128)(2,1)S(1)}, u32[]{:S(2)}, u32[]{:S(2)}) %collective-permute-start.20) | collective-permute-done | bytes 262176 | tf_op jit(solution)/shard_map/ppermute | solution.py:46
  304.9 9.3 %collective-permute-done.23 = bf16[128,2048]{1,0:T(8,128)(2,1)S(1)} collective-permute-done((bf16[128,2048]{1,0:T(8,128)(2,1)S(1)}, bf16[128,2048]{1,0:T(8,128)(2,1)S(1)}, u32[]{:S(2)}, u32[]{:S(2)}) %collective-permute-start.23) | collective-permute-done | bytes 524320 | tf_op jit(solution)/shard_map/ppermute | solution.py:53
  314.9 4.0 %collective-permute-done.21 = bf16[128,2048]{1,0:T(8,128)(2,1)} collective-permute-done((bf16[128,2048]{1,0:T(8,128)(2,1)}, bf16[128,2048]{1,0:T(8,128)(2,1)}, u32[]{:S(2)}, u32[]{:S(2)}) %collective-permute-start.21) | collective-permute-done | bytes 524320 | tf_op jit(solution)/shard_map/ppermute | solution.py:52
  327.4 6.6 %collective-permute-done.25 = bf16[128,2048]{1,0:T(8,128)(2,1)} collective-permute-done((bf16[128,2048]{1,0:T(8,128)(2,1)}, bf16[128,2048]{1,0:T(8,128)(2,1)}, u32[]{:S(2)}, u32[]{:S(2)}) %collective-permute-start.25) | collective-permute-done | bytes 524320 | tf_op jit(solution)/shard_map/ppermute | solution.py:64
  338.1 6.9 %fusion.6 = f32[256,2,1024]{2,0,1:T(8,128)S(1)} fusion(bf16[2048,2,1024]{2,1,0:T(2,128)(2,1)} %get-tuple-element.8, bf16[128,2048]{1,0:T(8,128)(2,1)} %collective-permute-done.25, bf16[128,2048]{1,0:T(8,128)(2,1)} %collective-permute-done.24), kind=kOutput, calls=%fused_computation.16 | convolution fusion | flops 2149580800 | bytes 11534336 | tf_op jit(solution)/shard_map/rd,dtf->rtf/dot_general | solution.py:85
  345.0 3.7 fusion.181
  355.9 4.3 %collective-permute-done.28 = bf16[64,2048]{1,0:T(8,128)(2,1)S(1)} collective-permute-done((bf16[64,2048]{1,0:T(8,128)(2,1)S(1)}, bf16[64,2048]{1,0:T(8,128)(2,1)S(1)}, u32[]{:S(2)}, u32[]{:S(2)}) %collective-permute-start.28) | collective-permute-done | bytes 262176 | tf_op jit(solution)/shard_map/ppermute | solution.py:75
  360.8 3.8 collective-permute-start.31
  365.0 4.0 %fusion.8 = f32[128,2,1024]{2,0,1:T(8,128)S(1)} fusion(bf16[2048,2,1024]{2,1,0:T(2,128)(2,1)S(1)} %bitcast.299, bf16[128,2048]{1,0:T(8,128)(2,1)} %multiply_convert_fusion), kind=kOutput, calls=%fused_computation.18 | convolution fusion | flops 1073741824 | bytes 9961472 | tf_op jit(solution)/shard_map/rd,dtf->rtf/dot_general | solution.py:85
  371.2 4.1 %collective-permute-done.29 = bf16[128,2048]{1,0:T(8,128)(2,1)S(1)} collective-permute-done((bf16[128,2048]{1,0:T(8,128)(2,1)S(1)}, bf16[128,2048]{1,0:T(8,128)(2,1)S(1)}, u32[]{:S(2)}, u32[]{:S(2)}) %collective-permute-start.29) | collective-permute-done | bytes 524320 | tf_op jit(solution)/shard_map/ppermute | solution.py:79
  (300 shorter events, 151.5 us)
Async XLA Ops:
  7.2 96.8 %all-gather.7.cloned.1.call-start = ((), (), s32[]{:S(2)}) async-start(), calls=%async_computation | async-start | bytes 4595712 | tf_op jit(solution)/shard_map/all_gather | solution.py:189
  12.2 27.0 %collective-permute-start = (bf16[128,2048]{1,0:T(8,128)(2,1)}, bf16[128,2048]{1,0:T(8,128)(2,1)}, u32[]{:S(2)}, u32[]{:S(2)}) collective-permute-start(bf16[128,2048]{1,0:T(8,128)(2,1)} %get-tuple-element.24), channel_id=1, source_target_pairs={{0,3},{1,0},{2,1},{3,2},{4,7},{5,4},{6,5},{7,6},{8,11},{9,8},{10,9... | collective-permute-start | bytes 1572872 | tf_op jit(solution)/shard_map/ppermute | solution.py:27
  16.3 18.1 %collective-permute-start.1 = (bf16[128,2048]{1,0:T(8,128)(2,1)}, bf16[128,2048]{1,0:T(8,128)(2,1)}, u32[]{:S(2)}, u32[]{:S(2)}) collective-permute-start(bf16[128,2048]{1,0:T(8,128)(2,1)} %get-tuple-element.24), channel_id=1, source_target_pairs={{0,1},{1,2},{2,3},{3,0},{4,5},{5,6},{6,7},{7,4},{8,9},{9,10},{10,1... | collective-permute-start | bytes 1572872 | tf_op jit(solution)/shard_map/ppermute | solution.py:26
  36.1 9.3 %collective-permute-start.2 = (bf16[64,2048]{1,0:T(8,128)(2,1)}, bf16[64,2048]{1,0:T(8,128)(2,1)}, u32[]{:S(2)}, u32[]{:S(2)}) collective-permute-start(bf16[64,2048]{1,0:T(8,128)(2,1)} %slice.390), channel_id=1, source_target_pairs={{0,1},{1,2},{2,3},{3,0},{4,5},{5,6},{6,7},{7,4},{8,9},{9,10},{10,1... | collective-permute-start | bytes 786440 | tf_op jit(solution)/shard_map/ppermute | solution.py:28
  40.2 8.3 %collective-permute-start.3 = (bf16[64,2048]{1,0:T(8,128)(2,1)S(1)}, bf16[64,2048]{1,0:T(8,128)(2,1)S(1)}, u32[]{:S(2)}, u32[]{:S(2)}) collective-permute-start(bf16[64,2048]{1,0:T(8,128)(2,1)S(1)} %slice.391), channel_id=1, source_target_pairs={{0,3},{1,0},{2,1},{3,2},{4,7},{5,4},{6,5},{7,6},{8,11},{9,8},{10,9... | collective-permute-start | bytes 786440 | tf_op jit(solution)/shard_map/ppermute | solution.py:29
  55.6 224.0 %all-gather.9.cloned.1.call-start = ((), (), s32[]{:S(2)}) async-start(), calls=%async_computation.1 | async-start | bytes 4595712 | tf_op jit(solution)/shard_map/all_gather | solution.py:189
  116.2 9.7 %collective-permute-start.4 = (bf16[64,2048]{1,0:T(8,128)(2,1)S(1)}, bf16[64,2048]{1,0:T(8,128)(2,1)S(1)}, u32[]{:S(2)}, u32[]{:S(2)}) collective-permute-start(bf16[64,2048]{1,0:T(8,128)(2,1)S(1)} %get-tuple-element.61), channel_id=1, source_target_pairs={{0,1},{1,2},{2,3},{3,0},{4,5},{5,6},{6,7},{7,4},{8,9},{9,10},{10,1... | collective-permute-start | bytes 786440 | tf_op jit(solution)/shard_map/ppermute | solution.py:46
  117.9 8.2 %collective-permute-start.6 = (bf16[64,2048]{1,0:T(8,128)(2,1)S(1)}, bf16[64,2048]{1,0:T(8,128)(2,1)S(1)}, u32[]{:S(2)}, u32[]{:S(2)}) collective-permute-start(bf16[64,2048]{1,0:T(8,128)(2,1)S(1)} %get-tuple-element.62), channel_id=1, source_target_pairs={{0,3},{1,0},{2,1},{3,2},{4,7},{5,4},{6,5},{7,6},{8,11},{9,8},{10,9... | collective-permute-start | bytes 786440 | tf_op jit(solution)/shard_map/ppermute | solution.py:47
  128.2 13.8 %collective-permute-start.7 = (bf16[128,2048]{1,0:T(8,128)(2,1)}, bf16[128,2048]{1,0:T(8,128)(2,1)S(1)}, u32[]{:S(2)}, u32[]{:S(2)}) collective-permute-start(bf16[128,2048]{1,0:T(8,128)(2,1)} %pad_maximum_fusion.2), channel_id=1, source_target_pairs={{0,3},{1,0},{2,1},{3,2},{4,7},{5,4},{6,5},{7,6},{8,11},{9,8},{10,9... | collective-permute-start | bytes 1572872 | tf_op jit(solution)/shard_map/ppermute | solution.py:53
  132.0 14.5 %collective-permute-start.5 = (bf16[128,2048]{1,0:T(8,128)(2,1)}, bf16[128,2048]{1,0:T(8,128)(2,1)S(1)}, u32[]{:S(2)}, u32[]{:S(2)}) collective-permute-start(bf16[128,2048]{1,0:T(8,128)(2,1)} %pad_maximum_fusion.1), channel_id=1, source_target_pairs={{0,1},{1,2},{2,3},{3,0},{4,5},{5,6},{6,7},{7,4},{8,9},{9,10},{10,1... | collective-permute-start | bytes 1572872 | tf_op jit(solution)/shard_map/ppermute | solution.py:52
  148.4 12.1 %collective-permute-start.9 = (bf16[128,2048]{1,0:T(8,128)(2,1)S(1)}, bf16[128,2048]{1,0:T(8,128)(2,1)S(1)}, u32[]{:S(2)}, u32[]{:S(2)}) collective-permute-start(bf16[128,2048]{1,0:T(8,128)(2,1)S(1)} %multiply_convert_fusion.2), channel_id=1, source_target_pairs={{0,3},{1,0},{2,1},{3,2},{4,7},{5,4},{6,5},{7,6},{8,11},{9,8},{10,9... | collective-permute-start | bytes 1572872 | tf_op jit(solution)/shard_map/ppermute | solution.py:64
  148.5 13.4 %collective-permute-start.8 = (bf16[128,2048]{1,0:T(8,128)(2,1)S(1)}, bf16[128,2048]{1,0:T(8,128)(2,1)S(1)}, u32[]{:S(2)}, u32[]{:S(2)}) collective-permute-start(bf16[128,2048]{1,0:T(8,128)(2,1)S(1)} %multiply_convert_fusion.2), channel_id=1, source_target_pairs={{0,1},{1,2},{2,3},{3,0},{4,5},{5,6},{6,7},{7,4},{8,9},{9,10},{10,1... | collective-permute-start | bytes 1572872 | tf_op jit(solution)/shard_map/ppermute | solution.py:63
  160.5 10.3 %collective-permute-start.11 = (bf16[64,2048]{1,0:T(8,128)(2,1)S(1)}, bf16[64,2048]{1,0:T(8,128)(2,1)S(1)}, u32[]{:S(2)}, u32[]{:S(2)}) collective-permute-start(bf16[64,2048]{1,0:T(8,128)(2,1)S(1)} %slice.412), channel_id=1, source_target_pairs={{0,3},{1,0},{2,1},{3,2},{4,7},{5,4},{6,5},{7,6},{8,11},{9,8},{10,9... | collective-permute-start | bytes 786440 | tf_op jit(solution)/shard_map/ppermute | solution.py:66
  162.0 8.8 %collective-permute-start.10 = (bf16[64,2048]{1,0:T(8,128)(2,1)S(1)}, bf16[64,2048]{1,0:T(8,128)(2,1)S(1)}, u32[]{:S(2)}, u32[]{:S(2)}) collective-permute-start(bf16[64,2048]{1,0:T(8,128)(2,1)S(1)} %slice.411), channel_id=1, source_target_pairs={{0,1},{1,2},{2,3},{3,0},{4,5},{5,6},{6,7},{7,4},{8,9},{9,10},{10,1... | collective-permute-start | bytes 786440 | tf_op jit(solution)/shard_map/ppermute | solution.py:65
  174.6 7.7 %collective-permute-start.12 = (bf16[64,2048]{1,0:T(8,128)(2,1)S(1)}, bf16[64,2048]{1,0:T(8,128)(2,1)S(1)}, u32[]{:S(2)}, u32[]{:S(2)}) collective-permute-start(bf16[64,2048]{1,0:T(8,128)(2,1)S(1)} %get-tuple-element.59), channel_id=1, source_target_pairs={{0,1},{1,2},{2,3},{3,0},{4,5},{5,6},{6,7},{7,4},{8,9},{9,10},{10,1... | collective-permute-start | bytes 786440 | tf_op jit(solution)/shard_map/ppermute | solution.py:75
  174.7 8.2 %collective-permute-start.14 = (bf16[64,2048]{1,0:T(8,128)(2,1)S(1)}, bf16[64,2048]{1,0:T(8,128)(2,1)S(1)}, u32[]{:S(2)}, u32[]{:S(2)}) collective-permute-start(bf16[64,2048]{1,0:T(8,128)(2,1)S(1)} %get-tuple-element.60), channel_id=1, source_target_pairs={{0,3},{1,0},{2,1},{3,2},{4,7},{5,4},{6,5},{7,6},{8,11},{9,8},{10,9... | collective-permute-start | bytes 786440 | tf_op jit(solution)/shard_map/ppermute | solution.py:76
  183.0 10.5 %collective-permute-start.15 = (bf16[128,2048]{1,0:T(8,128)(2,1)S(1)}, bf16[128,2048]{1,0:T(8,128)(2,1)S(1)}, u32[]{:S(2)}, u32[]{:S(2)}) collective-permute-start(bf16[128,2048]{1,0:T(8,128)(2,1)S(1)} %pad_maximum_fusion.4), channel_id=1, source_target_pairs={{0,3},{1,0},{2,1},{3,2},{4,7},{5,4},{6,5},{7,6},{8,11},{9,8},{10,9... | collective-permute-start | bytes 1572872 | tf_op jit(solution)/shard_map/ppermute | solution.py:80
  186.9 12.7 %collective-permute-start.13 = (bf16[128,2048]{1,0:T(8,128)(2,1)S(1)}, bf16[128,2048]{1,0:T(8,128)(2,1)S(1)}, u32[]{:S(2)}, u32[]{:S(2)}) collective-permute-start(bf16[128,2048]{1,0:T(8,128)(2,1)S(1)} %pad_maximum_fusion.3), channel_id=1, source_target_pairs={{0,1},{1,2},{2,3},{3,0},{4,5},{5,6},{6,7},{7,4},{8,9},{9,10},{10,1... | collective-permute-start | bytes 1572872 | tf_op jit(solution)/shard_map/ppermute | solution.py:79
  201.1 13.4 %collective-permute-start.17 = (bf16[128,2048]{1,0:T(8,128)(2,1)}, bf16[128,2048]{1,0:T(8,128)(2,1)S(1)}, u32[]{:S(2)}, u32[]{:S(2)}) collective-permute-start(bf16[128,2048]{1,0:T(8,128)(2,1)} %get-tuple-element.18), channel_id=1, source_target_pairs={{0,1},{1,2},{2,3},{3,0},{4,5},{5,6},{6,7},{7,4},{8,9},{9,10},{10,1... | collective-permute-start | bytes 1572872 | tf_op jit(solution)/shard_map/ppermute | solution.py:26
  201.1 16.2 %collective-permute-start.16 = (bf16[128,2048]{1,0:T(8,128)(2,1)}, bf16[128,2048]{1,0:T(8,128)(2,1)}, u32[]{:S(2)}, u32[]{:S(2)}) collective-permute-start(bf16[128,2048]{1,0:T(8,128)(2,1)} %get-tuple-element.18), channel_id=1, source_target_pairs={{0,3},{1,0},{2,1},{3,2},{4,7},{5,4},{6,5},{7,6},{8,11},{9,8},{10,9... | collective-permute-start | bytes 1572872 | tf_op jit(solution)/shard_map/ppermute | solution.py:27
  215.3 8.2 %collective-permute-start.18 = (bf16[64,2048]{1,0:T(8,128)(2,1)}, bf16[64,2048]{1,0:T(8,128)(2,1)}, u32[]{:S(2)}, u32[]{:S(2)}) collective-permute-start(bf16[64,2048]{1,0:T(8,128)(2,1)} %slice.420), channel_id=1, source_target_pairs={{0,1},{1,2},{2,3},{3,0},{4,5},{5,6},{6,7},{7,4},{8,9},{9,10},{10,1... | collective-permute-start | bytes 786440 | tf_op jit(solution)/shard_map/ppermute | solution.py:28
  290.6 9.7 %collective-permute-start.20 = (bf16[64,2048]{1,0:T(8,128)(2,1)S(1)}, bf16[64,2048]{1,0:T(8,128)(2,1)S(1)}, u32[]{:S(2)}, u32[]{:S(2)}) collective-permute-start(bf16[64,2048]{1,0:T(8,128)(2,1)S(1)} %get-tuple-element.55), channel_id=1, source_target_pairs={{0,1},{1,2},{2,3},{3,0},{4,5},{5,6},{6,7},{7,4},{8,9},{9,10},{10,1... | collective-permute-start | bytes 786440 | tf_op jit(solution)/shard_map/ppermute | solution.py:46
  292.2 8.2 %collective-permute-start.22 = (bf16[64,2048]{1,0:T(8,128)(2,1)S(1)}, bf16[64,2048]{1,0:T(8,128)(2,1)S(1)}, u32[]{:S(2)}, u32[]{:S(2)}) collective-permute-start(bf16[64,2048]{1,0:T(8,128)(2,1)S(1)} %get-tuple-element.56), channel_id=1, source_target_pairs={{0,3},{1,0},{2,1},{3,2},{4,7},{5,4},{6,5},{7,6},{8,11},{9,8},{10,9... | collective-permute-start | bytes 786440 | tf_op jit(solution)/shard_map/ppermute | solution.py:47
  300.6 13.5 %collective-permute-start.23 = (bf16[128,2048]{1,0:T(8,128)(2,1)S(1)}, bf16[128,2048]{1,0:T(8,128)(2,1)S(1)}, u32[]{:S(2)}, u32[]{:S(2)}) collective-permute-start(bf16[128,2048]{1,0:T(8,128)(2,1)S(1)} %pad_maximum_fusion.7), channel_id=1, source_target_pairs={{0,3},{1,0},{2,1},{3,2},{4,7},{5,4},{6,5},{7,6},{8,11},{9,8},{10,9... | collective-permute-start | bytes 1572872 | tf_op jit(solution)/shard_map/ppermute | solution.py:53
  304.5 14.5 %collective-permute-start.21 = (bf16[128,2048]{1,0:T(8,128)(2,1)}, bf16[128,2048]{1,0:T(8,128)(2,1)}, u32[]{:S(2)}, u32[]{:S(2)}) collective-permute-start(bf16[128,2048]{1,0:T(8,128)(2,1)} %pad_maximum_fusion.6), channel_id=1, source_target_pairs={{0,1},{1,2},{2,3},{3,0},{4,5},{5,6},{6,7},{7,4},{8,9},{9,10},{10,1... | collective-permute-start | bytes 1572872 | tf_op jit(solution)/shard_map/ppermute | solution.py:52
  321.8 12.2 %collective-permute-start.25 = (bf16[128,2048]{1,0:T(8,128)(2,1)}, bf16[128,2048]{1,0:T(8,128)(2,1)}, u32[]{:S(2)}, u32[]{:S(2)}) collective-permute-start(bf16[128,2048]{1,0:T(8,128)(2,1)} %multiply_convert_fusion), channel_id=1, source_target_pairs={{0,3},{1,0},{2,1},{3,2},{4,7},{5,4},{6,5},{7,6},{8,11},{9,8},{10,9... | collective-permute-start | bytes 1572872 | tf_op jit(solution)/shard_map/ppermute | solution.py:64
  321.8 14.7 %collective-permute-start.24 = (bf16[128,2048]{1,0:T(8,128)(2,1)}, bf16[128,2048]{1,0:T(8,128)(2,1)}, u32[]{:S(2)}, u32[]{:S(2)}) collective-permute-start(bf16[128,2048]{1,0:T(8,128)(2,1)} %multiply_convert_fusion), channel_id=1, source_target_pairs={{0,1},{1,2},{2,3},{3,0},{4,5},{5,6},{6,7},{7,4},{8,9},{9,10},{10,1... | collective-permute-start | bytes 1572872 | tf_op jit(solution)/shard_map/ppermute | solution.py:63
  335.0 13.8 %collective-permute-start.27 = (bf16[64,2048]{1,0:T(8,128)(2,1)S(1)}, bf16[64,2048]{1,0:T(8,128)(2,1)S(1)}, u32[]{:S(2)}, u32[]{:S(2)}) collective-permute-start(bf16[64,2048]{1,0:T(8,128)(2,1)S(1)} %slice.442), channel_id=1, source_target_pairs={{0,3},{1,0},{2,1},{3,2},{4,7},{5,4},{6,5},{7,6},{8,11},{9,8},{10,9... | collective-permute-start | bytes 786440 | tf_op jit(solution)/shard_map/ppermute | solution.py:66
  337.5 11.2 %collective-permute-start.26 = (bf16[64,2048]{1,0:T(8,128)(2,1)S(1)}, bf16[64,2048]{1,0:T(8,128)(2,1)S(1)}, u32[]{:S(2)}, u32[]{:S(2)}) collective-permute-start(bf16[64,2048]{1,0:T(8,128)(2,1)S(1)} %slice.441), channel_id=1, source_target_pairs={{0,1},{1,2},{2,3},{3,0},{4,5},{5,6},{6,7},{7,4},{8,9},{9,10},{10,1... | collective-permute-start | bytes 786440 | tf_op jit(solution)/shard_map/ppermute | solution.py:65
  352.7 7.9 %collective-permute-start.30 = (bf16[64,2048]{1,0:T(8,128)(2,1)S(1)}, bf16[64,2048]{1,0:T(8,128)(2,1)S(1)}, u32[]{:S(2)}, u32[]{:S(2)}) collective-permute-start(bf16[64,2048]{1,0:T(8,128)(2,1)S(1)} %get-tuple-element.54), channel_id=1, source_target_pairs={{0,3},{1,0},{2,1},{3,2},{4,7},{5,4},{6,5},{7,6},{8,11},{9,8},{10,9... | collective-permute-start | bytes 786440 | tf_op jit(solution)/shard_map/ppermute | solution.py:76
  360.8 10.5 %collective-permute-start.31 = (bf16[128,2048]{1,0:T(8,128)(2,1)S(1)}, bf16[128,2048]{1,0:T(8,128)(2,1)S(1)}, u32[]{:S(2)}, u32[]{:S(2)}) collective-permute-start(bf16[128,2048]{1,0:T(8,128)(2,1)S(1)} %pad_maximum_fusion.9), channel_id=1, source_target_pairs={{0,3},{1,0},{2,1},{3,2},{4,7},{5,4},{6,5},{7,6},{8,11},{9,8},{10,9... | collective-permute-start | bytes 1572872 | tf_op jit(solution)/shard_map/ppermute | solution.py:80
  364.6 10.8 %collective-permute-start.29 = (bf16[128,2048]{1,0:T(8,128)(2,1)S(1)}, bf16[128,2048]{1,0:T(8,128)(2,1)S(1)}, u32[]{:S(2)}, u32[]{:S(2)}) collective-permute-start(bf16[128,2048]{1,0:T(8,128)(2,1)S(1)} %pad_maximum_fusion.8), channel_id=1, source_target_pairs={{0,1},{1,2},{2,3},{3,0},{4,5},{5,6},{6,7},{7,4},{8,9},{9,10},{10,1... | collective-permute-start | bytes 1572872 | tf_op jit(solution)/shard_map/ppermute | solution.py:79
  (48 other events, 599.1 us)
Sparse Core Ops, SparseCore 0:
  55.7 48.1 all-gather.6
  233.3 46.1 all-gather.8

commit v7 on v6

--- a/solution.py
+++ b/solution.py
@@ -148,19 +148,18 @@
             project_piece, gate_up_slices = lax.optimization_barrier(
                 (project_piece, [w_gate_up[index] for index in range(DEPTH_NUMBER)])
             )
-        projected = jnp.concatenate(
-            [
-                jnp.dot(project_piece, query_weight, preferred_element_type=jnp.float32),
-                jnp.dot(project_piece, pair_weight, preferred_element_type=jnp.float32),
-            ],
-            axis=1,
-        )
-        query = rotate(
-            projected[:, :cols_query].reshape(rows_all, local_heads, HD), cosine, sine
-        ).astype(jnp.bfloat16)
-        pairs = projected[:, cols_query:].reshape(rows_all, local_kv, 2, HD)
+        pairs = jnp.dot(
+            project_piece, pair_weight, preferred_element_type=jnp.float32
+        ).reshape(rows_all, local_kv, 2, HD)
         lookup_vectors = rotate(pairs[:, :, 0], cosine, sine).astype(jnp.bfloat16)
         values = pairs[:, :, 1].astype(jnp.bfloat16)
+        query = rotate(
+            jnp.dot(project_piece, query_weight, preferred_element_type=jnp.float32).reshape(
+                rows_all, local_heads, HD
+            ),
+            cosine,
+            sine,
+        ).astype(jnp.bfloat16)
         query = query.reshape(seg_local, SEG_LEN, local_kv, group, HD)
         lookup_vectors = lookup_vectors.reshape(seg_local, SEG_LEN, local_kv, HD)
         values = values.reshape(seg_local, SEG_LEN, local_kv, HD)

time: 391 us -> 391 us (level)
  no operation moved by 1% of the time
where the time goes in v7:
time: 391 us; the launch traced here: 384 us
  waiting for transfers between devices  144 us (37%)
  matrix products  68.1 us (17%)
  local copies, waits for them, and re-layouts  62.9 us (16%)
  starting transfers between devices  50.7 us (13%)
  other arithmetic  42.6 us (11%)
  between operations  15.8 us (4%)
    all_gather x2, waiting for transfers between devices, body(): gathered = lax.all_gather(payload, 'seg')  51.5 us
    dot_general x6, matrix products, feed_forward(): jnp.einsum('rd,dtf->rtf', rows, widening_matrix, preferred_element_type=j...  26.4 us
    ppermute x2, waiting for transfers between devices, ring_scatter(): got_after = lax.ppermute(prev_part.astype(jnp.bfloat16), axis, behind)  18.2 us
    ppermute x2, waiting for transfers between devices, ring_pieces(): from_after = lax.ppermute(piece, axis, behind)  16.6 us
    squeeze x1, local copies, waits for them, and re-layouts, body(): w_gate_up[index]  14.2 us
    ppermute x2, waiting for transfers between devices, ring_scatter(): sent_top = lax.ppermute(far[:half].astype(jnp.bfloat16), axis, ahead)  11.5 us
    dot_general x3, local copies, waits for them, and re-layouts, body(): jnp.dot(project_piece, query_weight, preferred_element_type=jnp.float32)  10.5 us
    ppermute x2, waiting for transfers between devices, ring_scatter_parts(): got_before = lax.ppermute(next_part.astype(jnp.bfloat16), axis, ahead)  10.1 us
  transfers between devices with their start and end apart: 34, of which 24 were waited for; matrix products, arithmetic and copies ran while one was open for 29% of the time, Pallas kernels for 0%

profile of v7, /device:TPU:0, one launch (start us, length us, event | category | flops | bytes accessed | tf_op | source)
XLA Modules:
  0.0 383.9 jit_solution(3296475473165009302)
XLA Ops:
  12.2 4.1 %collective-permute-start = (bf16[128,2048]{1,0:T(8,128)(2,1)}, bf16[128,2048]{1,0:T(8,128)(2,1)}, u32[]{:S(2)}, u32[]{:S(2)}) collective-permute-start(bf16[128,2048]{1,0:T(8,128)(2,1)} %get-tuple-element.24), channel_id=1, source_target_pairs={{0,3},{1,0},{2,1},{3,2},{4,7},{5,4},{6,5},{7,6},{8,11},{9,8},{10,9... | collective-permute-start | bytes 1572872 | tf_op jit(solution)/shard_map/ppermute | solution.py:27
  16.4 14.2 %slice_bitcast_fusion = (bf16[2048,2,1024]{2,1,0:T(2,128)(2,1)}, bf16[2048,2,1024]{2,1,0:T(2,128)(2,1)}) fusion(bf16[2,2048,2,1024]{3,2,1,0:T(2,128)(2,1)} %param.26), kind=kLoop, calls=%fused_computation.10 | loop fusion | bytes 33554432 | tf_op jit(solution)/shard_map/squeeze | solution.py:149
  40.2 3.3 collective-permute-start.3
  55.9 3.9 %slice_bitcast_fusion.2 = (bf16[512,2048]{0,1:T(8,128)(2,1)}, bf16[512,2048]{0,1:T(8,128)(2,1)S(1)}) fusion(bf16[2,2048,512]{2,1,0:T(8,128)(2,1)} %param.23), kind=kLoop, calls=%fused_computation.75 | loop fusion | bytes 8388608 | tf_op jit(solution)/shard_map/dot_general | solution.py:157
  63.7 3.5 fusion.57
  70.9 4.6 %divide_convert_fusion.1 = bf16[2,4,512,640]{2,3,1,0:T(8,128)(2,1)} fusion(f32[2,4,512,512]{2,3,1,0:T(8,128)S(1)} %get-tuple-element.88, f32[2,4,512,128]{2,3,1,0:T(8,128)} %copy-done.1, f32[2,4,512]{2,1,0:T(4,128)S(1)} %fusion.3, f32[2,4,512]{2,1,0:T(4,128)S(1)} %reduce_max.61), kind=kLoop, calls=%fused_computation.5 | loop fusion | flops 10485760 | bytes 15761408 | tf_op jit(solution)/shard_map/convert_element_type | solution.py:224
  78.5 25.4 %all-gather.7.cloned.1.call-done = bf16[32,131,512]{2,1,0:T(8,128)(2,1)} async-done(((bf16[1,131,512]{2,1,0:T(8,128)(2,1)}), bf16[32,131,512]{2,1,0:T(8,128)(2,1)}) %all-gather.7.cloned.1.call-update) | async-done | bytes 4292624 | tf_op jit(solution)/shard_map/all_gather | solution.py:188
  120.8 5.1 %collective-permute-done.4 = bf16[64,2048]{1,0:T(8,128)(2,1)S(1)} collective-permute-done((bf16[64,2048]{1,0:T(8,128)(2,1)S(1)}, bf16[64,2048]{1,0:T(8,128)(2,1)S(1)}, u32[]{:S(2)}, u32[]{:S(2)}) %collective-permute-start.4) | collective-permute-done | bytes 262176 | tf_op jit(solution)/shard_map/ppermute | solution.py:46
  133.0 8.9 %collective-permute-done.7 = bf16[128,2048]{1,0:T(8,128)(2,1)S(1)} collective-permute-done((bf16[128,2048]{1,0:T(8,128)(2,1)}, bf16[128,2048]{1,0:T(8,128)(2,1)S(1)}, u32[]{:S(2)}, u32[]{:S(2)}) %collective-permute-start.7) | collective-permute-done | bytes 524320 | tf_op jit(solution)/shard_map/ppermute | solution.py:53
  141.9 4.6 %collective-permute-done.5 = bf16[128,2048]{1,0:T(8,128)(2,1)S(1)} collective-permute-done((bf16[128,2048]{1,0:T(8,128)(2,1)}, bf16[128,2048]{1,0:T(8,128)(2,1)S(1)}, u32[]{:S(2)}, u32[]{:S(2)}) %collective-permute-start.5) | collective-permute-done | bytes 524320 | tf_op jit(solution)/shard_map/ppermute | solution.py:52
  150.5 10.0 %collective-permute-done.9 = bf16[128,2048]{1,0:T(8,128)(2,1)S(1)} collective-permute-done((bf16[128,2048]{1,0:T(8,128)(2,1)S(1)}, bf16[128,2048]{1,0:T(8,128)(2,1)S(1)}, u32[]{:S(2)}, u32[]{:S(2)}) %collective-permute-start.9) | collective-permute-done | bytes 524320 | tf_op jit(solution)/shard_map/ppermute | solution.py:64
  162.7 6.6 %fusion.12 = f32[256,2,1024]{2,0,1:T(8,128)S(1)} fusion(bf16[2048,2,1024]{2,1,0:T(2,128)(2,1)} %get-tuple-element.7, bf16[128,2048]{1,0:T(8,128)(2,1)S(1)} %collective-permute-done.9, bf16[128,2048]{1,0:T(8,128)(2,1)S(1)} %collective-permute-done.8), kind=kOutput, calls=%fused_computation.22 | convolution fusion | flops 2149580800 | bytes 11534336 | tf_op jit(solution)/shard_map/rd,dtf->rtf/dot_general | solution.py:85
  177.9 4.3 %collective-permute-done.12 = bf16[64,2048]{1,0:T(8,128)(2,1)S(1)} collective-permute-done((bf16[64,2048]{1,0:T(8,128)(2,1)S(1)}, bf16[64,2048]{1,0:T(8,128)(2,1)S(1)}, u32[]{:S(2)}, u32[]{:S(2)}) %collective-permute-start.12) | collective-permute-done | bytes 262176 | tf_op jit(solution)/shard_map/ppermute | solution.py:75
  183.0 3.8 collective-permute-start.15
  193.5 6.0 %collective-permute-done.13 = bf16[128,2048]{1,0:T(8,128)(2,1)S(1)} collective-permute-done((bf16[128,2048]{1,0:T(8,128)(2,1)S(1)}, bf16[128,2048]{1,0:T(8,128)(2,1)S(1)}, u32[]{:S(2)}, u32[]{:S(2)}) %collective-permute-start.13) | collective-permute-done | bytes 524320 | tf_op jit(solution)/shard_map/ppermute | solution.py:79
  201.1 3.2 collective-permute-start.16
  204.5 10.0 %collective-permute-done.17 = bf16[128,2048]{1,0:T(8,128)(2,1)S(1)} collective-permute-done((bf16[128,2048]{1,0:T(8,128)(2,1)}, bf16[128,2048]{1,0:T(8,128)(2,1)S(1)}, u32[]{:S(2)}, u32[]{:S(2)}) %collective-permute-start.17) | collective-permute-done | bytes 524320 | tf_op jit(solution)/shard_map/ppermute | solution.py:26
  218.3 3.3 collective-permute-start.19
  233.2 4.2 %copy.161 = bf16[512,2048]{1,0:T(8,128)(2,1)} copy(bf16[512,2048]{0,1:T(8,128)(2,1)} %get-tuple-element.31) | data formatting | bytes 4194304 | tf_op jit(solution)/shard_map/dot_general | solution.py:157
  238.2 3.7 fusion.52
  245.7 4.6 %divide_convert_fusion = bf16[2,4,512,640]{2,3,1,0:T(8,128)(2,1)} fusion(f32[2,4,512,512]{2,3,1,0:T(8,128)S(1)} %get-tuple-element.98, f32[2,4,512,128]{2,3,1,0:T(8,128)} %copy-done, f32[2,4,512]{2,1,0:T(4,128)S(1)} %fusion.2, f32[2,4,512]{2,1,0:T(4,128)S(1)} %reduce_max.65), kind=kLoop, calls=%fused_computation.4 | loop fusion | flops 10485760 | bytes 15761408 | tf_op jit(solution)/shard_map/convert_element_type | solution.py:224
  253.5 26.1 %all-gather.9.cloned.1.call-done = bf16[32,131,512]{2,1,0:T(8,128)(2,1)} async-done(((bf16[1,131,512]{2,1,0:T(8,128)(2,1)}), bf16[32,131,512]{2,1,0:T(8,128)(2,1)}) %all-gather.9.cloned.1.call-update) | async-done | bytes 4292624 | tf_op jit(solution)/shard_map/all_gather | solution.py:188
  294.0 6.3 %collective-permute-done.20 = bf16[64,2048]{1,0:T(8,128)(2,1)S(1)} collective-permute-done((bf16[64,2048]{1,0:T(8,128)(2,1)S(1)}, bf16[64,2048]{1,0:T(8,128)(2,1)S(1)}, u32[]{:S(2)}, u32[]{:S(2)}) %collective-permute-start.20) | collective-permute-done | bytes 262176 | tf_op jit(solution)/shard_map/ppermute | solution.py:46
  304.9 9.3 %collective-permute-done.23 = bf16[128,2048]{1,0:T(8,128)(2,1)S(1)} collective-permute-done((bf16[128,2048]{1,0:T(8,128)(2,1)S(1)}, bf16[128,2048]{1,0:T(8,128)(2,1)S(1)}, u32[]{:S(2)}, u32[]{:S(2)}) %collective-permute-start.23) | collective-permute-done | bytes 524320 | tf_op jit(solution)/shard_map/ppermute | solution.py:53
  314.9 4.0 %collective-permute-done.21 = bf16[128,2048]{1,0:T(8,128)(2,1)} collective-permute-done((bf16[128,2048]{1,0:T(8,128)(2,1)}, bf16[128,2048]{1,0:T(8,128)(2,1)}, u32[]{:S(2)}, u32[]{:S(2)}) %collective-permute-start.21) | collective-permute-done | bytes 524320 | tf_op jit(solution)/shard_map/ppermute | solution.py:52
  327.4 6.6 %collective-permute-done.25 = bf16[128,2048]{1,0:T(8,128)(2,1)} collective-permute-done((bf16[128,2048]{1,0:T(8,128)(2,1)}, bf16[128,2048]{1,0:T(8,128)(2,1)}, u32[]{:S(2)}, u32[]{:S(2)}) %collective-permute-start.25) | collective-permute-done | bytes 524320 | tf_op jit(solution)/shard_map/ppermute | solution.py:64
  338.1 6.9 %fusion.6 = f32[256,2,1024]{2,0,1:T(8,128)S(1)} fusion(bf16[2048,2,1024]{2,1,0:T(2,128)(2,1)} %get-tuple-element.8, bf16[128,2048]{1,0:T(8,128)(2,1)} %collective-permute-done.25, bf16[128,2048]{1,0:T(8,128)(2,1)} %collective-permute-done.24), kind=kOutput, calls=%fused_computation.16 | convolution fusion | flops 2149580800 | bytes 11534336 | tf_op jit(solution)/shard_map/rd,dtf->rtf/dot_general | solution.py:85
  345.0 3.7 fusion.181
  355.9 4.3 %collective-permute-done.28 = bf16[64,2048]{1,0:T(8,128)(2,1)S(1)} collective-permute-done((bf16[64,2048]{1,0:T(8,128)(2,1)S(1)}, bf16[64,2048]{1,0:T(8,128)(2,1)S(1)}, u32[]{:S(2)}, u32[]{:S(2)}) %collective-permute-start.28) | collective-permute-done | bytes 262176 | tf_op jit(solution)/shard_map/ppermute | solution.py:75
  360.8 3.8 collective-permute-start.31
  365.0 4.0 %fusion.8 = f32[128,2,1024]{2,0,1:T(8,128)S(1)} fusion(bf16[2048,2,1024]{2,1,0:T(2,128)(2,1)S(1)} %bitcast.299, bf16[128,2048]{1,0:T(8,128)(2,1)} %multiply_convert_fusion), kind=kOutput, calls=%fused_computation.18 | convolution fusion | flops 1073741824 | bytes 9961472 | tf_op jit(solution)/shard_map/rd,dtf->rtf/dot_general | solution.py:85
  371.2 4.1 %collective-permute-done.29 = bf16[128,2048]{1,0:T(8,128)(2,1)S(1)} collective-permute-done((bf16[128,2048]{1,0:T(8,128)(2,1)S(1)}, bf16[128,2048]{1,0:T(8,128)(2,1)S(1)}, u32[]{:S(2)}, u32[]{:S(2)}) %collective-permute-start.29) | collective-permute-done | bytes 524320 | tf_op jit(solution)/shard_map/ppermute | solution.py:79
  (300 shorter events, 151.5 us)
Async XLA Ops:
  7.2 96.8 %all-gather.7.cloned.1.call-start = ((), (), s32[]{:S(2)}) async-start(), calls=%async_computation | async-start | bytes 4595712 | tf_op jit(solution)/shard_map/all_gather | solution.py:188
  12.2 27.0 %collective-permute-start = (bf16[128,2048]{1,0:T(8,128)(2,1)}, bf16[128,2048]{1,0:T(8,128)(2,1)}, u32[]{:S(2)}, u32[]{:S(2)}) collective-permute-start(bf16[128,2048]{1,0:T(8,128)(2,1)} %get-tuple-element.24), channel_id=1, source_target_pairs={{0,3},{1,0},{2,1},{3,2},{4,7},{5,4},{6,5},{7,6},{8,11},{9,8},{10,9... | collective-permute-start | bytes 1572872 | tf_op jit(solution)/shard_map/ppermute | solution.py:27
  16.3 18.1 %collective-permute-start.1 = (bf16[128,2048]{1,0:T(8,128)(2,1)}, bf16[128,2048]{1,0:T(8,128)(2,1)}, u32[]{:S(2)}, u32[]{:S(2)}) collective-permute-start(bf16[128,2048]{1,0:T(8,128)(2,1)} %get-tuple-element.24), channel_id=1, source_target_pairs={{0,1},{1,2},{2,3},{3,0},{4,5},{5,6},{6,7},{7,4},{8,9},{9,10},{10,1... | collective-permute-start | bytes 1572872 | tf_op jit(solution)/shard_map/ppermute | solution.py:26
  36.1 9.3 %collective-permute-start.2 = (bf16[64,2048]{1,0:T(8,128)(2,1)}, bf16[64,2048]{1,0:T(8,128)(2,1)}, u32[]{:S(2)}, u32[]{:S(2)}) collective-permute-start(bf16[64,2048]{1,0:T(8,128)(2,1)} %slice.390), channel_id=1, source_target_pairs={{0,1},{1,2},{2,3},{3,0},{4,5},{5,6},{6,7},{7,4},{8,9},{9,10},{10,1... | collective-permute-start | bytes 786440 | tf_op jit(solution)/shard_map/ppermute | solution.py:28
  40.2 8.3 %collective-permute-start.3 = (bf16[64,2048]{1,0:T(8,128)(2,1)S(1)}, bf16[64,2048]{1,0:T(8,128)(2,1)S(1)}, u32[]{:S(2)}, u32[]{:S(2)}) collective-permute-start(bf16[64,2048]{1,0:T(8,128)(2,1)S(1)} %slice.391), channel_id=1, source_target_pairs={{0,3},{1,0},{2,1},{3,2},{4,7},{5,4},{6,5},{7,6},{8,11},{9,8},{10,9... | collective-permute-start | bytes 786440 | tf_op jit(solution)/shard_map/ppermute | solution.py:29
  55.6 224.0 %all-gather.9.cloned.1.call-start = ((), (), s32[]{:S(2)}) async-start(), calls=%async_computation.1 | async-start | bytes 4595712 | tf_op jit(solution)/shard_map/all_gather | solution.py:188
  116.2 9.7 %collective-permute-start.4 = (bf16[64,2048]{1,0:T(8,128)(2,1)S(1)}, bf16[64,2048]{1,0:T(8,128)(2,1)S(1)}, u32[]{:S(2)}, u32[]{:S(2)}) collective-permute-start(bf16[64,2048]{1,0:T(8,128)(2,1)S(1)} %get-tuple-element.61), channel_id=1, source_target_pairs={{0,1},{1,2},{2,3},{3,0},{4,5},{5,6},{6,7},{7,4},{8,9},{9,10},{10,1... | collective-permute-start | bytes 786440 | tf_op jit(solution)/shard_map/ppermute | solution.py:46
  117.9 8.2 %collective-permute-start.6 = (bf16[64,2048]{1,0:T(8,128)(2,1)S(1)}, bf16[64,2048]{1,0:T(8,128)(2,1)S(1)}, u32[]{:S(2)}, u32[]{:S(2)}) collective-permute-start(bf16[64,2048]{1,0:T(8,128)(2,1)S(1)} %get-tuple-element.62), channel_id=1, source_target_pairs={{0,3},{1,0},{2,1},{3,2},{4,7},{5,4},{6,5},{7,6},{8,11},{9,8},{10,9... | collective-permute-start | bytes 786440 | tf_op jit(solution)/shard_map/ppermute | solution.py:47
  128.2 13.8 %collective-permute-start.7 = (bf16[128,2048]{1,0:T(8,128)(2,1)}, bf16[128,2048]{1,0:T(8,128)(2,1)S(1)}, u32[]{:S(2)}, u32[]{:S(2)}) collective-permute-start(bf16[128,2048]{1,0:T(8,128)(2,1)} %pad_maximum_fusion.2), channel_id=1, source_target_pairs={{0,3},{1,0},{2,1},{3,2},{4,7},{5,4},{6,5},{7,6},{8,11},{9,8},{10,9... | collective-permute-start | bytes 1572872 | tf_op jit(solution)/shard_map/ppermute | solution.py:53
  132.0 14.5 %collective-permute-start.5 = (bf16[128,2048]{1,0:T(8,128)(2,1)}, bf16[128,2048]{1,0:T(8,128)(2,1)S(1)}, u32[]{:S(2)}, u32[]{:S(2)}) collective-permute-start(bf16[128,2048]{1,0:T(8,128)(2,1)} %pad_maximum_fusion.1), channel_id=1, source_target_pairs={{0,1},{1,2},{2,3},{3,0},{4,5},{5,6},{6,7},{7,4},{8,9},{9,10},{10,1... | collective-permute-start | bytes 1572872 | tf_op jit(solution)/shard_map/ppermute | solution.py:52
  148.4 12.1 %collective-permute-start.9 = (bf16[128,2048]{1,0:T(8,128)(2,1)S(1)}, bf16[128,2048]{1,0:T(8,128)(2,1)S(1)}, u32[]{:S(2)}, u32[]{:S(2)}) collective-permute-start(bf16[128,2048]{1,0:T(8,128)(2,1)S(1)} %multiply_convert_fusion.2), channel_id=1, source_target_pairs={{0,3},{1,0},{2,1},{3,2},{4,7},{5,4},{6,5},{7,6},{8,11},{9,8},{10,9... | collective-permute-start | bytes 1572872 | tf_op jit(solution)/shard_map/ppermute | solution.py:64
  148.5 13.4 %collective-permute-start.8 = (bf16[128,2048]{1,0:T(8,128)(2,1)S(1)}, bf16[128,2048]{1,0:T(8,128)(2,1)S(1)}, u32[]{:S(2)}, u32[]{:S(2)}) collective-permute-start(bf16[128,2048]{1,0:T(8,128)(2,1)S(1)} %multiply_convert_fusion.2), channel_id=1, source_target_pairs={{0,1},{1,2},{2,3},{3,0},{4,5},{5,6},{6,7},{7,4},{8,9},{9,10},{10,1... | collective-permute-start | bytes 1572872 | tf_op jit(solution)/shard_map/ppermute | solution.py:63
  160.5 10.3 %collective-permute-start.11 = (bf16[64,2048]{1,0:T(8,128)(2,1)S(1)}, bf16[64,2048]{1,0:T(8,128)(2,1)S(1)}, u32[]{:S(2)}, u32[]{:S(2)}) collective-permute-start(bf16[64,2048]{1,0:T(8,128)(2,1)S(1)} %slice.412), channel_id=1, source_target_pairs={{0,3},{1,0},{2,1},{3,2},{4,7},{5,4},{6,5},{7,6},{8,11},{9,8},{10,9... | collective-permute-start | bytes 786440 | tf_op jit(solution)/shard_map/ppermute | solution.py:66
  162.0 8.8 %collective-permute-start.10 = (bf16[64,2048]{1,0:T(8,128)(2,1)S(1)}, bf16[64,2048]{1,0:T(8,128)(2,1)S(1)}, u32[]{:S(2)}, u32[]{:S(2)}) collective-permute-start(bf16[64,2048]{1,0:T(8,128)(2,1)S(1)} %slice.411), channel_id=1, source_target_pairs={{0,1},{1,2},{2,3},{3,0},{4,5},{5,6},{6,7},{7,4},{8,9},{9,10},{10,1... | collective-permute-start | bytes 786440 | tf_op jit(solution)/shard_map/ppermute | solution.py:65
  174.6 7.7 %collective-permute-start.12 = (bf16[64,2048]{1,0:T(8,128)(2,1)S(1)}, bf16[64,2048]{1,0:T(8,128)(2,1)S(1)}, u32[]{:S(2)}, u32[]{:S(2)}) collective-permute-start(bf16[64,2048]{1,0:T(8,128)(2,1)S(1)} %get-tuple-element.59), channel_id=1, source_target_pairs={{0,1},{1,2},{2,3},{3,0},{4,5},{5,6},{6,7},{7,4},{8,9},{9,10},{10,1... | collective-permute-start | bytes 786440 | tf_op jit(solution)/shard_map/ppermute | solution.py:75
  174.7 8.2 %collective-permute-start.14 = (bf16[64,2048]{1,0:T(8,128)(2,1)S(1)}, bf16[64,2048]{1,0:T(8,128)(2,1)S(1)}, u32[]{:S(2)}, u32[]{:S(2)}) collective-permute-start(bf16[64,2048]{1,0:T(8,128)(2,1)S(1)} %get-tuple-element.60), channel_id=1, source_target_pairs={{0,3},{1,0},{2,1},{3,2},{4,7},{5,4},{6,5},{7,6},{8,11},{9,8},{10,9... | collective-permute-start | bytes 786440 | tf_op jit(solution)/shard_map/ppermute | solution.py:76
  183.0 10.5 %collective-permute-start.15 = (bf16[128,2048]{1,0:T(8,128)(2,1)S(1)}, bf16[128,2048]{1,0:T(8,128)(2,1)S(1)}, u32[]{:S(2)}, u32[]{:S(2)}) collective-permute-start(bf16[128,2048]{1,0:T(8,128)(2,1)S(1)} %pad_maximum_fusion.4), channel_id=1, source_target_pairs={{0,3},{1,0},{2,1},{3,2},{4,7},{5,4},{6,5},{7,6},{8,11},{9,8},{10,9... | collective-permute-start | bytes 1572872 | tf_op jit(solution)/shard_map/ppermute | solution.py:80
  186.9 12.7 %collective-permute-start.13 = (bf16[128,2048]{1,0:T(8,128)(2,1)S(1)}, bf16[128,2048]{1,0:T(8,128)(2,1)S(1)}, u32[]{:S(2)}, u32[]{:S(2)}) collective-permute-start(bf16[128,2048]{1,0:T(8,128)(2,1)S(1)} %pad_maximum_fusion.3), channel_id=1, source_target_pairs={{0,1},{1,2},{2,3},{3,0},{4,5},{5,6},{6,7},{7,4},{8,9},{9,10},{10,1... | collective-permute-start | bytes 1572872 | tf_op jit(solution)/shard_map/ppermute | solution.py:79
  201.1 13.4 %collective-permute-start.17 = (bf16[128,2048]{1,0:T(8,128)(2,1)}, bf16[128,2048]{1,0:T(8,128)(2,1)S(1)}, u32[]{:S(2)}, u32[]{:S(2)}) collective-permute-start(bf16[128,2048]{1,0:T(8,128)(2,1)} %get-tuple-element.18), channel_id=1, source_target_pairs={{0,1},{1,2},{2,3},{3,0},{4,5},{5,6},{6,7},{7,4},{8,9},{9,10},{10,1... | collective-permute-start | bytes 1572872 | tf_op jit(solution)/shard_map/ppermute | solution.py:26
  201.1 16.2 %collective-permute-start.16 = (bf16[128,2048]{1,0:T(8,128)(2,1)}, bf16[128,2048]{1,0:T(8,128)(2,1)}, u32[]{:S(2)}, u32[]{:S(2)}) collective-permute-start(bf16[128,2048]{1,0:T(8,128)(2,1)} %get-tuple-element.18), channel_id=1, source_target_pairs={{0,3},{1,0},{2,1},{3,2},{4,7},{5,4},{6,5},{7,6},{8,11},{9,8},{10,9... | collective-permute-start | bytes 1572872 | tf_op jit(solution)/shard_map/ppermute | solution.py:27
  215.3 8.2 %collective-permute-start.18 = (bf16[64,2048]{1,0:T(8,128)(2,1)}, bf16[64,2048]{1,0:T(8,128)(2,1)}, u32[]{:S(2)}, u32[]{:S(2)}) collective-permute-start(bf16[64,2048]{1,0:T(8,128)(2,1)} %slice.420), channel_id=1, source_target_pairs={{0,1},{1,2},{2,3},{3,0},{4,5},{5,6},{6,7},{7,4},{8,9},{9,10},{10,1... | collective-permute-start | bytes 786440 | tf_op jit(solution)/shard_map/ppermute | solution.py:28
  290.6 9.7 %collective-permute-start.20 = (bf16[64,2048]{1,0:T(8,128)(2,1)S(1)}, bf16[64,2048]{1,0:T(8,128)(2,1)S(1)}, u32[]{:S(2)}, u32[]{:S(2)}) collective-permute-start(bf16[64,2048]{1,0:T(8,128)(2,1)S(1)} %get-tuple-element.55), channel_id=1, source_target_pairs={{0,1},{1,2},{2,3},{3,0},{4,5},{5,6},{6,7},{7,4},{8,9},{9,10},{10,1... | collective-permute-start | bytes 786440 | tf_op jit(solution)/shard_map/ppermute | solution.py:46
  292.2 8.2 %collective-permute-start.22 = (bf16[64,2048]{1,0:T(8,128)(2,1)S(1)}, bf16[64,2048]{1,0:T(8,128)(2,1)S(1)}, u32[]{:S(2)}, u32[]{:S(2)}) collective-permute-start(bf16[64,2048]{1,0:T(8,128)(2,1)S(1)} %get-tuple-element.56), channel_id=1, source_target_pairs={{0,3},{1,0},{2,1},{3,2},{4,7},{5,4},{6,5},{7,6},{8,11},{9,8},{10,9... | collective-permute-start | bytes 786440 | tf_op jit(solution)/shard_map/ppermute | solution.py:47
  300.6 13.5 %collective-permute-start.23 = (bf16[128,2048]{1,0:T(8,128)(2,1)S(1)}, bf16[128,2048]{1,0:T(8,128)(2,1)S(1)}, u32[]{:S(2)}, u32[]{:S(2)}) collective-permute-start(bf16[128,2048]{1,0:T(8,128)(2,1)S(1)} %pad_maximum_fusion.7), channel_id=1, source_target_pairs={{0,3},{1,0},{2,1},{3,2},{4,7},{5,4},{6,5},{7,6},{8,11},{9,8},{10,9... | collective-permute-start | bytes 1572872 | tf_op jit(solution)/shard_map/ppermute | solution.py:53
  304.5 14.5 %collective-permute-start.21 = (bf16[128,2048]{1,0:T(8,128)(2,1)}, bf16[128,2048]{1,0:T(8,128)(2,1)}, u32[]{:S(2)}, u32[]{:S(2)}) collective-permute-start(bf16[128,2048]{1,0:T(8,128)(2,1)} %pad_maximum_fusion.6), channel_id=1, source_target_pairs={{0,1},{1,2},{2,3},{3,0},{4,5},{5,6},{6,7},{7,4},{8,9},{9,10},{10,1... | collective-permute-start | bytes 1572872 | tf_op jit(solution)/shard_map/ppermute | solution.py:52
  321.8 12.2 %collective-permute-start.25 = (bf16[128,2048]{1,0:T(8,128)(2,1)}, bf16[128,2048]{1,0:T(8,128)(2,1)}, u32[]{:S(2)}, u32[]{:S(2)}) collective-permute-start(bf16[128,2048]{1,0:T(8,128)(2,1)} %multiply_convert_fusion), channel_id=1, source_target_pairs={{0,3},{1,0},{2,1},{3,2},{4,7},{5,4},{6,5},{7,6},{8,11},{9,8},{10,9... | collective-permute-start | bytes 1572872 | tf_op jit(solution)/shard_map/ppermute | solution.py:64
  321.8 14.7 %collective-permute-start.24 = (bf16[128,2048]{1,0:T(8,128)(2,1)}, bf16[128,2048]{1,0:T(8,128)(2,1)}, u32[]{:S(2)}, u32[]{:S(2)}) collective-permute-start(bf16[128,2048]{1,0:T(8,128)(2,1)} %multiply_convert_fusion), channel_id=1, source_target_pairs={{0,1},{1,2},{2,3},{3,0},{4,5},{5,6},{6,7},{7,4},{8,9},{9,10},{10,1... | collective-permute-start | bytes 1572872 | tf_op jit(solution)/shard_map/ppermute | solution.py:63
  335.0 13.8 %collective-permute-start.27 = (bf16[64,2048]{1,0:T(8,128)(2,1)S(1)}, bf16[64,2048]{1,0:T(8,128)(2,1)S(1)}, u32[]{:S(2)}, u32[]{:S(2)}) collective-permute-start(bf16[64,2048]{1,0:T(8,128)(2,1)S(1)} %slice.442), channel_id=1, source_target_pairs={{0,3},{1,0},{2,1},{3,2},{4,7},{5,4},{6,5},{7,6},{8,11},{9,8},{10,9... | collective-permute-start | bytes 786440 | tf_op jit(solution)/shard_map/ppermute | solution.py:66
  337.5 11.2 %collective-permute-start.26 = (bf16[64,2048]{1,0:T(8,128)(2,1)S(1)}, bf16[64,2048]{1,0:T(8,128)(2,1)S(1)}, u32[]{:S(2)}, u32[]{:S(2)}) collective-permute-start(bf16[64,2048]{1,0:T(8,128)(2,1)S(1)} %slice.441), channel_id=1, source_target_pairs={{0,1},{1,2},{2,3},{3,0},{4,5},{5,6},{6,7},{7,4},{8,9},{9,10},{10,1... | collective-permute-start | bytes 786440 | tf_op jit(solution)/shard_map/ppermute | solution.py:65
  352.7 7.9 %collective-permute-start.30 = (bf16[64,2048]{1,0:T(8,128)(2,1)S(1)}, bf16[64,2048]{1,0:T(8,128)(2,1)S(1)}, u32[]{:S(2)}, u32[]{:S(2)}) collective-permute-start(bf16[64,2048]{1,0:T(8,128)(2,1)S(1)} %get-tuple-element.54), channel_id=1, source_target_pairs={{0,3},{1,0},{2,1},{3,2},{4,7},{5,4},{6,5},{7,6},{8,11},{9,8},{10,9... | collective-permute-start | bytes 786440 | tf_op jit(solution)/shard_map/ppermute | solution.py:76
  360.8 10.5 %collective-permute-start.31 = (bf16[128,2048]{1,0:T(8,128)(2,1)S(1)}, bf16[128,2048]{1,0:T(8,128)(2,1)S(1)}, u32[]{:S(2)}, u32[]{:S(2)}) collective-permute-start(bf16[128,2048]{1,0:T(8,128)(2,1)S(1)} %pad_maximum_fusion.9), channel_id=1, source_target_pairs={{0,3},{1,0},{2,1},{3,2},{4,7},{5,4},{6,5},{7,6},{8,11},{9,8},{10,9... | collective-permute-start | bytes 1572872 | tf_op jit(solution)/shard_map/ppermute | solution.py:80
  364.6 10.8 %collective-permute-start.29 = (bf16[128,2048]{1,0:T(8,128)(2,1)S(1)}, bf16[128,2048]{1,0:T(8,128)(2,1)S(1)}, u32[]{:S(2)}, u32[]{:S(2)}) collective-permute-start(bf16[128,2048]{1,0:T(8,128)(2,1)S(1)} %pad_maximum_fusion.8), channel_id=1, source_target_pairs={{0,1},{1,2},{2,3},{3,0},{4,5},{5,6},{6,7},{7,4},{8,9},{9,10},{10,1... | collective-permute-start | bytes 1572872 | tf_op jit(solution)/shard_map/ppermute | solution.py:79
  (48 other events, 599.1 us)
Sparse Core Ops, SparseCore 0:
  55.7 48.1 all-gather.6
  233.3 46.1 all-gather.8

commit v8 on v7

--- a/solution.py
+++ b/solution.py
@@ -144,10 +144,6 @@
         down_weight = w_down[layer]
         normed = rms_norm(stream, attn_gain[layer])
         project_piece = ring_gather(normed, "head")
-        if layer == 0:
-            project_piece, gate_up_slices = lax.optimization_barrier(
-                (project_piece, [w_gate_up[index] for index in range(DEPTH_NUMBER)])
-            )
         pairs = jnp.dot(
             project_piece, pair_weight, preferred_element_type=jnp.float32
         ).reshape(rows_all, local_kv, 2, HD)
@@ -199,6 +195,10 @@
         state = carry[None, :] * mem_init[layer] + jnp.sum(
             weight[:, None, :] * written_all, axis=0
         )
+        if layer == 0:
+            state, gate_up_slices = lax.optimization_barrier(
+                (state, [w_gate_up[index] for index in range(DEPTH_NUMBER)])
+            )
         segment = 0
         memory_read = state.astype(jnp.bfloat16).reshape(MEM, local_kv, group, HD)
         state = rates[segment] * state + (1.0 - rates[segment]) * written[segment]

time: 391 us -> 384 us (0.982)
    all_gather x2, waiting for transfers between devices: 51.5 us -> 39.1 us  [body(): gathered = lax.all_gather(payload, 'seg')]
    ppermute x2, waiting for transfers between devices: 10 us -> 19.8 us  [ring_gather(): from_before = lax.ppermute(piece, axis, ahead)]
    unnamed x101 -> x87, local copies, waits for them, and re-layouts: 9.79 us -> 10 us
  transfers between devices with their start and end apart: 34 -> 34, of which waited for: 24 -> 25; matrix products, arithmetic and copies ran while one was open for 29% -> 27% of each run, Pallas kernels for 0% -> 0%
where the time goes in v8:
time: 384 us; the launch traced here: 379 us
  waiting for transfers between devices  144 us (38%)
  matrix products  68.1 us (18%)
  local copies, waits for them, and re-layouts  60.3 us (16%)
  starting transfers between devices  50.6 us (13%)
  other arithmetic  40.2 us (10%)
  between operations  15.8 us (4%)
    all_gather x2, waiting for transfers between devices, body(): gathered = lax.all_gather(payload, 'seg')  39.1 us
    dot_general x6, matrix products, feed_forward(): jnp.einsum('rd,dtf->rtf', rows, widening_matrix, preferred_element_type=j...  29 us
    ppermute x2, waiting for transfers between devices, ring_gather(): from_before = lax.ppermute(piece, axis, ahead)  19.8 us
    ppermute x2, waiting for transfers between devices, ring_scatter(): got_after = lax.ppermute(prev_part.astype(jnp.bfloat16), axis, behind)  18.7 us
    ppermute x2, waiting for transfers between devices, ring_pieces(): from_after = lax.ppermute(piece, axis, behind)  17.7 us
    squeeze x1, local copies, waits for them, and re-layouts, body(): w_gate_up[index]  14.5 us
    ppermute x2, waiting for transfers between devices, ring_scatter(): sent_top = lax.ppermute(far[:half].astype(jnp.bfloat16), axis, ahead)  11.5 us
    dot_general x3, local copies, waits for them, and re-layouts, body(): jnp.dot(project_piece, query_weight, preferred_element_type=jnp.float32)  10.6 us
  transfers between devices with their start and end apart: 34, of which 25 were waited for; matrix products, arithmetic and copies ran while one was open for 27% of the time, Pallas kernels for 0%

profile of v8, /device:TPU:0, one launch (start us, length us, event | category | flops | bytes accessed | tf_op | source)
XLA Modules:
  0.0 378.7 jit_solution(4141673017973432198)
XLA Ops:
  18.7 9.6 %collective-permute-done.1 = bf16[128,2048]{1,0:T(8,128)(2,1)} collective-permute-done((bf16[128,2048]{1,0:T(8,128)(2,1)}, bf16[128,2048]{1,0:T(8,128)(2,1)}, u32[]{:S(2)}, u32[]{:S(2)}) %collective-permute-start.1) | collective-permute-done | bytes 524320 | tf_op jit(solution)/shard_map/ppermute | solution.py:26
  31.2 3.3 collective-permute-start.3
  47.2 3.8 %slice_bitcast_fusion.2 = (bf16[512,2048]{0,1:T(8,128)(2,1)}, bf16[512,2048]{0,1:T(8,128)(2,1)S(1)}) fusion(bf16[2,2048,512]{2,1,0:T(8,128)(2,1)} %param.23), kind=kLoop, calls=%fused_computation.75 | loop fusion | bytes 8388608 | tf_op jit(solution)/shard_map/dot_general | solution.py:153
  54.1 14.5 %slice_bitcast_fusion = (bf16[2048,2,1024]{2,1,0:T(2,128)(2,1)}, bf16[2048,2,1024]{2,1,0:T(2,128)(2,1)}) fusion(bf16[2,2048,2,1024]{3,2,1,0:T(2,128)(2,1)} %param.26), kind=kLoop, calls=%fused_computation.9 | loop fusion | bytes 33554432 | tf_op jit(solution)/shard_map/squeeze | solution.py:200
  74.3 4.6 %divide_convert_fusion.1 = bf16[2,4,512,640]{2,3,1,0:T(8,128)(2,1)} fusion(f32[2,4,512,512]{2,3,1,0:T(8,128)S(1)} %get-tuple-element.88, f32[2,4,512,128]{2,3,1,0:T(8,128)} %copy-done.1, f32[2,4,512]{2,1,0:T(4,128)S(1)} %fusion.3, f32[2,4,512]{2,1,0:T(4,128)S(1)} %reduce_max.61), kind=kLoop, calls=%fused_computation.5 | loop fusion | flops 10485760 | bytes 15761408 | tf_op jit(solution)/shard_map/convert_element_type | solution.py:224
  82.0 13.1 %all-gather.7.cloned.1.call-done = bf16[32,131,512]{2,1,0:T(8,128)(2,1)} async-done(((bf16[1,131,512]{2,1,0:T(8,128)(2,1)}), bf16[32,131,512]{2,1,0:T(8,128)(2,1)}) %all-gather.7.cloned.1.call-update) | async-done | bytes 4292624 | tf_op jit(solution)/shard_map/all_gather | solution.py:184
  113.2 5.1 %collective-permute-done.4 = bf16[64,2048]{1,0:T(8,128)(2,1)S(1)} collective-permute-done((bf16[64,2048]{1,0:T(8,128)(2,1)S(1)}, bf16[64,2048]{1,0:T(8,128)(2,1)S(1)}, u32[]{:S(2)}, u32[]{:S(2)}) %collective-permute-start.4) | collective-permute-done | bytes 262176 | tf_op jit(solution)/shard_map/ppermute | solution.py:46
  125.1 9.4 %collective-permute-done.7 = bf16[128,2048]{1,0:T(8,128)(2,1)S(1)} collective-permute-done((bf16[128,2048]{1,0:T(8,128)(2,1)}, bf16[128,2048]{1,0:T(8,128)(2,1)S(1)}, u32[]{:S(2)}, u32[]{:S(2)}) %collective-permute-start.7) | collective-permute-done | bytes 524320 | tf_op jit(solution)/shard_map/ppermute | solution.py:53
  134.5 4.1 %collective-permute-done.5 = bf16[128,2048]{1,0:T(8,128)(2,1)S(1)} collective-permute-done((bf16[128,2048]{1,0:T(8,128)(2,1)}, bf16[128,2048]{1,0:T(8,128)(2,1)S(1)}, u32[]{:S(2)}, u32[]{:S(2)}) %collective-permute-start.5) | collective-permute-done | bytes 524320 | tf_op jit(solution)/shard_map/ppermute | solution.py:52
  142.7 10.0 %collective-permute-done.9 = bf16[128,2048]{1,0:T(8,128)(2,1)S(1)} collective-permute-done((bf16[128,2048]{1,0:T(8,128)(2,1)S(1)}, bf16[128,2048]{1,0:T(8,128)(2,1)S(1)}, u32[]{:S(2)}, u32[]{:S(2)}) %collective-permute-start.9) | collective-permute-done | bytes 524320 | tf_op jit(solution)/shard_map/ppermute | solution.py:64
  154.9 6.6 %fusion.12 = f32[256,2,1024]{2,0,1:T(8,128)S(1)} fusion(bf16[2048,2,1024]{2,1,0:T(2,128)(2,1)} %get-tuple-element.7, bf16[128,2048]{1,0:T(8,128)(2,1)S(1)} %collective-permute-done.9, bf16[128,2048]{1,0:T(8,128)(2,1)S(1)} %collective-permute-done.8), kind=kOutput, calls=%fused_computation.22 | convolution fusion | flops 2149580800 | bytes 11534336 | tf_op jit(solution)/shard_map/rd,dtf->rtf/dot_general | solution.py:85
  166.8 3.2 collective-permute-start.14
  170.1 4.3 %collective-permute-done.12 = bf16[64,2048]{1,0:T(8,128)(2,1)S(1)} collective-permute-done((bf16[64,2048]{1,0:T(8,128)(2,1)S(1)}, bf16[64,2048]{1,0:T(8,128)(2,1)S(1)}, u32[]{:S(2)}, u32[]{:S(2)}) %collective-permute-start.12) | collective-permute-done | bytes 262176 | tf_op jit(solution)/shard_map/ppermute | solution.py:75
  175.2 3.8 collective-permute-start.15
  185.6 6.0 %collective-permute-done.13 = bf16[128,2048]{1,0:T(8,128)(2,1)S(1)} collective-permute-done((bf16[128,2048]{1,0:T(8,128)(2,1)S(1)}, bf16[128,2048]{1,0:T(8,128)(2,1)S(1)}, u32[]{:S(2)}, u32[]{:S(2)}) %collective-permute-start.13) | collective-permute-done | bytes 524320 | tf_op jit(solution)/shard_map/ppermute | solution.py:79
  193.2 3.2 collective-permute-start.16
  196.6 10.1 %collective-permute-done.17 = bf16[128,2048]{1,0:T(8,128)(2,1)} collective-permute-done((bf16[128,2048]{1,0:T(8,128)(2,1)}, bf16[128,2048]{1,0:T(8,128)(2,1)}, u32[]{:S(2)}, u32[]{:S(2)}) %collective-permute-start.17) | collective-permute-done | bytes 524320 | tf_op jit(solution)/shard_map/ppermute | solution.py:26
  211.5 3.3 collective-permute-start.19
  228.3 4.1 %copy.158 = bf16[512,2048]{1,0:T(8,128)(2,1)} copy(bf16[512,2048]{0,1:T(8,128)(2,1)} %get-tuple-element.31) | data formatting | bytes 4194304 | tf_op jit(solution)/shard_map/dot_general | solution.py:153
  232.4 3.7 fusion.52
  239.9 4.6 %divide_convert_fusion = bf16[2,4,512,640]{2,3,1,0:T(8,128)(2,1)} fusion(f32[2,4,512,512]{2,3,1,0:T(8,128)S(1)} %get-tuple-element.94, f32[2,4,512,128]{2,3,1,0:T(8,128)} %copy-done, f32[2,4,512]{2,1,0:T(4,128)S(1)} %fusion.2, f32[2,4,512]{2,1,0:T(4,128)S(1)} %reduce_max.65), kind=kLoop, calls=%fused_computation.4 | loop fusion | flops 10485760 | bytes 15761408 | tf_op jit(solution)/shard_map/convert_element_type | solution.py:224
  247.7 26.0 %all-gather.9.cloned.1.call-done = bf16[32,131,512]{2,1,0:T(8,128)(2,1)} async-done(((bf16[1,131,512]{2,1,0:T(8,128)(2,1)}), bf16[32,131,512]{2,1,0:T(8,128)(2,1)}) %all-gather.9.cloned.1.call-update) | async-done | bytes 4292624 | tf_op jit(solution)/shard_map/all_gather | solution.py:184
  288.1 6.3 %collective-permute-done.20 = bf16[64,2048]{1,0:T(8,128)(2,1)S(1)} collective-permute-done((bf16[64,2048]{1,0:T(8,128)(2,1)S(1)}, bf16[64,2048]{1,0:T(8,128)(2,1)S(1)}, u32[]{:S(2)}, u32[]{:S(2)}) %collective-permute-start.20) | collective-permute-done | bytes 262176 | tf_op jit(solution)/shard_map/ppermute | solution.py:46
  298.9 9.3 %collective-permute-done.23 = bf16[128,2048]{1,0:T(8,128)(2,1)S(1)} collective-permute-done((bf16[128,2048]{1,0:T(8,128)(2,1)S(1)}, bf16[128,2048]{1,0:T(8,128)(2,1)S(1)}, u32[]{:S(2)}, u32[]{:S(2)}) %collective-permute-start.23) | collective-permute-done | bytes 524320 | tf_op jit(solution)/shard_map/ppermute | solution.py:53
  309.0 4.0 %collective-permute-done.21 = bf16[128,2048]{1,0:T(8,128)(2,1)} collective-permute-done((bf16[128,2048]{1,0:T(8,128)(2,1)}, bf16[128,2048]{1,0:T(8,128)(2,1)}, u32[]{:S(2)}, u32[]{:S(2)}) %collective-permute-start.21) | collective-permute-done | bytes 524320 | tf_op jit(solution)/shard_map/ppermute | solution.py:52
  319.4 7.8 %collective-permute-done.25 = bf16[128,2048]{1,0:T(8,128)(2,1)} collective-permute-done((bf16[128,2048]{1,0:T(8,128)(2,1)S(1)}, bf16[128,2048]{1,0:T(8,128)(2,1)}, u32[]{:S(2)}, u32[]{:S(2)}) %collective-permute-start.25) | collective-permute-done | bytes 524320 | tf_op jit(solution)/shard_map/ppermute | solution.py:64
  331.4 7.0 %fusion.6 = f32[256,2,1024]{2,0,1:T(8,128)S(1)} fusion(bf16[2048,2,1024]{2,1,0:T(2,128)(2,1)} %get-tuple-element.8, bf16[128,2048]{1,0:T(8,128)(2,1)} %collective-permute-done.25, bf16[128,2048]{1,0:T(8,128)(2,1)} %collective-permute-done.24), kind=kOutput, calls=%fused_computation.16 | convolution fusion | flops 2149580800 | bytes 11534336 | tf_op jit(solution)/shard_map/rd,dtf->rtf/dot_general | solution.py:85
  339.9 6.5 %fusion.4 = f32[128,2,1024]{2,0,1:T(8,128)S(1)} fusion(bf16[2048,2,1024]{2,1,0:T(2,128)(2,1)} %get-tuple-element.8, bf16[64,2048]{1,0:T(8,128)(2,1)S(1)} %collective-permute-done.27, bf16[64,2048]{1,0:T(8,128)(2,1)S(1)} %collective-permute-done.26), kind=kOutput, calls=%fused_computation.14 | convolution fusion | flops 1074790400 | bytes 9961472 | tf_op jit(solution)/shard_map/rd,dtf->rtf/dot_general | solution.py:85
  347.3 3.2 collective-permute-start.30
  350.6 4.3 %collective-permute-done.28 = bf16[64,2048]{1,0:T(8,128)(2,1)S(1)} collective-permute-done((bf16[64,2048]{1,0:T(8,128)(2,1)S(1)}, bf16[64,2048]{1,0:T(8,128)(2,1)S(1)}, u32[]{:S(2)}, u32[]{:S(2)}) %collective-permute-start.28) | collective-permute-done | bytes 262176 | tf_op jit(solution)/shard_map/ppermute | solution.py:75
  355.5 3.8 collective-permute-start.31
  366.0 4.1 %collective-permute-done.29 = bf16[128,2048]{1,0:T(8,128)(2,1)S(1)} collective-permute-done((bf16[128,2048]{1,0:T(8,128)(2,1)S(1)}, bf16[128,2048]{1,0:T(8,128)(2,1)S(1)}, u32[]{:S(2)}, u32[]{:S(2)}) %collective-permute-start.29) | collective-permute-done | bytes 524320 | tf_op jit(solution)/shard_map/ppermute | solution.py:79
  (287 shorter events, 149.9 us)
Async XLA Ops:
  7.2 88.0 %all-gather.7.cloned.1.call-start = ((), (), s32[]{:S(2)}) async-start(), calls=%async_computation | async-start | bytes 4595712 | tf_op jit(solution)/shard_map/all_gather | solution.py:184
  11.9 16.4 %collective-permute-start.1 = (bf16[128,2048]{1,0:T(8,128)(2,1)}, bf16[128,2048]{1,0:T(8,128)(2,1)}, u32[]{:S(2)}, u32[]{:S(2)}) collective-permute-start(bf16[128,2048]{1,0:T(8,128)(2,1)} %get-tuple-element.24), channel_id=1, source_target_pairs={{0,1},{1,2},{2,3},{3,0},{4,5},{5,6},{6,7},{7,4},{8,9},{9,10},{10,1... | collective-permute-start | bytes 1572872 | tf_op jit(solution)/shard_map/ppermute | solution.py:26
  14.0 16.2 %collective-permute-start = (bf16[128,2048]{1,0:T(8,128)(2,1)}, bf16[128,2048]{1,0:T(8,128)(2,1)}, u32[]{:S(2)}, u32[]{:S(2)}) collective-permute-start(bf16[128,2048]{1,0:T(8,128)(2,1)} %get-tuple-element.24), channel_id=1, source_target_pairs={{0,3},{1,0},{2,1},{3,2},{4,7},{5,4},{6,5},{7,6},{8,11},{9,8},{10,9... | collective-permute-start | bytes 1572872 | tf_op jit(solution)/shard_map/ppermute | solution.py:27
  29.3 8.8 %collective-permute-start.2 = (bf16[64,2048]{1,0:T(8,128)(2,1)S(1)}, bf16[64,2048]{1,0:T(8,128)(2,1)S(1)}, u32[]{:S(2)}, u32[]{:S(2)}) collective-permute-start(bf16[64,2048]{1,0:T(8,128)(2,1)S(1)} %slice.390), channel_id=1, source_target_pairs={{0,1},{1,2},{2,3},{3,0},{4,5},{5,6},{6,7},{7,4},{8,9},{9,10},{10,1... | collective-permute-start | bytes 786440 | tf_op jit(solution)/shard_map/ppermute | solution.py:28
  31.2 8.0 %collective-permute-start.3 = (bf16[64,2048]{1,0:T(8,128)(2,1)S(1)}, bf16[64,2048]{1,0:T(8,128)(2,1)S(1)}, u32[]{:S(2)}, u32[]{:S(2)}) collective-permute-start(bf16[64,2048]{1,0:T(8,128)(2,1)S(1)} %slice.391), channel_id=1, source_target_pairs={{0,3},{1,0},{2,1},{3,2},{4,7},{5,4},{6,5},{7,6},{8,11},{9,8},{10,9... | collective-permute-start | bytes 786440 | tf_op jit(solution)/shard_map/ppermute | solution.py:29
  46.9 226.8 %all-gather.9.cloned.1.call-start = ((), (), s32[]{:S(2)}) async-start(), calls=%async_computation.1 | async-start | bytes 4595712 | tf_op jit(solution)/shard_map/all_gather | solution.py:184
  108.2 10.1 %collective-permute-start.4 = (bf16[64,2048]{1,0:T(8,128)(2,1)S(1)}, bf16[64,2048]{1,0:T(8,128)(2,1)S(1)}, u32[]{:S(2)}, u32[]{:S(2)}) collective-permute-start(bf16[64,2048]{1,0:T(8,128)(2,1)S(1)} %get-tuple-element.57), channel_id=1, source_target_pairs={{0,1},{1,2},{2,3},{3,0},{4,5},{5,6},{6,7},{7,4},{8,9},{9,10},{10,1... | collective-permute-start | bytes 786440 | tf_op jit(solution)/shard_map/ppermute | solution.py:46
  110.2 8.3 %collective-permute-start.6 = (bf16[64,2048]{1,0:T(8,128)(2,1)S(1)}, bf16[64,2048]{1,0:T(8,128)(2,1)}, u32[]{:S(2)}, u32[]{:S(2)}) collective-permute-start(bf16[64,2048]{1,0:T(8,128)(2,1)S(1)} %get-tuple-element.58), channel_id=1, source_target_pairs={{0,3},{1,0},{2,1},{3,2},{4,7},{5,4},{6,5},{7,6},{8,11},{9,8},{10,9... | collective-permute-start | bytes 786440 | tf_op jit(solution)/shard_map/ppermute | solution.py:47
  120.7 13.8 %collective-permute-start.7 = (bf16[128,2048]{1,0:T(8,128)(2,1)}, bf16[128,2048]{1,0:T(8,128)(2,1)S(1)}, u32[]{:S(2)}, u32[]{:S(2)}) collective-permute-start(bf16[128,2048]{1,0:T(8,128)(2,1)} %pad_maximum_fusion.2), channel_id=1, source_target_pairs={{0,3},{1,0},{2,1},{3,2},{4,7},{5,4},{6,5},{7,6},{8,11},{9,8},{10,9... | collective-permute-start | bytes 1572872 | tf_op jit(solution)/shard_map/ppermute | solution.py:53
  124.5 14.1 %collective-permute-start.5 = (bf16[128,2048]{1,0:T(8,128)(2,1)}, bf16[128,2048]{1,0:T(8,128)(2,1)S(1)}, u32[]{:S(2)}, u32[]{:S(2)}) collective-permute-start(bf16[128,2048]{1,0:T(8,128)(2,1)} %pad_maximum_fusion.1), channel_id=1, source_target_pairs={{0,1},{1,2},{2,3},{3,0},{4,5},{5,6},{6,7},{7,4},{8,9},{9,10},{10,1... | collective-permute-start | bytes 1572872 | tf_op jit(solution)/shard_map/ppermute | solution.py:52
  140.6 12.1 %collective-permute-start.9 = (bf16[128,2048]{1,0:T(8,128)(2,1)S(1)}, bf16[128,2048]{1,0:T(8,128)(2,1)S(1)}, u32[]{:S(2)}, u32[]{:S(2)}) collective-permute-start(bf16[128,2048]{1,0:T(8,128)(2,1)S(1)} %multiply_convert_fusion.2), channel_id=1, source_target_pairs={{0,3},{1,0},{2,1},{3,2},{4,7},{5,4},{6,5},{7,6},{8,11},{9,8},{10,9... | collective-permute-start | bytes 1572872 | tf_op jit(solution)/shard_map/ppermute | solution.py:64
  140.7 13.4 %collective-permute-start.8 = (bf16[128,2048]{1,0:T(8,128)(2,1)S(1)}, bf16[128,2048]{1,0:T(8,128)(2,1)S(1)}, u32[]{:S(2)}, u32[]{:S(2)}) collective-permute-start(bf16[128,2048]{1,0:T(8,128)(2,1)S(1)} %multiply_convert_fusion.2), channel_id=1, source_target_pairs={{0,1},{1,2},{2,3},{3,0},{4,5},{5,6},{6,7},{7,4},{8,9},{9,10},{10,1... | collective-permute-start | bytes 1572872 | tf_op jit(solution)/shard_map/ppermute | solution.py:63
  152.7 10.3 %collective-permute-start.11 = (bf16[64,2048]{1,0:T(8,128)(2,1)S(1)}, bf16[64,2048]{1,0:T(8,128)(2,1)S(1)}, u32[]{:S(2)}, u32[]{:S(2)}) collective-permute-start(bf16[64,2048]{1,0:T(8,128)(2,1)S(1)} %slice.412), channel_id=1, source_target_pairs={{0,3},{1,0},{2,1},{3,2},{4,7},{5,4},{6,5},{7,6},{8,11},{9,8},{10,9... | collective-permute-start | bytes 786440 | tf_op jit(solution)/shard_map/ppermute | solution.py:66
  154.1 8.8 %collective-permute-start.10 = (bf16[64,2048]{1,0:T(8,128)(2,1)S(1)}, bf16[64,2048]{1,0:T(8,128)(2,1)S(1)}, u32[]{:S(2)}, u32[]{:S(2)}) collective-permute-start(bf16[64,2048]{1,0:T(8,128)(2,1)S(1)} %slice.411), channel_id=1, source_target_pairs={{0,1},{1,2},{2,3},{3,0},{4,5},{5,6},{6,7},{7,4},{8,9},{9,10},{10,1... | collective-permute-start | bytes 786440 | tf_op jit(solution)/shard_map/ppermute | solution.py:65
  166.7 7.7 %collective-permute-start.12 = (bf16[64,2048]{1,0:T(8,128)(2,1)S(1)}, bf16[64,2048]{1,0:T(8,128)(2,1)S(1)}, u32[]{:S(2)}, u32[]{:S(2)}) collective-permute-start(bf16[64,2048]{1,0:T(8,128)(2,1)S(1)} %get-tuple-element.55), channel_id=1, source_target_pairs={{0,1},{1,2},{2,3},{3,0},{4,5},{5,6},{6,7},{7,4},{8,9},{9,10},{10,1... | collective-permute-start | bytes 786440 | tf_op jit(solution)/shard_map/ppermute | solution.py:75
  166.8 8.2 %collective-permute-start.14 = (bf16[64,2048]{1,0:T(8,128)(2,1)S(1)}, bf16[64,2048]{1,0:T(8,128)(2,1)S(1)}, u32[]{:S(2)}, u32[]{:S(2)}) collective-permute-start(bf16[64,2048]{1,0:T(8,128)(2,1)S(1)} %get-tuple-element.56), channel_id=1, source_target_pairs={{0,3},{1,0},{2,1},{3,2},{4,7},{5,4},{6,5},{7,6},{8,11},{9,8},{10,9... | collective-permute-start | bytes 786440 | tf_op jit(solution)/shard_map/ppermute | solution.py:76
  175.2 10.5 %collective-permute-start.15 = (bf16[128,2048]{1,0:T(8,128)(2,1)S(1)}, bf16[128,2048]{1,0:T(8,128)(2,1)S(1)}, u32[]{:S(2)}, u32[]{:S(2)}) collective-permute-start(bf16[128,2048]{1,0:T(8,128)(2,1)S(1)} %pad_maximum_fusion.4), channel_id=1, source_target_pairs={{0,3},{1,0},{2,1},{3,2},{4,7},{5,4},{6,5},{7,6},{8,11},{9,8},{10,9... | collective-permute-start | bytes 1572872 | tf_op jit(solution)/shard_map/ppermute | solution.py:80
  179.0 12.6 %collective-permute-start.13 = (bf16[128,2048]{1,0:T(8,128)(2,1)S(1)}, bf16[128,2048]{1,0:T(8,128)(2,1)S(1)}, u32[]{:S(2)}, u32[]{:S(2)}) collective-permute-start(bf16[128,2048]{1,0:T(8,128)(2,1)S(1)} %pad_maximum_fusion.3), channel_id=1, source_target_pairs={{0,1},{1,2},{2,3},{3,0},{4,5},{5,6},{6,7},{7,4},{8,9},{9,10},{10,1... | collective-permute-start | bytes 1572872 | tf_op jit(solution)/shard_map/ppermute | solution.py:79
  193.2 13.5 %collective-permute-start.17 = (bf16[128,2048]{1,0:T(8,128)(2,1)}, bf16[128,2048]{1,0:T(8,128)(2,1)}, u32[]{:S(2)}, u32[]{:S(2)}) collective-permute-start(bf16[128,2048]{1,0:T(8,128)(2,1)} %get-tuple-element.18), channel_id=1, source_target_pairs={{0,1},{1,2},{2,3},{3,0},{4,5},{5,6},{6,7},{7,4},{8,9},{9,10},{10,1... | collective-permute-start | bytes 1572872 | tf_op jit(solution)/shard_map/ppermute | solution.py:26
  193.2 17.4 %collective-permute-start.16 = (bf16[128,2048]{1,0:T(8,128)(2,1)}, bf16[128,2048]{1,0:T(8,128)(2,1)}, u32[]{:S(2)}, u32[]{:S(2)}) collective-permute-start(bf16[128,2048]{1,0:T(8,128)(2,1)} %get-tuple-element.18), channel_id=1, source_target_pairs={{0,3},{1,0},{2,1},{3,2},{4,7},{5,4},{6,5},{7,6},{8,11},{9,8},{10,9... | collective-permute-start | bytes 1572872 | tf_op jit(solution)/shard_map/ppermute | solution.py:27
  208.4 8.3 %collective-permute-start.18 = (bf16[64,2048]{1,0:T(8,128)(2,1)}, bf16[64,2048]{1,0:T(8,128)(2,1)S(1)}, u32[]{:S(2)}, u32[]{:S(2)}) collective-permute-start(bf16[64,2048]{1,0:T(8,128)(2,1)} %slice.420), channel_id=1, source_target_pairs={{0,1},{1,2},{2,3},{3,0},{4,5},{5,6},{6,7},{7,4},{8,9},{9,10},{10,1... | collective-permute-start | bytes 786440 | tf_op jit(solution)/shard_map/ppermute | solution.py:28
  284.7 9.7 %collective-permute-start.20 = (bf16[64,2048]{1,0:T(8,128)(2,1)S(1)}, bf16[64,2048]{1,0:T(8,128)(2,1)S(1)}, u32[]{:S(2)}, u32[]{:S(2)}) collective-permute-start(bf16[64,2048]{1,0:T(8,128)(2,1)S(1)} %get-tuple-element.53), channel_id=1, source_target_pairs={{0,1},{1,2},{2,3},{3,0},{4,5},{5,6},{6,7},{7,4},{8,9},{9,10},{10,1... | collective-permute-start | bytes 786440 | tf_op jit(solution)/shard_map/ppermute | solution.py:46
  286.3 8.2 %collective-permute-start.22 = (bf16[64,2048]{1,0:T(8,128)(2,1)S(1)}, bf16[64,2048]{1,0:T(8,128)(2,1)S(1)}, u32[]{:S(2)}, u32[]{:S(2)}) collective-permute-start(bf16[64,2048]{1,0:T(8,128)(2,1)S(1)} %get-tuple-element.54), channel_id=1, source_target_pairs={{0,3},{1,0},{2,1},{3,2},{4,7},{5,4},{6,5},{7,6},{8,11},{9,8},{10,9... | collective-permute-start | bytes 786440 | tf_op jit(solution)/shard_map/ppermute | solution.py:47
  294.7 13.5 %collective-permute-start.23 = (bf16[128,2048]{1,0:T(8,128)(2,1)S(1)}, bf16[128,2048]{1,0:T(8,128)(2,1)S(1)}, u32[]{:S(2)}, u32[]{:S(2)}) collective-permute-start(bf16[128,2048]{1,0:T(8,128)(2,1)S(1)} %pad_maximum_fusion.7), channel_id=1, source_target_pairs={{0,3},{1,0},{2,1},{3,2},{4,7},{5,4},{6,5},{7,6},{8,11},{9,8},{10,9... | collective-permute-start | bytes 1572872 | tf_op jit(solution)/shard_map/ppermute | solution.py:53
  298.6 14.5 %collective-permute-start.21 = (bf16[128,2048]{1,0:T(8,128)(2,1)}, bf16[128,2048]{1,0:T(8,128)(2,1)}, u32[]{:S(2)}, u32[]{:S(2)}) collective-permute-start(bf16[128,2048]{1,0:T(8,128)(2,1)} %pad_maximum_fusion.6), channel_id=1, source_target_pairs={{0,1},{1,2},{2,3},{3,0},{4,5},{5,6},{6,7},{7,4},{8,9},{9,10},{10,1... | collective-permute-start | bytes 1572872 | tf_op jit(solution)/shard_map/ppermute | solution.py:52
  315.1 12.0 %collective-permute-start.25 = (bf16[128,2048]{1,0:T(8,128)(2,1)S(1)}, bf16[128,2048]{1,0:T(8,128)(2,1)}, u32[]{:S(2)}, u32[]{:S(2)}) collective-permute-start(bf16[128,2048]{1,0:T(8,128)(2,1)S(1)} %multiply_convert_fusion), channel_id=1, source_target_pairs={{0,3},{1,0},{2,1},{3,2},{4,7},{5,4},{6,5},{7,6},{8,11},{9,8},{10,9... | collective-permute-start | bytes 1572872 | tf_op jit(solution)/shard_map/ppermute | solution.py:64
  315.2 14.5 %collective-permute-start.24 = (bf16[128,2048]{1,0:T(8,128)(2,1)S(1)}, bf16[128,2048]{1,0:T(8,128)(2,1)}, u32[]{:S(2)}, u32[]{:S(2)}) collective-permute-start(bf16[128,2048]{1,0:T(8,128)(2,1)S(1)} %multiply_convert_fusion), channel_id=1, source_target_pairs={{0,1},{1,2},{2,3},{3,0},{4,5},{5,6},{6,7},{7,4},{8,9},{9,10},{10,1... | collective-permute-start | bytes 1572872 | tf_op jit(solution)/shard_map/ppermute | solution.py:63
  328.1 11.8 %collective-permute-start.27 = (bf16[64,2048]{1,0:T(8,128)(2,1)S(1)}, bf16[64,2048]{1,0:T(8,128)(2,1)S(1)}, u32[]{:S(2)}, u32[]{:S(2)}) collective-permute-start(bf16[64,2048]{1,0:T(8,128)(2,1)S(1)} %slice.442), channel_id=1, source_target_pairs={{0,3},{1,0},{2,1},{3,2},{4,7},{5,4},{6,5},{7,6},{8,11},{9,8},{10,9... | collective-permute-start | bytes 786440 | tf_op jit(solution)/shard_map/ppermute | solution.py:66
  330.8 9.1 %collective-permute-start.26 = (bf16[64,2048]{1,0:T(8,128)(2,1)S(1)}, bf16[64,2048]{1,0:T(8,128)(2,1)S(1)}, u32[]{:S(2)}, u32[]{:S(2)}) collective-permute-start(bf16[64,2048]{1,0:T(8,128)(2,1)S(1)} %slice.441), channel_id=1, source_target_pairs={{0,1},{1,2},{2,3},{3,0},{4,5},{5,6},{6,7},{7,4},{8,9},{9,10},{10,1... | collective-permute-start | bytes 786440 | tf_op jit(solution)/shard_map/ppermute | solution.py:65
  347.3 8.1 %collective-permute-start.30 = (bf16[64,2048]{1,0:T(8,128)(2,1)S(1)}, bf16[64,2048]{1,0:T(8,128)(2,1)S(1)}, u32[]{:S(2)}, u32[]{:S(2)}) collective-permute-start(bf16[64,2048]{1,0:T(8,128)(2,1)S(1)} %get-tuple-element.52), channel_id=1, source_target_pairs={{0,3},{1,0},{2,1},{3,2},{4,7},{5,4},{6,5},{7,6},{8,11},{9,8},{10,9... | collective-permute-start | bytes 786440 | tf_op jit(solution)/shard_map/ppermute | solution.py:76
  355.5 10.5 %collective-permute-start.31 = (bf16[128,2048]{1,0:T(8,128)(2,1)S(1)}, bf16[128,2048]{1,0:T(8,128)(2,1)S(1)}, u32[]{:S(2)}, u32[]{:S(2)}) collective-permute-start(bf16[128,2048]{1,0:T(8,128)(2,1)S(1)} %pad_maximum_fusion.9), channel_id=1, source_target_pairs={{0,3},{1,0},{2,1},{3,2},{4,7},{5,4},{6,5},{7,6},{8,11},{9,8},{10,9... | collective-permute-start | bytes 1572872 | tf_op jit(solution)/shard_map/ppermute | solution.py:80
  359.3 10.8 %collective-permute-start.29 = (bf16[128,2048]{1,0:T(8,128)(2,1)S(1)}, bf16[128,2048]{1,0:T(8,128)(2,1)S(1)}, u32[]{:S(2)}, u32[]{:S(2)}) collective-permute-start(bf16[128,2048]{1,0:T(8,128)(2,1)S(1)} %pad_maximum_fusion.8), channel_id=1, source_target_pairs={{0,1},{1,2},{2,3},{3,0},{4,5},{5,6},{6,7},{7,4},{8,9},{9,10},{10,1... | collective-permute-start | bytes 1572872 | tf_op jit(solution)/shard_map/ppermute | solution.py:79
  (42 other events, 573.3 us)
Sparse Core Ops, SparseCore 0:
  47.0 48.1 all-gather.6
  227.6 46.1 all-gather.8

commit v9 on v8

--- a/solution.py
+++ b/solution.py
@@ -132,9 +132,12 @@
     group = HEADS // KV_HEADS
     local_kv = local_heads // group
     scale = HD ** (-0.5)
-    cosine, sine = rope_tables(jnp.arange(rows_all) % SEG_LEN)
+    piece_count = lax.axis_size("head")
+    piece_len = SEG_LEN // piece_count
+    origin = (jnp.arange(SEG_LEN) + lax.axis_index("head") * piece_len) % SEG_LEN
+    cosine, sine = rope_tables(origin)
     docs = document_index.reshape(seg_local, SEG_LEN)
-    causal = jnp.arange(SEG_LEN)[:, None] >= jnp.arange(SEG_LEN)[None, :]
+    causal = origin[:, None] >= origin[None, :]
     stream = tokens
     stored = []
     for layer in range(DEPTH_NUMBER):
@@ -143,7 +146,8 @@
         out_weight = w_out[layer]
         down_weight = w_down[layer]
         normed = rms_norm(stream, attn_gain[layer])
-        project_piece = ring_gather(normed, "head")
+        from_before, from_after, far_rows = ring_pieces(normed, "head")
+        project_piece = jnp.concatenate([normed, from_after, far_rows, from_before], axis=0)
         pairs = jnp.dot(
             project_piece, pair_weight, preferred_element_type=jnp.float32
         ).reshape(rows_all, local_kv, 2, HD)
@@ -203,8 +207,10 @@
         memory_read = state.astype(jnp.bfloat16).reshape(MEM, local_kv, group, HD)
         state = rates[segment] * state + (1.0 - rates[segment]) * written[segment]
         after_list = [state]
-        blocks = jnp.repeat(jnp.repeat(block_mask[segment], BLOCK, axis=0), BLOCK, axis=1)
-        allowed = causal & (docs[segment][:, None] == docs[segment][None, :]) & (blocks == 1)
+        block_of = origin // BLOCK
+        blocks = block_mask[segment][block_of[:, None], block_of[None, :]]
+        seg_docs = docs[segment][origin]
+        allowed = causal & (seg_docs[:, None] == seg_docs[None, :]) & (blocks == 1)
         slot_scores = (
             jnp.einsum("ikgd,mkgd->kgim", query[segment], slots, preferred_element_type=jnp.float32)
             * scale
@@ -230,8 +236,13 @@
         )
         outputs = result.reshape(SEG_LEN, cols_query).astype(jnp.bfloat16)
         stored.append(jnp.stack(after_list))
-        mixed = ring_scatter(
-            jnp.dot(outputs, out_weight, preferred_element_type=jnp.float32), "head"
+        mixed_parts = jnp.dot(outputs, out_weight, preferred_element_type=jnp.float32)
+        mixed = ring_scatter_parts(
+            mixed_parts[:piece_len],
+            mixed_parts[piece_len : 2 * piece_len],
+            mixed_parts[3 * piece_len :],
+            mixed_parts[2 * piece_len : 3 * piece_len],
+            "head",
         )
         middle = stream + mixed
         mlp_piece = rms_norm(middle, mlp_gain[layer])

time: 384 us -> 2570 us (6.69)
  local copies, waits for them, and re-layouts: 60.3 us -> 2260 us
    gather x0 -> x2, local copies, waits for them, and re-layouts: none -> 2190 us  [the longest x1 2190 us: body(): blocks = block_mask[segment][block_of[:, None], block_of[None, :]]]
    ppermute x16 -> x0, waiting for transfers between devices: 61.8 us -> none  [the longest x2 19.8 us: ring_gather(): from_before = lax.ppermute(piece, axis, ahead)]
    ppermute x16 -> x0, starting transfers between devices: 27.3 us -> none  [the longest x2 6.56 us: ring_gather(): far_bottom = lax.ppermute(from_after[half:], axis, behind)]
  transfers between devices with their start and end apart: 34 -> 34, of which waited for: 25 -> 25; matrix products, arithmetic and copies ran while one was open for 27% -> 90% of each run, Pallas kernels for 0% -> 0%
where the time goes in v9:
time: 2570 us; the launch traced here: 2560 us
  local copies, waits for them, and re-layouts  2260 us (88%)
  waiting for transfers between devices  141 us (5%)
  matrix products  63.3 us (2%)
  starting transfers between devices  51 us (2%)
  other arithmetic  38.8 us (2%)
    gather x1, local copies, waits for them, and re-layouts, body(): blocks = block_mask[segment][block_of[:, None], block_of[None, :]]  2190 us
  transfers between devices with their start and end apart: 34, of which 25 were waited for; matrix products, arithmetic and copies ran while one was open for 90% of the time, Pallas kernels for 0%

profile of v9, /device:TPU:0, one launch (start us, length us, event | category | flops | bytes accessed | tf_op | source)
XLA Modules:
  0.0 2564.6 jit_solution(13251626055390982639)
XLA Ops:
  21.8 7.1 collective-permute-done.1
  33.7 2188.7 %gather_fusion.1 = s32[262144]{0:T(1024)S(1)} fusion(s32[4,4]{1,0:T(4,128)S(1)} %bitcast.285, s32[262144]{0:T(1024)S(1)} %bitcast.286), kind=kCustom, calls=%fused_computation.1 | custom fusion | bytes 4194304 | tf_op jit(solution)/shard_map/gather | solution.py:211
  2223.3 3.3 collective-permute-start.3
  2239.9 3.5 gather_fusion
  2244.2 4.0 slice_bitcast_fusion.2
  2251.2 14.5 slice_bitcast_fusion
  2270.7 4.6 divide_convert_fusion.1
  2275.2 3.3 fusion.62
  2278.5 8.9 all-gather.7.cloned.1.call-done
  2302.2 6.4 collective-permute-done.4
  2312.7 9.8 collective-permute-done.7
  2322.4 3.5 collective-permute-done.5
  2328.7 10.0 collective-permute-done.9
  2355.5 4.3 collective-permute-done.12
  2360.9 3.8 collective-permute-start.15
  2371.4 6.6 collective-permute-done.13
  2379.5 3.2 collective-permute-start.16
  2382.9 10.1 collective-permute-done.17
  2397.8 3.3 collective-permute-start.19
  2414.2 4.1 copy.157
  2418.3 3.5 fusion.50
  2425.7 4.5 divide_convert_fusion
  2433.4 26.2 %all-gather.9.cloned.1.call-done = bf16[32,131,512]{2,1,0:T(8,128)(2,1)} async-done(((bf16[1,131,512]{2,1,0:T(8,128)(2,1)}), bf16[32,131,512]{2,1,0:T(8,128)(2,1)}) %all-gather.9.cloned.1.call-update) | async-done | bytes 4292624 | tf_op jit(solution)/shard_map/all_gather | solution.py:188
  2473.9 6.4 collective-permute-done.20
  2484.6 9.6 collective-permute-done.23
  2494.9 3.8 collective-permute-done.21
  2505.3 7.8 collective-permute-done.25
  2517.3 7.0 fusion.6
  2525.9 6.5 fusion.4
  2536.6 4.3 collective-permute-done.28
  2541.5 3.8 collective-permute-start.31
  2552.0 4.1 collective-permute-done.29
  (319 shorter events, 158.4 us)
Async XLA Ops:
  7.2 2280.2 %all-gather.7.cloned.1.call-start = ((), (), s32[]{:S(2)}) async-start(), calls=%async_computation | async-start | bytes 4595712 | tf_op jit(solution)/shard_map/all_gather | solution.py:188
  12.6 16.4 collective-permute-start.1
  14.6 2207.7 %collective-permute-start = (bf16[128,2048]{1,0:T(8,128)(2,1)}, bf16[128,2048]{1,0:T(8,128)(2,1)}, u32[]{:S(2)}, u32[]{:S(2)}) collective-permute-start(bf16[128,2048]{1,0:T(8,128)(2,1)} %get-tuple-element.23), channel_id=1, source_target_pairs={{0,3},{1,0},{2,1},{3,2},{4,7},{5,4},{6,5},{7,6},{8,11},{9,8},{10,9... | collective-permute-start | bytes 1572872 | tf_op jit(solution)/shard_map/ppermute | solution.py:64
  30.6 2197.9 %collective-permute-start.2 = (bf16[64,2048]{1,0:T(8,128)(2,1)}, bf16[64,2048]{1,0:T(8,128)(2,1)}, u32[]{:S(2)}, u32[]{:S(2)}) collective-permute-start(bf16[64,2048]{1,0:T(8,128)(2,1)} %slice.420), channel_id=1, source_target_pairs={{0,1},{1,2},{2,3},{3,0},{4,5},{5,6},{6,7},{7,4},{8,9},{9,10},{10,1... | collective-permute-start | bytes 786440 | tf_op jit(solution)/shard_map/ppermute | solution.py:65
  2223.3 8.0 collective-permute-start.3
  2239.0 220.5 %all-gather.9.cloned.1.call-start = ((), (), s32[]{:S(2)}) async-start(), calls=%async_computation.1 | async-start | bytes 4595712 | tf_op jit(solution)/shard_map/all_gather | solution.py:188
  2298.9 9.7 collective-permute-start.4
  2300.6 8.2 collective-permute-start.6
  2308.9 13.6 collective-permute-start.7
  2312.0 14.0 collective-permute-start.5
  2326.6 12.1 collective-permute-start.9
  2326.8 13.4 collective-permute-start.8
  2340.3 8.1 collective-permute-start.10
  2352.2 7.7 collective-permute-start.12
  2352.3 8.5 collective-permute-start.14
  2360.9 10.5 collective-permute-start.15
  2364.7 13.2 collective-permute-start.13
  2379.5 13.5 collective-permute-start.17
  2379.5 17.3 collective-permute-start.16
  2394.7 8.3 collective-permute-start.18
  2470.6 9.7 collective-permute-start.20
  2472.2 8.2 collective-permute-start.22
  2480.6 13.6 collective-permute-start.23
  2484.5 14.2 collective-permute-start.21
  2500.8 12.3 collective-permute-start.25
  2501.1 14.5 collective-permute-start.24
  2514.0 11.8 collective-permute-start.27
  2516.7 9.1 collective-permute-start.26
  2533.2 7.7 collective-permute-start.28
  2533.3 8.1 collective-permute-start.30
  2541.5 10.5 collective-permute-start.31
  2545.3 10.8 collective-permute-start.29
  (57 other events, 762.4 us)
Sparse Core Ops, SparseCore 0:
  2239.2 48.1 all-gather.6
  2413.4 46.0 all-gather.8

commit v10 on v9

--- a/solution.py
+++ b/solution.py
@@ -207,9 +207,10 @@
         memory_read = state.astype(jnp.bfloat16).reshape(MEM, local_kv, group, HD)
         state = rates[segment] * state + (1.0 - rates[segment]) * written[segment]
         after_list = [state]
-        block_of = origin // BLOCK
-        blocks = block_mask[segment][block_of[:, None], block_of[None, :]]
-        seg_docs = docs[segment][origin]
+        shift = -lax.axis_index("head") * piece_len
+        blocks = jnp.repeat(jnp.repeat(block_mask[segment], BLOCK, axis=0), BLOCK, axis=1)
+        blocks = jnp.roll(jnp.roll(blocks, shift, axis=0), shift, axis=1)
+        seg_docs = jnp.roll(docs[segment], shift)
         allowed = causal & (seg_docs[:, None] == seg_docs[None, :]) & (blocks == 1)
         slot_scores = (
             jnp.einsum("ikgd,mkgd->kgim", query[segment], slots, preferred_element_type=jnp.float32)

time: 2570 us -> 377 us (0.15)
  local copies, waits for them, and re-layouts: 2260 us -> 56.9 us
    gather x2 -> x0, local copies, waits for them, and re-layouts: 2190 us -> none  [the longest x1 2190 us: body(): blocks = block_mask[segment][block_of[:, None], block_of[None, :]]]
  transfers between devices with their start and end apart: 34 -> 34, of which waited for: 25 -> 26; matrix products, arithmetic and copies ran while one was open for 90% -> 26% of each run, Pallas kernels for 0% -> 0%
where the time goes in v10:
time: 377 us; the launch traced here: 372 us
  waiting for transfers between devices  149 us (40%)
  matrix products  62.8 us (17%)
  local copies, waits for them, and re-layouts  56.9 us (15%)
  starting transfers between devices  51 us (14%)
  other arithmetic  36.5 us (10%)
  between operations  15.8 us (4%)
    all_gather x2, waiting for transfers between devices, body(): gathered = lax.all_gather(payload, 'seg')  39.4 us
    dot_general x6, matrix products, feed_forward(): jnp.einsum('rd,dtf->rtf', rows, widening_matrix, preferred_element_type=j...  25.3 us
    ppermute x4, waiting for transfers between devices, ring_scatter_parts(): got_after = lax.ppermute(prev_part.astype(jnp.bfloat16), axis, behind)  24.6 us
    ppermute x4, waiting for transfers between devices, ring_scatter_parts(): sent_top = lax.ppermute(far[:half].astype(jnp.bfloat16), axis, ahead)  21.4 us
    ppermute x4, waiting for transfers between devices, ring_pieces(): from_before = lax.ppermute(piece, axis, ahead)  19.8 us
    ppermute x4, waiting for transfers between devices, ring_scatter_parts(): got_before = lax.ppermute(next_part.astype(jnp.bfloat16), axis, ahead)  18 us
    ppermute x4, waiting for transfers between devices, ring_pieces(): from_after = lax.ppermute(piece, axis, behind)  17.7 us
    squeeze x1, local copies, waits for them, and re-layouts, body(): w_gate_up[index]  14.6 us
  transfers between devices with their start and end apart: 34, of which 26 were waited for; matrix products, arithmetic and copies ran while one was open for 26% of the time, Pallas kernels for 0%

profile of v10, /device:TPU:0, one launch (start us, length us, event | category | flops | bytes accessed | tf_op | source)
XLA Modules:
  0.0 371.6 jit_solution(6163418166690787516)
XLA Ops:
  18.7 9.6 %collective-permute-done.1 = bf16[128,2048]{1,0:T(8,128)(2,1)} collective-permute-done((bf16[128,2048]{1,0:T(8,128)(2,1)}, bf16[128,2048]{1,0:T(8,128)(2,1)}, u32[]{:S(2)}, u32[]{:S(2)}) %collective-permute-start.1) | collective-permute-done | bytes 524320 | tf_op jit(solution)/shard_map/ppermute | solution.py:63
  31.1 3.3 collective-permute-start.3
  47.0 3.8 %slice_bitcast_fusion.2 = (bf16[512,2048]{0,1:T(8,128)(2,1)}, bf16[512,2048]{0,1:T(8,128)(2,1)S(1)}) fusion(bf16[2,2048,512]{2,1,0:T(8,128)(2,1)} %param.27), kind=kLoop, calls=%fused_computation.73 | loop fusion | bytes 8388608 | tf_op jit(solution)/shard_map/dot_general | solution.py:157
  54.3 14.6 %slice_bitcast_fusion = (bf16[2048,2,1024]{2,1,0:T(2,128)(2,1)}, bf16[2048,2,1024]{2,1,0:T(2,128)(2,1)}) fusion(bf16[2,2048,2,1024]{3,2,1,0:T(2,128)(2,1)} %param.30), kind=kLoop, calls=%fused_computation.9 | loop fusion | bytes 33554432 | tf_op jit(solution)/shard_map/squeeze | solution.py:204
  73.9 4.6 %divide_convert_fusion.1 = bf16[2,4,512,640]{2,3,1,0:T(8,128)(2,1)} fusion(f32[2,4,512,512]{2,3,1,0:T(8,128)S(1)} %get-tuple-element.90, f32[2,4,512,128]{2,3,1,0:T(8,128)} %copy-done.1, f32[2,4,512]{2,1,0:T(4,128)S(1)} %fusion.3, f32[2,4,512]{2,1,0:T(4,128)S(1)} %reduce_max.61), kind=kLoop, calls=%fused_computation.5 | loop fusion | flops 10485760 | bytes 15761408 | tf_op jit(solution)/shard_map/convert_element_type | solution.py:231
  81.6 13.3 %all-gather.7.cloned.1.call-done = bf16[32,131,512]{2,1,0:T(8,128)(2,1)} async-done(((bf16[1,131,512]{2,1,0:T(8,128)(2,1)}), bf16[32,131,512]{2,1,0:T(8,128)(2,1)}) %all-gather.7.cloned.1.call-update) | async-done | bytes 4292624 | tf_op jit(solution)/shard_map/all_gather | solution.py:188
  109.7 6.4 %collective-permute-done.4 = bf16[64,2048]{1,0:T(8,128)(2,1)S(1)} collective-permute-done((bf16[64,2048]{1,0:T(8,128)(2,1)S(1)}, bf16[64,2048]{1,0:T(8,128)(2,1)S(1)}, u32[]{:S(2)}, u32[]{:S(2)}) %collective-permute-start.4) | collective-permute-done | bytes 262176 | tf_op jit(solution)/shard_map/ppermute | solution.py:75
  120.2 9.8 %collective-permute-done.7 = bf16[128,2048]{1,0:T(8,128)(2,1)S(1)} collective-permute-done((bf16[128,2048]{1,0:T(8,128)(2,1)S(1)}, bf16[128,2048]{1,0:T(8,128)(2,1)S(1)}, u32[]{:S(2)}, u32[]{:S(2)}) %collective-permute-start.7) | collective-permute-done | bytes 524320 | tf_op jit(solution)/shard_map/ppermute | solution.py:80
  129.9 3.5 collective-permute-done.5
  136.2 10.0 %collective-permute-done.9 = bf16[128,2048]{1,0:T(8,128)(2,1)S(1)} collective-permute-done((bf16[128,2048]{1,0:T(8,128)(2,1)S(1)}, bf16[128,2048]{1,0:T(8,128)(2,1)S(1)}, u32[]{:S(2)}, u32[]{:S(2)}) %collective-permute-start.9) | collective-permute-done | bytes 524320 | tf_op jit(solution)/shard_map/ppermute | solution.py:64
  159.3 3.2 collective-permute-start.14
  162.6 4.3 %collective-permute-done.12 = bf16[64,2048]{1,0:T(8,128)(2,1)S(1)} collective-permute-done((bf16[64,2048]{1,0:T(8,128)(2,1)S(1)}, bf16[64,2048]{1,0:T(8,128)(2,1)S(1)}, u32[]{:S(2)}, u32[]{:S(2)}) %collective-permute-start.12) | collective-permute-done | bytes 262176 | tf_op jit(solution)/shard_map/ppermute | solution.py:75
  167.9 3.8 %collective-permute-start.15 = (bf16[128,2048]{1,0:T(8,128)(2,1)S(1)}, bf16[128,2048]{1,0:T(8,128)(2,1)S(1)}, u32[]{:S(2)}, u32[]{:S(2)}) collective-permute-start(bf16[128,2048]{1,0:T(8,128)(2,1)S(1)} %pad_maximum_fusion.4), channel_id=1, source_target_pairs={{0,3},{1,0},{2,1},{3,2},{4,7},{5,4},{6,5},{7,6},{8,11},{9,8},{10,9... | collective-permute-start | bytes 1572872 | tf_op jit(solution)/shard_map/ppermute | solution.py:80
  178.4 6.6 %collective-permute-done.13 = bf16[128,2048]{1,0:T(8,128)(2,1)S(1)} collective-permute-done((bf16[128,2048]{1,0:T(8,128)(2,1)S(1)}, bf16[128,2048]{1,0:T(8,128)(2,1)S(1)}, u32[]{:S(2)}, u32[]{:S(2)}) %collective-permute-start.13) | collective-permute-done | bytes 524320 | tf_op jit(solution)/shard_map/ppermute | solution.py:79
  186.6 3.2 collective-permute-start.16
  189.9 10.1 %collective-permute-done.17 = bf16[128,2048]{1,0:T(8,128)(2,1)} collective-permute-done((bf16[128,2048]{1,0:T(8,128)(2,1)}, bf16[128,2048]{1,0:T(8,128)(2,1)}, u32[]{:S(2)}, u32[]{:S(2)}) %collective-permute-start.17) | collective-permute-done | bytes 524320 | tf_op jit(solution)/shard_map/ppermute | solution.py:63
  204.9 3.3 collective-permute-start.19
  221.2 4.1 %copy.158 = bf16[512,2048]{1,0:T(8,128)(2,1)} copy(bf16[512,2048]{0,1:T(8,128)(2,1)} %get-tuple-element.31) | data formatting | bytes 4194304 | tf_op jit(solution)/shard_map/dot_general | solution.py:157
  225.3 3.5 fusion.50
  232.7 4.6 %divide_convert_fusion = bf16[2,4,512,640]{2,3,1,0:T(8,128)(2,1)} fusion(f32[2,4,512,512]{2,3,1,0:T(8,128)S(1)} %get-tuple-element.98, f32[2,4,512,128]{2,3,1,0:T(8,128)} %copy-done, f32[2,4,512]{2,1,0:T(4,128)S(1)} %fusion.2, f32[2,4,512]{2,1,0:T(4,128)S(1)} %reduce_max.65), kind=kLoop, calls=%fused_computation.4 | loop fusion | flops 10485760 | bytes 15761408 | tf_op jit(solution)/shard_map/convert_element_type | solution.py:231
  237.3 3.1 fusion.65
  240.5 26.2 %all-gather.9.cloned.1.call-done = bf16[32,131,512]{2,1,0:T(8,128)(2,1)} async-done(((bf16[1,131,512]{2,1,0:T(8,128)(2,1)}), bf16[32,131,512]{2,1,0:T(8,128)(2,1)}) %all-gather.9.cloned.1.call-update) | async-done | bytes 4292624 | tf_op jit(solution)/shard_map/all_gather | solution.py:188
  280.9 6.4 %collective-permute-done.20 = bf16[64,2048]{1,0:T(8,128)(2,1)S(1)} collective-permute-done((bf16[64,2048]{1,0:T(8,128)(2,1)S(1)}, bf16[64,2048]{1,0:T(8,128)(2,1)S(1)}, u32[]{:S(2)}, u32[]{:S(2)}) %collective-permute-start.20) | collective-permute-done | bytes 262176 | tf_op jit(solution)/shard_map/ppermute | solution.py:75
  291.6 9.6 %collective-permute-done.23 = bf16[128,2048]{1,0:T(8,128)(2,1)S(1)} collective-permute-done((bf16[128,2048]{1,0:T(8,128)(2,1)S(1)}, bf16[128,2048]{1,0:T(8,128)(2,1)S(1)}, u32[]{:S(2)}, u32[]{:S(2)}) %collective-permute-start.23) | collective-permute-done | bytes 524320 | tf_op jit(solution)/shard_map/ppermute | solution.py:80
  301.9 3.8 %collective-permute-done.21 = bf16[128,2048]{1,0:T(8,128)(2,1)} collective-permute-done((bf16[128,2048]{1,0:T(8,128)(2,1)}, bf16[128,2048]{1,0:T(8,128)(2,1)}, u32[]{:S(2)}, u32[]{:S(2)}) %collective-permute-start.21) | collective-permute-done | bytes 524320 | tf_op jit(solution)/shard_map/ppermute | solution.py:79
  312.3 7.8 %collective-permute-done.25 = bf16[128,2048]{1,0:T(8,128)(2,1)} collective-permute-done((bf16[128,2048]{1,0:T(8,128)(2,1)S(1)}, bf16[128,2048]{1,0:T(8,128)(2,1)}, u32[]{:S(2)}, u32[]{:S(2)}) %collective-permute-start.25) | collective-permute-done | bytes 524320 | tf_op jit(solution)/shard_map/ppermute | solution.py:64
  324.4 7.1 %fusion.6 = f32[256,2,1024]{2,0,1:T(8,128)S(1)} fusion(bf16[2048,2,1024]{2,1,0:T(2,128)(2,1)} %get-tuple-element.10, bf16[128,2048]{1,0:T(8,128)(2,1)} %collective-permute-done.25, bf16[128,2048]{1,0:T(8,128)(2,1)} %collective-permute-done.24), kind=kOutput, calls=%fused_computation.16 | convolution fusion | flops 2149580800 | bytes 11534336 | tf_op jit(solution)/shard_map/rd,dtf->rtf/dot_general | solution.py:85
  332.9 6.5 %fusion.4 = f32[128,2,1024]{2,0,1:T(8,128)S(1)} fusion(bf16[2048,2,1024]{2,1,0:T(2,128)(2,1)} %get-tuple-element.10, bf16[64,2048]{1,0:T(8,128)(2,1)S(1)} %collective-permute-done.27, bf16[64,2048]{1,0:T(8,128)(2,1)S(1)} %collective-permute-done.26), kind=kOutput, calls=%fused_computation.14 | convolution fusion | flops 1074790400 | bytes 9961472 | tf_op jit(solution)/shard_map/rd,dtf->rtf/dot_general | solution.py:85
  340.3 3.2 collective-permute-start.30
  343.6 4.3 %collective-permute-done.28 = bf16[64,2048]{1,0:T(8,128)(2,1)S(1)} collective-permute-done((bf16[64,2048]{1,0:T(8,128)(2,1)S(1)}, bf16[64,2048]{1,0:T(8,128)(2,1)S(1)}, u32[]{:S(2)}, u32[]{:S(2)}) %collective-permute-start.28) | collective-permute-done | bytes 262176 | tf_op jit(solution)/shard_map/ppermute | solution.py:75
  348.5 3.8 %collective-permute-start.31 = (bf16[128,2048]{1,0:T(8,128)(2,1)S(1)}, bf16[128,2048]{1,0:T(8,128)(2,1)S(1)}, u32[]{:S(2)}, u32[]{:S(2)}) collective-permute-start(bf16[128,2048]{1,0:T(8,128)(2,1)S(1)} %pad_maximum_fusion.9), channel_id=1, source_target_pairs={{0,3},{1,0},{2,1},{3,2},{4,7},{5,4},{6,5},{7,6},{8,11},{9,8},{10,9... | collective-permute-start | bytes 1572872 | tf_op jit(solution)/shard_map/ppermute | solution.py:80
  359.0 4.1 %collective-permute-done.29 = bf16[128,2048]{1,0:T(8,128)(2,1)S(1)} collective-permute-done((bf16[128,2048]{1,0:T(8,128)(2,1)S(1)}, bf16[128,2048]{1,0:T(8,128)(2,1)S(1)}, u32[]{:S(2)}, u32[]{:S(2)}) %collective-permute-start.29) | collective-permute-done | bytes 524320 | tf_op jit(solution)/shard_map/ppermute | solution.py:79
  (284 shorter events, 144.4 us)
Async XLA Ops:
  7.2 87.6 %all-gather.7.cloned.1.call-start = ((), (), s32[]{:S(2)}) async-start(), calls=%async_computation | async-start | bytes 4595712 | tf_op jit(solution)/shard_map/all_gather | solution.py:188
  11.9 16.4 %collective-permute-start.1 = (bf16[128,2048]{1,0:T(8,128)(2,1)}, bf16[128,2048]{1,0:T(8,128)(2,1)}, u32[]{:S(2)}, u32[]{:S(2)}) collective-permute-start(bf16[128,2048]{1,0:T(8,128)(2,1)} %get-tuple-element.26), channel_id=1, source_target_pairs={{0,1},{1,2},{2,3},{3,0},{4,5},{5,6},{6,7},{7,4},{8,9},{9,10},{10,1... | collective-permute-start | bytes 1572872 | tf_op jit(solution)/shard_map/ppermute | solution.py:63
  14.0 16.2 %collective-permute-start = (bf16[128,2048]{1,0:T(8,128)(2,1)}, bf16[128,2048]{1,0:T(8,128)(2,1)}, u32[]{:S(2)}, u32[]{:S(2)}) collective-permute-start(bf16[128,2048]{1,0:T(8,128)(2,1)} %get-tuple-element.26), channel_id=1, source_target_pairs={{0,3},{1,0},{2,1},{3,2},{4,7},{5,4},{6,5},{7,6},{8,11},{9,8},{10,9... | collective-permute-start | bytes 1572872 | tf_op jit(solution)/shard_map/ppermute | solution.py:64
  29.3 8.8 %collective-permute-start.2 = (bf16[64,2048]{1,0:T(8,128)(2,1)S(1)}, bf16[64,2048]{1,0:T(8,128)(2,1)S(1)}, u32[]{:S(2)}, u32[]{:S(2)}) collective-permute-start(bf16[64,2048]{1,0:T(8,128)(2,1)S(1)} %slice.416), channel_id=1, source_target_pairs={{0,1},{1,2},{2,3},{3,0},{4,5},{5,6},{6,7},{7,4},{8,9},{9,10},{10,1... | collective-permute-start | bytes 786440 | tf_op jit(solution)/shard_map/ppermute | solution.py:65
  31.1 8.0 %collective-permute-start.3 = (bf16[64,2048]{1,0:T(8,128)(2,1)S(1)}, bf16[64,2048]{1,0:T(8,128)(2,1)S(1)}, u32[]{:S(2)}, u32[]{:S(2)}) collective-permute-start(bf16[64,2048]{1,0:T(8,128)(2,1)S(1)} %slice.417), channel_id=1, source_target_pairs={{0,3},{1,0},{2,1},{3,2},{4,7},{5,4},{6,5},{7,6},{8,11},{9,8},{10,9... | collective-permute-start | bytes 786440 | tf_op jit(solution)/shard_map/ppermute | solution.py:66
  46.5 220.2 %all-gather.9.cloned.1.call-start = ((), (), s32[]{:S(2)}) async-start(), calls=%async_computation.1 | async-start | bytes 4595712 | tf_op jit(solution)/shard_map/all_gather | solution.py:188
  106.0 10.1 %collective-permute-start.4 = (bf16[64,2048]{1,0:T(8,128)(2,1)S(1)}, bf16[64,2048]{1,0:T(8,128)(2,1)S(1)}, u32[]{:S(2)}, u32[]{:S(2)}) collective-permute-start(bf16[64,2048]{1,0:T(8,128)(2,1)S(1)} %get-tuple-element.45), channel_id=1, source_target_pairs={{0,1},{1,2},{2,3},{3,0},{4,5},{5,6},{6,7},{7,4},{8,9},{9,10},{10,1... | collective-permute-start | bytes 786440 | tf_op jit(solution)/shard_map/ppermute | solution.py:75
  108.0 8.2 %collective-permute-start.6 = (bf16[64,2048]{1,0:T(8,128)(2,1)S(1)}, bf16[64,2048]{1,0:T(8,128)(2,1)S(1)}, u32[]{:S(2)}, u32[]{:S(2)}) collective-permute-start(bf16[64,2048]{1,0:T(8,128)(2,1)S(1)} %get-tuple-element.46), channel_id=1, source_target_pairs={{0,3},{1,0},{2,1},{3,2},{4,7},{5,4},{6,5},{7,6},{8,11},{9,8},{10,9... | collective-permute-start | bytes 786440 | tf_op jit(solution)/shard_map/ppermute | solution.py:76
  116.4 13.5 %collective-permute-start.7 = (bf16[128,2048]{1,0:T(8,128)(2,1)S(1)}, bf16[128,2048]{1,0:T(8,128)(2,1)S(1)}, u32[]{:S(2)}, u32[]{:S(2)}) collective-permute-start(bf16[128,2048]{1,0:T(8,128)(2,1)S(1)} %pad_maximum_fusion.2), channel_id=1, source_target_pairs={{0,3},{1,0},{2,1},{3,2},{4,7},{5,4},{6,5},{7,6},{8,11},{9,8},{10,9... | collective-permute-start | bytes 1572872 | tf_op jit(solution)/shard_map/ppermute | solution.py:80
  119.5 14.0 %collective-permute-start.5 = (bf16[128,2048]{1,0:T(8,128)(2,1)S(1)}, bf16[128,2048]{1,0:T(8,128)(2,1)S(1)}, u32[]{:S(2)}, u32[]{:S(2)}) collective-permute-start(bf16[128,2048]{1,0:T(8,128)(2,1)S(1)} %pad_maximum_fusion.1), channel_id=1, source_target_pairs={{0,1},{1,2},{2,3},{3,0},{4,5},{5,6},{6,7},{7,4},{8,9},{9,10},{10,1... | collective-permute-start | bytes 1572872 | tf_op jit(solution)/shard_map/ppermute | solution.py:79
  134.1 12.1 %collective-permute-start.9 = (bf16[128,2048]{1,0:T(8,128)(2,1)S(1)}, bf16[128,2048]{1,0:T(8,128)(2,1)S(1)}, u32[]{:S(2)}, u32[]{:S(2)}) collective-permute-start(bf16[128,2048]{1,0:T(8,128)(2,1)S(1)} %multiply_convert_fusion.2), channel_id=1, source_target_pairs={{0,3},{1,0},{2,1},{3,2},{4,7},{5,4},{6,5},{7,6},{8,11},{9,8},{10,9... | collective-permute-start | bytes 1572872 | tf_op jit(solution)/shard_map/ppermute | solution.py:64
  134.3 13.4 %collective-permute-start.8 = (bf16[128,2048]{1,0:T(8,128)(2,1)S(1)}, bf16[128,2048]{1,0:T(8,128)(2,1)S(1)}, u32[]{:S(2)}, u32[]{:S(2)}) collective-permute-start(bf16[128,2048]{1,0:T(8,128)(2,1)S(1)} %multiply_convert_fusion.2), channel_id=1, source_target_pairs={{0,1},{1,2},{2,3},{3,0},{4,5},{5,6},{6,7},{7,4},{8,9},{9,10},{10,1... | collective-permute-start | bytes 1572872 | tf_op jit(solution)/shard_map/ppermute | solution.py:63
  147.8 7.7 %collective-permute-start.10 = (bf16[64,2048]{1,0:T(8,128)(2,1)S(1)}, bf16[64,2048]{1,0:T(8,128)(2,1)S(1)}, u32[]{:S(2)}, u32[]{:S(2)}) collective-permute-start(bf16[64,2048]{1,0:T(8,128)(2,1)S(1)} %slice.442), channel_id=1, source_target_pairs={{0,1},{1,2},{2,3},{3,0},{4,5},{5,6},{6,7},{7,4},{8,9},{9,10},{10,1... | collective-permute-start | bytes 786440 | tf_op jit(solution)/shard_map/ppermute | solution.py:65
  159.2 7.7 %collective-permute-start.12 = (bf16[64,2048]{1,0:T(8,128)(2,1)S(1)}, bf16[64,2048]{1,0:T(8,128)(2,1)S(1)}, u32[]{:S(2)}, u32[]{:S(2)}) collective-permute-start(bf16[64,2048]{1,0:T(8,128)(2,1)S(1)} %get-tuple-element.59), channel_id=1, source_target_pairs={{0,1},{1,2},{2,3},{3,0},{4,5},{5,6},{6,7},{7,4},{8,9},{9,10},{10,1... | collective-permute-start | bytes 786440 | tf_op jit(solution)/shard_map/ppermute | solution.py:75
  159.3 8.5 %collective-permute-start.14 = (bf16[64,2048]{1,0:T(8,128)(2,1)S(1)}, bf16[64,2048]{1,0:T(8,128)(2,1)S(1)}, u32[]{:S(2)}, u32[]{:S(2)}) collective-permute-start(bf16[64,2048]{1,0:T(8,128)(2,1)S(1)} %get-tuple-element.60), channel_id=1, source_target_pairs={{0,3},{1,0},{2,1},{3,2},{4,7},{5,4},{6,5},{7,6},{8,11},{9,8},{10,9... | collective-permute-start | bytes 786440 | tf_op jit(solution)/shard_map/ppermute | solution.py:76
  167.9 10.5 %collective-permute-start.15 = (bf16[128,2048]{1,0:T(8,128)(2,1)S(1)}, bf16[128,2048]{1,0:T(8,128)(2,1)S(1)}, u32[]{:S(2)}, u32[]{:S(2)}) collective-permute-start(bf16[128,2048]{1,0:T(8,128)(2,1)S(1)} %pad_maximum_fusion.4), channel_id=1, source_target_pairs={{0,3},{1,0},{2,1},{3,2},{4,7},{5,4},{6,5},{7,6},{8,11},{9,8},{10,9... | collective-permute-start | bytes 1572872 | tf_op jit(solution)/shard_map/ppermute | solution.py:80
  171.8 13.2 %collective-permute-start.13 = (bf16[128,2048]{1,0:T(8,128)(2,1)S(1)}, bf16[128,2048]{1,0:T(8,128)(2,1)S(1)}, u32[]{:S(2)}, u32[]{:S(2)}) collective-permute-start(bf16[128,2048]{1,0:T(8,128)(2,1)S(1)} %pad_maximum_fusion.3), channel_id=1, source_target_pairs={{0,1},{1,2},{2,3},{3,0},{4,5},{5,6},{6,7},{7,4},{8,9},{9,10},{10,1... | collective-permute-start | bytes 1572872 | tf_op jit(solution)/shard_map/ppermute | solution.py:79
  186.6 13.5 %collective-permute-start.17 = (bf16[128,2048]{1,0:T(8,128)(2,1)}, bf16[128,2048]{1,0:T(8,128)(2,1)}, u32[]{:S(2)}, u32[]{:S(2)}) collective-permute-start(bf16[128,2048]{1,0:T(8,128)(2,1)} %get-tuple-element.20), channel_id=1, source_target_pairs={{0,1},{1,2},{2,3},{3,0},{4,5},{5,6},{6,7},{7,4},{8,9},{9,10},{10,1... | collective-permute-start | bytes 1572872 | tf_op jit(solution)/shard_map/ppermute | solution.py:63
  186.6 17.3 %collective-permute-start.16 = (bf16[128,2048]{1,0:T(8,128)(2,1)}, bf16[128,2048]{1,0:T(8,128)(2,1)}, u32[]{:S(2)}, u32[]{:S(2)}) collective-permute-start(bf16[128,2048]{1,0:T(8,128)(2,1)} %get-tuple-element.20), channel_id=1, source_target_pairs={{0,3},{1,0},{2,1},{3,2},{4,7},{5,4},{6,5},{7,6},{8,11},{9,8},{10,9... | collective-permute-start | bytes 1572872 | tf_op jit(solution)/shard_map/ppermute | solution.py:64
  201.8 8.3 %collective-permute-start.18 = (bf16[64,2048]{1,0:T(8,128)(2,1)}, bf16[64,2048]{1,0:T(8,128)(2,1)S(1)}, u32[]{:S(2)}, u32[]{:S(2)}) collective-permute-start(bf16[64,2048]{1,0:T(8,128)(2,1)} %slice.451), channel_id=1, source_target_pairs={{0,1},{1,2},{2,3},{3,0},{4,5},{5,6},{6,7},{7,4},{8,9},{9,10},{10,1... | collective-permute-start | bytes 786440 | tf_op jit(solution)/shard_map/ppermute | solution.py:65
  277.6 9.7 %collective-permute-start.20 = (bf16[64,2048]{1,0:T(8,128)(2,1)S(1)}, bf16[64,2048]{1,0:T(8,128)(2,1)S(1)}, u32[]{:S(2)}, u32[]{:S(2)}) collective-permute-start(bf16[64,2048]{1,0:T(8,128)(2,1)S(1)} %get-tuple-element.37), channel_id=1, source_target_pairs={{0,1},{1,2},{2,3},{3,0},{4,5},{5,6},{6,7},{7,4},{8,9},{9,10},{10,1... | collective-permute-start | bytes 786440 | tf_op jit(solution)/shard_map/ppermute | solution.py:75
  279.2 8.2 %collective-permute-start.22 = (bf16[64,2048]{1,0:T(8,128)(2,1)S(1)}, bf16[64,2048]{1,0:T(8,128)(2,1)S(1)}, u32[]{:S(2)}, u32[]{:S(2)}) collective-permute-start(bf16[64,2048]{1,0:T(8,128)(2,1)S(1)} %get-tuple-element.38), channel_id=1, source_target_pairs={{0,3},{1,0},{2,1},{3,2},{4,7},{5,4},{6,5},{7,6},{8,11},{9,8},{10,9... | collective-permute-start | bytes 786440 | tf_op jit(solution)/shard_map/ppermute | solution.py:76
  287.6 13.5 %collective-permute-start.23 = (bf16[128,2048]{1,0:T(8,128)(2,1)S(1)}, bf16[128,2048]{1,0:T(8,128)(2,1)S(1)}, u32[]{:S(2)}, u32[]{:S(2)}) collective-permute-start(bf16[128,2048]{1,0:T(8,128)(2,1)S(1)} %pad_maximum_fusion.7), channel_id=1, source_target_pairs={{0,3},{1,0},{2,1},{3,2},{4,7},{5,4},{6,5},{7,6},{8,11},{9,8},{10,9... | collective-permute-start | bytes 1572872 | tf_op jit(solution)/shard_map/ppermute | solution.py:80
  291.5 14.2 %collective-permute-start.21 = (bf16[128,2048]{1,0:T(8,128)(2,1)}, bf16[128,2048]{1,0:T(8,128)(2,1)}, u32[]{:S(2)}, u32[]{:S(2)}) collective-permute-start(bf16[128,2048]{1,0:T(8,128)(2,1)} %pad_maximum_fusion.6), channel_id=1, source_target_pairs={{0,1},{1,2},{2,3},{3,0},{4,5},{5,6},{6,7},{7,4},{8,9},{9,10},{10,1... | collective-permute-start | bytes 1572872 | tf_op jit(solution)/shard_map/ppermute | solution.py:79
  307.8 12.3 %collective-permute-start.25 = (bf16[128,2048]{1,0:T(8,128)(2,1)S(1)}, bf16[128,2048]{1,0:T(8,128)(2,1)}, u32[]{:S(2)}, u32[]{:S(2)}) collective-permute-start(bf16[128,2048]{1,0:T(8,128)(2,1)S(1)} %multiply_convert_fusion), channel_id=1, source_target_pairs={{0,3},{1,0},{2,1},{3,2},{4,7},{5,4},{6,5},{7,6},{8,11},{9,8},{10,9... | collective-permute-start | bytes 1572872 | tf_op jit(solution)/shard_map/ppermute | solution.py:64
  308.2 14.5 %collective-permute-start.24 = (bf16[128,2048]{1,0:T(8,128)(2,1)S(1)}, bf16[128,2048]{1,0:T(8,128)(2,1)}, u32[]{:S(2)}, u32[]{:S(2)}) collective-permute-start(bf16[128,2048]{1,0:T(8,128)(2,1)S(1)} %multiply_convert_fusion), channel_id=1, source_target_pairs={{0,1},{1,2},{2,3},{3,0},{4,5},{5,6},{6,7},{7,4},{8,9},{9,10},{10,1... | collective-permute-start | bytes 1572872 | tf_op jit(solution)/shard_map/ppermute | solution.py:63
  321.1 11.8 %collective-permute-start.27 = (bf16[64,2048]{1,0:T(8,128)(2,1)S(1)}, bf16[64,2048]{1,0:T(8,128)(2,1)S(1)}, u32[]{:S(2)}, u32[]{:S(2)}) collective-permute-start(bf16[64,2048]{1,0:T(8,128)(2,1)S(1)} %slice.478), channel_id=1, source_target_pairs={{0,3},{1,0},{2,1},{3,2},{4,7},{5,4},{6,5},{7,6},{8,11},{9,8},{10,9... | collective-permute-start | bytes 786440 | tf_op jit(solution)/shard_map/ppermute | solution.py:66
  323.8 9.1 %collective-permute-start.26 = (bf16[64,2048]{1,0:T(8,128)(2,1)S(1)}, bf16[64,2048]{1,0:T(8,128)(2,1)S(1)}, u32[]{:S(2)}, u32[]{:S(2)}) collective-permute-start(bf16[64,2048]{1,0:T(8,128)(2,1)S(1)} %slice.477), channel_id=1, source_target_pairs={{0,1},{1,2},{2,3},{3,0},{4,5},{5,6},{6,7},{7,4},{8,9},{9,10},{10,1... | collective-permute-start | bytes 786440 | tf_op jit(solution)/shard_map/ppermute | solution.py:65
  340.2 7.7 %collective-permute-start.28 = (bf16[64,2048]{1,0:T(8,128)(2,1)S(1)}, bf16[64,2048]{1,0:T(8,128)(2,1)S(1)}, u32[]{:S(2)}, u32[]{:S(2)}) collective-permute-start(bf16[64,2048]{1,0:T(8,128)(2,1)S(1)} %get-tuple-element.57), channel_id=1, source_target_pairs={{0,1},{1,2},{2,3},{3,0},{4,5},{5,6},{6,7},{7,4},{8,9},{9,10},{10,1... | collective-permute-start | bytes 786440 | tf_op jit(solution)/shard_map/ppermute | solution.py:75
  340.3 8.1 %collective-permute-start.30 = (bf16[64,2048]{1,0:T(8,128)(2,1)S(1)}, bf16[64,2048]{1,0:T(8,128)(2,1)S(1)}, u32[]{:S(2)}, u32[]{:S(2)}) collective-permute-start(bf16[64,2048]{1,0:T(8,128)(2,1)S(1)} %get-tuple-element.58), channel_id=1, source_target_pairs={{0,3},{1,0},{2,1},{3,2},{4,7},{5,4},{6,5},{7,6},{8,11},{9,8},{10,9... | collective-permute-start | bytes 786440 | tf_op jit(solution)/shard_map/ppermute | solution.py:76
  348.5 10.5 %collective-permute-start.31 = (bf16[128,2048]{1,0:T(8,128)(2,1)S(1)}, bf16[128,2048]{1,0:T(8,128)(2,1)S(1)}, u32[]{:S(2)}, u32[]{:S(2)}) collective-permute-start(bf16[128,2048]{1,0:T(8,128)(2,1)S(1)} %pad_maximum_fusion.9), channel_id=1, source_target_pairs={{0,3},{1,0},{2,1},{3,2},{4,7},{5,4},{6,5},{7,6},{8,11},{9,8},{10,9... | collective-permute-start | bytes 1572872 | tf_op jit(solution)/shard_map/ppermute | solution.py:80
  352.3 10.8 %collective-permute-start.29 = (bf16[128,2048]{1,0:T(8,128)(2,1)S(1)}, bf16[128,2048]{1,0:T(8,128)(2,1)S(1)}, u32[]{:S(2)}, u32[]{:S(2)}) collective-permute-start(bf16[128,2048]{1,0:T(8,128)(2,1)S(1)} %pad_maximum_fusion.8), channel_id=1, source_target_pairs={{0,1},{1,2},{2,3},{3,0},{4,5},{5,6},{6,7},{7,4},{8,9},{9,10},{10,1... | collective-permute-start | bytes 1572872 | tf_op jit(solution)/shard_map/ppermute | solution.py:79
  (41 other events, 591.9 us)
Sparse Core Ops, SparseCore 0:
  46.6 48.1 all-gather.6
  220.5 46.1 all-gather.8

commit v11 on v10

--- a/solution.py
+++ b/solution.py
@@ -148,8 +148,16 @@
         normed = rms_norm(stream, attn_gain[layer])
         from_before, from_after, far_rows = ring_pieces(normed, "head")
         project_piece = jnp.concatenate([normed, from_after, far_rows, from_before], axis=0)
-        pairs = jnp.dot(
-            project_piece, pair_weight, preferred_element_type=jnp.float32
+        pairs = jnp.concatenate(
+            [
+                jnp.dot(normed, pair_weight, preferred_element_type=jnp.float32),
+                jnp.dot(
+                    jnp.concatenate([from_after, far_rows, from_before], axis=0),
+                    pair_weight,
+                    preferred_element_type=jnp.float32,
+                ),
+            ],
+            axis=0,
         ).reshape(rows_all, local_kv, 2, HD)
         lookup_vectors = rotate(pairs[:, :, 0], cosine, sine).astype(jnp.bfloat16)
         values = pairs[:, :, 1].astype(jnp.bfloat16)

time: 377 us -> 363 us (0.963)
  local copies, waits for them, and re-layouts: 56.9 us -> 42.9 us
    all_gather x2, waiting for transfers between devices: 39.4 us -> 34.5 us  [body(): gathered = lax.all_gather(payload, 'seg')]
    ppermute x4, waiting for transfers between devices: 4.47 us -> 9.1 us  [ring_pieces(): far_top = lax.ppermute(from_before[:half], axis, ahead)]
    unnamed x85 -> x113, local copies, waits for them, and re-layouts: 8.04 us -> 5.17 us
  transfers between devices with their start and end apart: 34 -> 34, of which waited for: 26 -> 25; matrix products, arithmetic and copies ran while one was open for 26% -> 25% of each run, Pallas kernels for 0% -> 0%
where the time goes in v11:
time: 363 us; the launch traced here: 358 us
  waiting for transfers between devices  147 us (40%)
  matrix products  64.5 us (18%)
  starting transfers between devices  50.8 us (14%)
  local copies, waits for them, and re-layouts  42.9 us (12%)
  other arithmetic  36.3 us (10%)
  between operations  16 us (4%)
    all_gather x2, waiting for transfers between devices, body(): gathered = lax.all_gather(payload, 'seg')  34.5 us
    dot_general x6, matrix products, feed_forward(): jnp.einsum('rd,dtf->rtf', rows, widening_matrix, preferred_element_type=j...  25.3 us
    ppermute x4, waiting for transfers between devices, ring_scatter_parts(): got_after = lax.ppermute(prev_part.astype(jnp.bfloat16), axis, behind)  24.3 us
    ppermute x4, waiting for transfers between devices, ring_scatter_parts(): sent_top = lax.ppermute(far[:half].astype(jnp.bfloat16), axis, ahead)  21.4 us
    ppermute x4, waiting for transfers between devices, ring_pieces(): from_before = lax.ppermute(piece, axis, ahead)  20.4 us
    ppermute x4, waiting for transfers between devices, ring_scatter_parts(): got_before = lax.ppermute(next_part.astype(jnp.bfloat16), axis, ahead)  18.2 us
    ppermute x4, waiting for transfers between devices, ring_pieces(): from_after = lax.ppermute(piece, axis, behind)  17.7 us
    squeeze x1, local copies, waits for them, and re-layouts, body(): w_gate_up[index]  14.4 us
  transfers between devices with their start and end apart: 34, of which 25 were waited for; matrix products, arithmetic and copies ran while one was open for 25% of the time, Pallas kernels for 0%

profile of v11, /device:TPU:0, one launch (start us, length us, event | category | flops | bytes accessed | tf_op | source)
XLA Modules:
  0.0 357.7 jit_solution(5874760493000677481)
XLA Ops:
  16.8 11.0 %collective-permute-done.1 = bf16[128,2048]{1,0:T(8,128)(2,1)S(1)} collective-permute-done((bf16[128,2048]{1,0:T(8,128)(2,1)S(1)}, bf16[128,2048]{1,0:T(8,128)(2,1)S(1)}, u32[]{:S(2)}, u32[]{:S(2)}) %collective-permute-start.1) | collective-permute-done | bytes 524320 | tf_op jit(solution)/shard_map/ppermute | solution.py:63
  27.9 3.3 collective-permute-start.3
  32.7 3.8 %collective-permute-done.2 = bf16[64,2048]{1,0:T(8,128)(2,1)S(1)} collective-permute-done((bf16[64,2048]{1,0:T(8,128)(2,1)S(1)}, bf16[64,2048]{1,0:T(8,128)(2,1)S(1)}, u32[]{:S(2)}, u32[]{:S(2)}) %collective-permute-start.2) | collective-permute-done | bytes 262176 | tf_op jit(solution)/shard_map/ppermute | solution.py:65
  41.2 3.9 %slice_bitcast_fusion.2 = (bf16[512,2048]{0,1:T(8,128)(2,1)}, bf16[512,2048]{0,1:T(8,128)(2,1)S(1)}) fusion(bf16[2,2048,512]{2,1,0:T(8,128)(2,1)} %param.27), kind=kLoop, calls=%fused_computation.69 | loop fusion | bytes 8388608 | tf_op jit(solution)/shard_map/dot_general | solution.py:165
  48.8 14.4 %slice_bitcast_fusion = (bf16[2048,2,1024]{2,1,0:T(2,128)(2,1)}, bf16[2048,2,1024]{2,1,0:T(2,128)(2,1)}) fusion(bf16[2,2048,2,1024]{3,2,1,0:T(2,128)(2,1)} %param.30), kind=kLoop, calls=%fused_computation.9 | loop fusion | bytes 33554432 | tf_op jit(solution)/shard_map/squeeze | solution.py:212
  69.8 4.6 %divide_convert_fusion.1 = bf16[2,4,512,640]{2,3,1,0:T(8,128)(2,1)} fusion(f32[2,4,512,512]{2,3,1,0:T(8,128)S(1)} %get-tuple-element.88, f32[2,4,512,128]{2,3,1,0:T(8,128)} %copy-done.1, f32[2,4,512]{2,1,0:T(4,128)S(1)} %fusion.3, f32[2,4,512]{2,1,0:T(4,128)S(1)} %reduce_max.61), kind=kLoop, calls=%fused_computation.5 | loop fusion | flops 10485760 | bytes 15761408 | tf_op jit(solution)/shard_map/convert_element_type | solution.py:239
  77.4 11.4 %all-gather.7.cloned.1.call-done = bf16[32,131,512]{2,1,0:T(8,128)(2,1)} async-done(((bf16[1,131,512]{2,1,0:T(8,128)(2,1)}), bf16[32,131,512]{2,1,0:T(8,128)(2,1)}) %all-gather.7.cloned.1.call-update) | async-done | bytes 4292624 | tf_op jit(solution)/shard_map/all_gather | solution.py:196
  103.7 6.4 %collective-permute-done.4 = bf16[64,2048]{1,0:T(8,128)(2,1)S(1)} collective-permute-done((bf16[64,2048]{1,0:T(8,128)(2,1)S(1)}, bf16[64,2048]{1,0:T(8,128)(2,1)S(1)}, u32[]{:S(2)}, u32[]{:S(2)}) %collective-permute-start.4) | collective-permute-done | bytes 262176 | tf_op jit(solution)/shard_map/ppermute | solution.py:75
  114.1 9.8 %collective-permute-done.7 = bf16[128,2048]{1,0:T(8,128)(2,1)S(1)} collective-permute-done((bf16[128,2048]{1,0:T(8,128)(2,1)S(1)}, bf16[128,2048]{1,0:T(8,128)(2,1)S(1)}, u32[]{:S(2)}, u32[]{:S(2)}) %collective-permute-start.7) | collective-permute-done | bytes 524320 | tf_op jit(solution)/shard_map/ppermute | solution.py:80
  123.9 3.5 collective-permute-done.5
  130.1 10.0 %collective-permute-done.9 = bf16[128,2048]{1,0:T(8,128)(2,1)S(1)} collective-permute-done((bf16[128,2048]{1,0:T(8,128)(2,1)S(1)}, bf16[128,2048]{1,0:T(8,128)(2,1)S(1)}, u32[]{:S(2)}, u32[]{:S(2)}) %collective-permute-start.9) | collective-permute-done | bytes 524320 | tf_op jit(solution)/shard_map/ppermute | solution.py:64
  153.3 3.2 collective-permute-start.14
  156.5 4.3 %collective-permute-done.12 = bf16[64,2048]{1,0:T(8,128)(2,1)S(1)} collective-permute-done((bf16[64,2048]{1,0:T(8,128)(2,1)S(1)}, bf16[64,2048]{1,0:T(8,128)(2,1)S(1)}, u32[]{:S(2)}, u32[]{:S(2)}) %collective-permute-start.12) | collective-permute-done | bytes 262176 | tf_op jit(solution)/shard_map/ppermute | solution.py:75
  161.9 3.8 %collective-permute-start.15 = (bf16[128,2048]{1,0:T(8,128)(2,1)S(1)}, bf16[128,2048]{1,0:T(8,128)(2,1)S(1)}, u32[]{:S(2)}, u32[]{:S(2)}) collective-permute-start(bf16[128,2048]{1,0:T(8,128)(2,1)S(1)} %pad_maximum_fusion.5), channel_id=1, source_target_pairs={{0,3},{1,0},{2,1},{3,2},{4,7},{5,4},{6,5},{7,6},{8,11},{9,8},{10,9... | collective-permute-start | bytes 1572872 | tf_op jit(solution)/shard_map/ppermute | solution.py:80
  172.4 6.6 %collective-permute-done.13 = bf16[128,2048]{1,0:T(8,128)(2,1)S(1)} collective-permute-done((bf16[128,2048]{1,0:T(8,128)(2,1)S(1)}, bf16[128,2048]{1,0:T(8,128)(2,1)S(1)}, u32[]{:S(2)}, u32[]{:S(2)}) %collective-permute-start.13) | collective-permute-done | bytes 524320 | tf_op jit(solution)/shard_map/ppermute | solution.py:79
  180.5 3.2 collective-permute-start.16
  184.6 9.4 %collective-permute-done.17 = bf16[128,2048]{1,0:T(8,128)(2,1)S(1)} collective-permute-done((bf16[128,2048]{1,0:T(8,128)(2,1)}, bf16[128,2048]{1,0:T(8,128)(2,1)S(1)}, u32[]{:S(2)}, u32[]{:S(2)}) %collective-permute-start.17) | collective-permute-done | bytes 524320 | tf_op jit(solution)/shard_map/ppermute | solution.py:63
  194.1 3.3 collective-permute-start.19
  207.8 4.2 %copy.169 = bf16[512,2048]{1,0:T(8,128)(2,1)} copy(bf16[512,2048]{0,1:T(8,128)(2,1)} %get-tuple-element.31) | data formatting | bytes 4194304 | tf_op jit(solution)/shard_map/dot_general | solution.py:165
  221.9 4.6 %divide_convert_fusion = bf16[2,4,512,640]{2,3,1,0:T(8,128)(2,1)} fusion(f32[2,4,512,512]{2,3,1,0:T(8,128)S(1)} %get-tuple-element.96, f32[2,4,512,128]{2,3,1,0:T(8,128)} %copy-done, f32[2,4,512]{2,1,0:T(4,128)S(1)} %fusion.2, f32[2,4,512]{2,1,0:T(4,128)S(1)} %reduce_max.65), kind=kLoop, calls=%fused_computation.4 | loop fusion | flops 10485760 | bytes 15761408 | tf_op jit(solution)/shard_map/convert_element_type | solution.py:239
  226.5 3.1 fusion.77
  229.6 23.1 %all-gather.9.cloned.1.call-done = bf16[32,131,512]{2,1,0:T(8,128)(2,1)} async-done(((bf16[1,131,512]{2,1,0:T(8,128)(2,1)}), bf16[32,131,512]{2,1,0:T(8,128)(2,1)}) %all-gather.9.cloned.1.call-update) | async-done | bytes 4292624 | tf_op jit(solution)/shard_map/all_gather | solution.py:196
  267.1 6.4 %collective-permute-done.20 = bf16[64,2048]{1,0:T(8,128)(2,1)S(1)} collective-permute-done((bf16[64,2048]{1,0:T(8,128)(2,1)S(1)}, bf16[64,2048]{1,0:T(8,128)(2,1)S(1)}, u32[]{:S(2)}, u32[]{:S(2)}) %collective-permute-start.20) | collective-permute-done | bytes 262176 | tf_op jit(solution)/shard_map/ppermute | solution.py:75
  277.9 9.3 %collective-permute-done.23 = bf16[128,2048]{1,0:T(8,128)(2,1)S(1)} collective-permute-done((bf16[128,2048]{1,0:T(8,128)(2,1)S(1)}, bf16[128,2048]{1,0:T(8,128)(2,1)S(1)}, u32[]{:S(2)}, u32[]{:S(2)}) %collective-permute-start.23) | collective-permute-done | bytes 524320 | tf_op jit(solution)/shard_map/ppermute | solution.py:80
  288.1 4.0 %collective-permute-done.21 = bf16[128,2048]{1,0:T(8,128)(2,1)} collective-permute-done((bf16[128,2048]{1,0:T(8,128)(2,1)}, bf16[128,2048]{1,0:T(8,128)(2,1)}, u32[]{:S(2)}, u32[]{:S(2)}) %collective-permute-start.21) | collective-permute-done | bytes 524320 | tf_op jit(solution)/shard_map/ppermute | solution.py:79
  298.4 7.8 %collective-permute-done.25 = bf16[128,2048]{1,0:T(8,128)(2,1)} collective-permute-done((bf16[128,2048]{1,0:T(8,128)(2,1)S(1)}, bf16[128,2048]{1,0:T(8,128)(2,1)}, u32[]{:S(2)}, u32[]{:S(2)}) %collective-permute-start.25) | collective-permute-done | bytes 524320 | tf_op jit(solution)/shard_map/ppermute | solution.py:64
  310.5 7.0 %fusion.6 = f32[256,2,1024]{2,0,1:T(8,128)S(1)} fusion(bf16[2048,2,1024]{2,1,0:T(2,128)(2,1)} %get-tuple-element.10, bf16[128,2048]{1,0:T(8,128)(2,1)} %collective-permute-done.25, bf16[128,2048]{1,0:T(8,128)(2,1)} %collective-permute-done.24), kind=kOutput, calls=%fused_computation.16 | convolution fusion | flops 2149580800 | bytes 11534336 | tf_op jit(solution)/shard_map/rd,dtf->rtf/dot_general | solution.py:85
  319.0 6.5 %fusion.4 = f32[128,2,1024]{2,0,1:T(8,128)S(1)} fusion(bf16[2048,2,1024]{2,1,0:T(2,128)(2,1)} %get-tuple-element.10, bf16[64,2048]{1,0:T(8,128)(2,1)S(1)} %collective-permute-done.27, bf16[64,2048]{1,0:T(8,128)(2,1)S(1)} %collective-permute-done.26), kind=kOutput, calls=%fused_computation.14 | convolution fusion | flops 1074790400 | bytes 9961472 | tf_op jit(solution)/shard_map/rd,dtf->rtf/dot_general | solution.py:85
  326.4 3.2 collective-permute-start.30
  329.7 4.3 %collective-permute-done.28 = bf16[64,2048]{1,0:T(8,128)(2,1)S(1)} collective-permute-done((bf16[64,2048]{1,0:T(8,128)(2,1)S(1)}, bf16[64,2048]{1,0:T(8,128)(2,1)S(1)}, u32[]{:S(2)}, u32[]{:S(2)}) %collective-permute-start.28) | collective-permute-done | bytes 262176 | tf_op jit(solution)/shard_map/ppermute | solution.py:75
  334.6 3.8 %collective-permute-start.31 = (bf16[128,2048]{1,0:T(8,128)(2,1)S(1)}, bf16[128,2048]{1,0:T(8,128)(2,1)S(1)}, u32[]{:S(2)}, u32[]{:S(2)}) collective-permute-start(bf16[128,2048]{1,0:T(8,128)(2,1)S(1)} %pad_maximum_fusion.11), channel_id=1, source_target_pairs={{0,3},{1,0},{2,1},{3,2},{4,7},{5,4},{6,5},{7,6},{8,11},{9,8},{10,9... | collective-permute-start | bytes 1572872 | tf_op jit(solution)/shard_map/ppermute | solution.py:80
  345.0 4.1 %collective-permute-done.29 = bf16[128,2048]{1,0:T(8,128)(2,1)S(1)} collective-permute-done((bf16[128,2048]{1,0:T(8,128)(2,1)S(1)}, bf16[128,2048]{1,0:T(8,128)(2,1)S(1)}, u32[]{:S(2)}, u32[]{:S(2)}) %collective-permute-start.29) | collective-permute-done | bytes 524320 | tf_op jit(solution)/shard_map/ppermute | solution.py:79
  (315 shorter events, 134.6 us)
Async XLA Ops:
  7.2 81.6 %all-gather.7.cloned.1.call-start = ((), (), s32[]{:S(2)}) async-start(), calls=%async_computation | async-start | bytes 4595712 | tf_op jit(solution)/shard_map/all_gather | solution.py:196
  11.7 16.1 %collective-permute-start.1 = (bf16[128,2048]{1,0:T(8,128)(2,1)S(1)}, bf16[128,2048]{1,0:T(8,128)(2,1)S(1)}, u32[]{:S(2)}, u32[]{:S(2)}) collective-permute-start(bf16[128,2048]{1,0:T(8,128)(2,1)S(1)} %get-tuple-element.26), channel_id=1, source_target_pairs={{0,1},{1,2},{2,3},{3,0},{4,5},{5,6},{6,7},{7,4},{8,9},{9,10},{10,1... | collective-permute-start | bytes 1572872 | tf_op jit(solution)/shard_map/ppermute | solution.py:63
  13.7 14.2 %collective-permute-start = (bf16[128,2048]{1,0:T(8,128)(2,1)S(1)}, bf16[128,2048]{1,0:T(8,128)(2,1)S(1)}, u32[]{:S(2)}, u32[]{:S(2)}) collective-permute-start(bf16[128,2048]{1,0:T(8,128)(2,1)S(1)} %get-tuple-element.26), channel_id=1, source_target_pairs={{0,3},{1,0},{2,1},{3,2},{4,7},{5,4},{6,5},{7,6},{8,11},{9,8},{10,9... | collective-permute-start | bytes 1572872 | tf_op jit(solution)/shard_map/ppermute | solution.py:64
  27.8 8.8 %collective-permute-start.2 = (bf16[64,2048]{1,0:T(8,128)(2,1)S(1)}, bf16[64,2048]{1,0:T(8,128)(2,1)S(1)}, u32[]{:S(2)}, u32[]{:S(2)}) collective-permute-start(bf16[64,2048]{1,0:T(8,128)(2,1)S(1)} %slice.416), channel_id=1, source_target_pairs={{0,1},{1,2},{2,3},{3,0},{4,5},{5,6},{6,7},{7,4},{8,9},{9,10},{10,1... | collective-permute-start | bytes 786440 | tf_op jit(solution)/shard_map/ppermute | solution.py:65
  27.9 8.6 %collective-permute-start.3 = (bf16[64,2048]{1,0:T(8,128)(2,1)S(1)}, bf16[64,2048]{1,0:T(8,128)(2,1)S(1)}, u32[]{:S(2)}, u32[]{:S(2)}) collective-permute-start(bf16[64,2048]{1,0:T(8,128)(2,1)S(1)} %slice.417), channel_id=1, source_target_pairs={{0,3},{1,0},{2,1},{3,2},{4,7},{5,4},{6,5},{7,6},{8,11},{9,8},{10,9... | collective-permute-start | bytes 786440 | tf_op jit(solution)/shard_map/ppermute | solution.py:66
  41.2 211.6 %all-gather.9.cloned.1.call-start = ((), (), s32[]{:S(2)}) async-start(), calls=%async_computation.1 | async-start | bytes 4595712 | tf_op jit(solution)/shard_map/all_gather | solution.py:196
  100.0 10.1 %collective-permute-start.4 = (bf16[64,2048]{1,0:T(8,128)(2,1)S(1)}, bf16[64,2048]{1,0:T(8,128)(2,1)S(1)}, u32[]{:S(2)}, u32[]{:S(2)}) collective-permute-start(bf16[64,2048]{1,0:T(8,128)(2,1)S(1)} %get-tuple-element.43), channel_id=1, source_target_pairs={{0,1},{1,2},{2,3},{3,0},{4,5},{5,6},{6,7},{7,4},{8,9},{9,10},{10,1... | collective-permute-start | bytes 786440 | tf_op jit(solution)/shard_map/ppermute | solution.py:75
  102.0 8.2 %collective-permute-start.6 = (bf16[64,2048]{1,0:T(8,128)(2,1)S(1)}, bf16[64,2048]{1,0:T(8,128)(2,1)S(1)}, u32[]{:S(2)}, u32[]{:S(2)}) collective-permute-start(bf16[64,2048]{1,0:T(8,128)(2,1)S(1)} %get-tuple-element.44), channel_id=1, source_target_pairs={{0,3},{1,0},{2,1},{3,2},{4,7},{5,4},{6,5},{7,6},{8,11},{9,8},{10,9... | collective-permute-start | bytes 786440 | tf_op jit(solution)/shard_map/ppermute | solution.py:76
  110.4 13.5 %collective-permute-start.7 = (bf16[128,2048]{1,0:T(8,128)(2,1)S(1)}, bf16[128,2048]{1,0:T(8,128)(2,1)S(1)}, u32[]{:S(2)}, u32[]{:S(2)}) collective-permute-start(bf16[128,2048]{1,0:T(8,128)(2,1)S(1)} %pad_maximum_fusion.3), channel_id=1, source_target_pairs={{0,3},{1,0},{2,1},{3,2},{4,7},{5,4},{6,5},{7,6},{8,11},{9,8},{10,9... | collective-permute-start | bytes 1572872 | tf_op jit(solution)/shard_map/ppermute | solution.py:80
  113.4 14.0 %collective-permute-start.5 = (bf16[128,2048]{1,0:T(8,128)(2,1)S(1)}, bf16[128,2048]{1,0:T(8,128)(2,1)S(1)}, u32[]{:S(2)}, u32[]{:S(2)}) collective-permute-start(bf16[128,2048]{1,0:T(8,128)(2,1)S(1)} %pad_maximum_fusion.2), channel_id=1, source_target_pairs={{0,1},{1,2},{2,3},{3,0},{4,5},{5,6},{6,7},{7,4},{8,9},{9,10},{10,1... | collective-permute-start | bytes 1572872 | tf_op jit(solution)/shard_map/ppermute | solution.py:79
  128.0 12.1 %collective-permute-start.9 = (bf16[128,2048]{1,0:T(8,128)(2,1)S(1)}, bf16[128,2048]{1,0:T(8,128)(2,1)S(1)}, u32[]{:S(2)}, u32[]{:S(2)}) collective-permute-start(bf16[128,2048]{1,0:T(8,128)(2,1)S(1)} %multiply_convert_fusion.2), channel_id=1, source_target_pairs={{0,3},{1,0},{2,1},{3,2},{4,7},{5,4},{6,5},{7,6},{8,11},{9,8},{10,9... | collective-permute-start | bytes 1572872 | tf_op jit(solution)/shard_map/ppermute | solution.py:64
  128.3 13.4 %collective-permute-start.8 = (bf16[128,2048]{1,0:T(8,128)(2,1)S(1)}, bf16[128,2048]{1,0:T(8,128)(2,1)S(1)}, u32[]{:S(2)}, u32[]{:S(2)}) collective-permute-start(bf16[128,2048]{1,0:T(8,128)(2,1)S(1)} %multiply_convert_fusion.2), channel_id=1, source_target_pairs={{0,1},{1,2},{2,3},{3,0},{4,5},{5,6},{6,7},{7,4},{8,9},{9,10},{10,1... | collective-permute-start | bytes 1572872 | tf_op jit(solution)/shard_map/ppermute | solution.py:63
  141.7 7.7 %collective-permute-start.10 = (bf16[64,2048]{1,0:T(8,128)(2,1)S(1)}, bf16[64,2048]{1,0:T(8,128)(2,1)S(1)}, u32[]{:S(2)}, u32[]{:S(2)}) collective-permute-start(bf16[64,2048]{1,0:T(8,128)(2,1)S(1)} %slice.442), channel_id=1, source_target_pairs={{0,1},{1,2},{2,3},{3,0},{4,5},{5,6},{6,7},{7,4},{8,9},{9,10},{10,1... | collective-permute-start | bytes 786440 | tf_op jit(solution)/shard_map/ppermute | solution.py:65
  153.2 7.7 %collective-permute-start.12 = (bf16[64,2048]{1,0:T(8,128)(2,1)S(1)}, bf16[64,2048]{1,0:T(8,128)(2,1)S(1)}, u32[]{:S(2)}, u32[]{:S(2)}) collective-permute-start(bf16[64,2048]{1,0:T(8,128)(2,1)S(1)} %get-tuple-element.57), channel_id=1, source_target_pairs={{0,1},{1,2},{2,3},{3,0},{4,5},{5,6},{6,7},{7,4},{8,9},{9,10},{10,1... | collective-permute-start | bytes 786440 | tf_op jit(solution)/shard_map/ppermute | solution.py:75
  153.3 8.5 %collective-permute-start.14 = (bf16[64,2048]{1,0:T(8,128)(2,1)S(1)}, bf16[64,2048]{1,0:T(8,128)(2,1)S(1)}, u32[]{:S(2)}, u32[]{:S(2)}) collective-permute-start(bf16[64,2048]{1,0:T(8,128)(2,1)S(1)} %get-tuple-element.58), channel_id=1, source_target_pairs={{0,3},{1,0},{2,1},{3,2},{4,7},{5,4},{6,5},{7,6},{8,11},{9,8},{10,9... | collective-permute-start | bytes 786440 | tf_op jit(solution)/shard_map/ppermute | solution.py:76
  161.9 10.5 %collective-permute-start.15 = (bf16[128,2048]{1,0:T(8,128)(2,1)S(1)}, bf16[128,2048]{1,0:T(8,128)(2,1)S(1)}, u32[]{:S(2)}, u32[]{:S(2)}) collective-permute-start(bf16[128,2048]{1,0:T(8,128)(2,1)S(1)} %pad_maximum_fusion.5), channel_id=1, source_target_pairs={{0,3},{1,0},{2,1},{3,2},{4,7},{5,4},{6,5},{7,6},{8,11},{9,8},{10,9... | collective-permute-start | bytes 1572872 | tf_op jit(solution)/shard_map/ppermute | solution.py:80
  165.7 13.2 %collective-permute-start.13 = (bf16[128,2048]{1,0:T(8,128)(2,1)S(1)}, bf16[128,2048]{1,0:T(8,128)(2,1)S(1)}, u32[]{:S(2)}, u32[]{:S(2)}) collective-permute-start(bf16[128,2048]{1,0:T(8,128)(2,1)S(1)} %pad_maximum_fusion.4), channel_id=1, source_target_pairs={{0,1},{1,2},{2,3},{3,0},{4,5},{5,6},{6,7},{7,4},{8,9},{9,10},{10,1... | collective-permute-start | bytes 1572872 | tf_op jit(solution)/shard_map/ppermute | solution.py:79
  180.5 13.4 %collective-permute-start.17 = (bf16[128,2048]{1,0:T(8,128)(2,1)}, bf16[128,2048]{1,0:T(8,128)(2,1)S(1)}, u32[]{:S(2)}, u32[]{:S(2)}) collective-permute-start(bf16[128,2048]{1,0:T(8,128)(2,1)} %get-tuple-element.20), channel_id=1, source_target_pairs={{0,1},{1,2},{2,3},{3,0},{4,5},{5,6},{6,7},{7,4},{8,9},{9,10},{10,1... | collective-permute-start | bytes 1572872 | tf_op jit(solution)/shard_map/ppermute | solution.py:63
  180.5 13.5 %collective-permute-start.16 = (bf16[128,2048]{1,0:T(8,128)(2,1)}, bf16[128,2048]{1,0:T(8,128)(2,1)S(1)}, u32[]{:S(2)}, u32[]{:S(2)}) collective-permute-start(bf16[128,2048]{1,0:T(8,128)(2,1)} %get-tuple-element.20), channel_id=1, source_target_pairs={{0,3},{1,0},{2,1},{3,2},{4,7},{5,4},{6,5},{7,6},{8,11},{9,8},{10,9... | collective-permute-start | bytes 1572872 | tf_op jit(solution)/shard_map/ppermute | solution.py:64
  194.0 7.7 %collective-permute-start.18 = (bf16[64,2048]{1,0:T(8,128)(2,1)S(1)}, bf16[64,2048]{1,0:T(8,128)(2,1)S(1)}, u32[]{:S(2)}, u32[]{:S(2)}) collective-permute-start(bf16[64,2048]{1,0:T(8,128)(2,1)S(1)} %slice.451), channel_id=1, source_target_pairs={{0,1},{1,2},{2,3},{3,0},{4,5},{5,6},{6,7},{7,4},{8,9},{9,10},{10,1... | collective-permute-start | bytes 786440 | tf_op jit(solution)/shard_map/ppermute | solution.py:65
  263.8 9.7 %collective-permute-start.20 = (bf16[64,2048]{1,0:T(8,128)(2,1)S(1)}, bf16[64,2048]{1,0:T(8,128)(2,1)S(1)}, u32[]{:S(2)}, u32[]{:S(2)}) collective-permute-start(bf16[64,2048]{1,0:T(8,128)(2,1)S(1)} %get-tuple-element.37), channel_id=1, source_target_pairs={{0,1},{1,2},{2,3},{3,0},{4,5},{5,6},{6,7},{7,4},{8,9},{9,10},{10,1... | collective-permute-start | bytes 786440 | tf_op jit(solution)/shard_map/ppermute | solution.py:75
  265.4 8.2 %collective-permute-start.22 = (bf16[64,2048]{1,0:T(8,128)(2,1)S(1)}, bf16[64,2048]{1,0:T(8,128)(2,1)S(1)}, u32[]{:S(2)}, u32[]{:S(2)}) collective-permute-start(bf16[64,2048]{1,0:T(8,128)(2,1)S(1)} %get-tuple-element.38), channel_id=1, source_target_pairs={{0,3},{1,0},{2,1},{3,2},{4,7},{5,4},{6,5},{7,6},{8,11},{9,8},{10,9... | collective-permute-start | bytes 786440 | tf_op jit(solution)/shard_map/ppermute | solution.py:76
  273.7 13.6 %collective-permute-start.23 = (bf16[128,2048]{1,0:T(8,128)(2,1)S(1)}, bf16[128,2048]{1,0:T(8,128)(2,1)S(1)}, u32[]{:S(2)}, u32[]{:S(2)}) collective-permute-start(bf16[128,2048]{1,0:T(8,128)(2,1)S(1)} %pad_maximum_fusion.9), channel_id=1, source_target_pairs={{0,3},{1,0},{2,1},{3,2},{4,7},{5,4},{6,5},{7,6},{8,11},{9,8},{10,9... | collective-permute-start | bytes 1572872 | tf_op jit(solution)/shard_map/ppermute | solution.py:80
  277.6 14.5 %collective-permute-start.21 = (bf16[128,2048]{1,0:T(8,128)(2,1)}, bf16[128,2048]{1,0:T(8,128)(2,1)}, u32[]{:S(2)}, u32[]{:S(2)}) collective-permute-start(bf16[128,2048]{1,0:T(8,128)(2,1)} %pad_maximum_fusion.8), channel_id=1, source_target_pairs={{0,1},{1,2},{2,3},{3,0},{4,5},{5,6},{6,7},{7,4},{8,9},{9,10},{10,1... | collective-permute-start | bytes 1572872 | tf_op jit(solution)/shard_map/ppermute | solution.py:79
  294.2 12.0 %collective-permute-start.25 = (bf16[128,2048]{1,0:T(8,128)(2,1)S(1)}, bf16[128,2048]{1,0:T(8,128)(2,1)}, u32[]{:S(2)}, u32[]{:S(2)}) collective-permute-start(bf16[128,2048]{1,0:T(8,128)(2,1)S(1)} %multiply_convert_fusion), channel_id=1, source_target_pairs={{0,3},{1,0},{2,1},{3,2},{4,7},{5,4},{6,5},{7,6},{8,11},{9,8},{10,9... | collective-permute-start | bytes 1572872 | tf_op jit(solution)/shard_map/ppermute | solution.py:64
  294.3 14.5 %collective-permute-start.24 = (bf16[128,2048]{1,0:T(8,128)(2,1)S(1)}, bf16[128,2048]{1,0:T(8,128)(2,1)}, u32[]{:S(2)}, u32[]{:S(2)}) collective-permute-start(bf16[128,2048]{1,0:T(8,128)(2,1)S(1)} %multiply_convert_fusion), channel_id=1, source_target_pairs={{0,1},{1,2},{2,3},{3,0},{4,5},{5,6},{6,7},{7,4},{8,9},{9,10},{10,1... | collective-permute-start | bytes 1572872 | tf_op jit(solution)/shard_map/ppermute | solution.py:63
  307.2 11.8 %collective-permute-start.27 = (bf16[64,2048]{1,0:T(8,128)(2,1)S(1)}, bf16[64,2048]{1,0:T(8,128)(2,1)S(1)}, u32[]{:S(2)}, u32[]{:S(2)}) collective-permute-start(bf16[64,2048]{1,0:T(8,128)(2,1)S(1)} %slice.478), channel_id=1, source_target_pairs={{0,3},{1,0},{2,1},{3,2},{4,7},{5,4},{6,5},{7,6},{8,11},{9,8},{10,9... | collective-permute-start | bytes 786440 | tf_op jit(solution)/shard_map/ppermute | solution.py:66
  309.9 9.1 %collective-permute-start.26 = (bf16[64,2048]{1,0:T(8,128)(2,1)S(1)}, bf16[64,2048]{1,0:T(8,128)(2,1)S(1)}, u32[]{:S(2)}, u32[]{:S(2)}) collective-permute-start(bf16[64,2048]{1,0:T(8,128)(2,1)S(1)} %slice.477), channel_id=1, source_target_pairs={{0,1},{1,2},{2,3},{3,0},{4,5},{5,6},{6,7},{7,4},{8,9},{9,10},{10,1... | collective-permute-start | bytes 786440 | tf_op jit(solution)/shard_map/ppermute | solution.py:65
  326.3 7.7 %collective-permute-start.28 = (bf16[64,2048]{1,0:T(8,128)(2,1)S(1)}, bf16[64,2048]{1,0:T(8,128)(2,1)S(1)}, u32[]{:S(2)}, u32[]{:S(2)}) collective-permute-start(bf16[64,2048]{1,0:T(8,128)(2,1)S(1)} %get-tuple-element.55), channel_id=1, source_target_pairs={{0,1},{1,2},{2,3},{3,0},{4,5},{5,6},{6,7},{7,4},{8,9},{9,10},{10,1... | collective-permute-start | bytes 786440 | tf_op jit(solution)/shard_map/ppermute | solution.py:75
  326.4 8.0 %collective-permute-start.30 = (bf16[64,2048]{1,0:T(8,128)(2,1)S(1)}, bf16[64,2048]{1,0:T(8,128)(2,1)S(1)}, u32[]{:S(2)}, u32[]{:S(2)}) collective-permute-start(bf16[64,2048]{1,0:T(8,128)(2,1)S(1)} %get-tuple-element.56), channel_id=1, source_target_pairs={{0,3},{1,0},{2,1},{3,2},{4,7},{5,4},{6,5},{7,6},{8,11},{9,8},{10,9... | collective-permute-start | bytes 786440 | tf_op jit(solution)/shard_map/ppermute | solution.py:76
  334.6 10.5 %collective-permute-start.31 = (bf16[128,2048]{1,0:T(8,128)(2,1)S(1)}, bf16[128,2048]{1,0:T(8,128)(2,1)S(1)}, u32[]{:S(2)}, u32[]{:S(2)}) collective-permute-start(bf16[128,2048]{1,0:T(8,128)(2,1)S(1)} %pad_maximum_fusion.11), channel_id=1, source_target_pairs={{0,3},{1,0},{2,1},{3,2},{4,7},{5,4},{6,5},{7,6},{8,11},{9,8},{10,9... | collective-permute-start | bytes 1572872 | tf_op jit(solution)/shard_map/ppermute | solution.py:80
  338.4 10.8 %collective-permute-start.29 = (bf16[128,2048]{1,0:T(8,128)(2,1)S(1)}, bf16[128,2048]{1,0:T(8,128)(2,1)S(1)}, u32[]{:S(2)}, u32[]{:S(2)}) collective-permute-start(bf16[128,2048]{1,0:T(8,128)(2,1)S(1)} %pad_maximum_fusion.10), channel_id=1, source_target_pairs={{0,1},{1,2},{2,3},{3,0},{4,5},{5,6},{6,7},{7,4},{8,9},{9,10},{10,1... | collective-permute-start | bytes 1572872 | tf_op jit(solution)/shard_map/ppermute | solution.py:79
  (55 other events, 667.7 us)
Sparse Core Ops, SparseCore 0:
  41.3 47.4 all-gather.6
  207.1 45.6 all-gather.8
